TPU v7x, 32 devices: a whole 2x2x4 slice. The times are simulated.
32 devices in a mesh: blk: 2 (over x), gy: 4 (over y, core), gz: 4 (over z).
Axes of the slice: x: 2, y: 2, z: 4, core: 2. Of those that a mesh axis runs over, the one named last changes fastest.
Arguments:
- vacancy: float32 [64, 64, 1024], P('blk', 'gy', 'gz'), may hold values from -6 to 6
- grain_label: int32 [64, 64, 1024], P('blk', 'gy', 'gz'), may hold values from 0 to 7
- pore_mask: int32 [64, 64, 1024], P('blk', 'gy', 'gz'), may hold values 0 or 1
- cotangent: float32 [64, 64, 1024], P('blk', 'gy', 'gz'), may hold values from -6 to 6
Outputs:
- final_field: float32 [64, 64, 1024], P('blk', 'gy', 'gz')
- gradient: float32 [64, 64, 1024], P('blk', 'gy', 'gz')
All inputs are finite; a program needn't handle non-finite values. No bound on the sum of `pore_mask` on one device may be relied on, other than what follows from the above.
Results may differ from a plain program's by a relative error of at most 0.00017.
Values sent between devices are 32-bit elements; how exact they have to be, the bound alone decides.
No kernel may reach another device: no remote copies, remote signals or barrier semaphores. Data moves between devices by JAX's collectives and lax.ppermute only.
A program may use at most 128 MiB of HBM per device.

v0:
```python
import jax
import jax.numpy as jnp
from jax import lax
from jax.experimental import pallas as pl
from jax.experimental.pallas import tpu as pltpu
from jax.sharding import PartitionSpec as P

cross_rate = 0.0125
boundary_gain = 3.0
F32 = jnp.float32


def face_value(mobility_here, mobility_there, label_here, label_there):
    harmonic = 2.0 * mobility_here * mobility_there / (mobility_here + mobility_there)
    return harmonic * jnp.where(label_here != label_there, boundary_gain, 1.0)


def _vmem():
    return pl.BlockSpec(memory_space=pltpu.VMEM)


def _smem():
    return pl.BlockSpec(memory_space=pltpu.SMEM)


def _shift(x, edge, axis, up):
    n = x.shape[axis]
    idx = lax.broadcasted_iota(jnp.int32, x.shape, axis)
    edge = jnp.broadcast_to(edge, x.shape)
    if up:
        return jnp.where(idx == n - 1, edge, pltpu.roll(x, n - 1, axis))
    return jnp.where(idx == 0, edge, pltpu.roll(x, 1, axis))


def _neighbours(x, ylo, yhi, zlo, zhi):
    return (
        _shift(x, yhi, 0, True),
        _shift(x, ylo, 0, False),
        _shift(x, zhi, 1, True),
        _shift(x, zlo, 1, False),
    )


def _faces(mob, lab, mob_n, lab_n):
    ups = (True, False, True, False)
    out = []
    for up, mn, ln in zip(ups, mob_n, lab_n):
        if up:
            out.append(face_value(mob, mn, lab, ln))
        else:
            out.append(face_value(mn, mob, ln, lab))
    return out


def _flux(u, u_n, faces):
    total = faces[0] * (u_n[0] - u)
    total = total + faces[1] * (u_n[1] - u)
    total = total + faces[2] * (u_n[2] - u)
    total = total + faces[3] * (u_n[3] - u)
    return total


def _geo_row(i, pore_ref, lab_ref, gy_lo, gy_hi, gz_lo, gz_hi):
    mob = 1.0 + 2.0 * pore_ref[i].astype(F32)
    lab = lab_ref[i].astype(F32)
    mob_n = _neighbours(mob, gy_lo[0, i], gy_hi[0, i], gz_lo[0, i], gz_hi[0, i])
    lab_n = _neighbours(lab, gy_lo[1, i], gy_hi[1, i], gz_lo[1, i], gz_hi[1, i])
    return mob, lab, mob_n, _faces(mob, lab, mob_n, lab_n)


def _sweep(m, lower, pivots, ratios, source):
    ys = [None] * m
    prev = None
    for r in range(m - 1):
        num = source[r]
        if num is None:
            if prev is None:
                continue
            num = -(lower[r] * prev)
        elif prev is not None:
            num = num - lower[r] * prev
        ys[r] = num / pivots[r]
        prev = ys[r]
    xs = [None] * m
    prev = None
    for r in range(m - 2, -1, -1):
        if prev is None:
            xs[r] = ys[r]
        elif ys[r] is None:
            xs[r] = -(ratios[r] * prev)
        else:
            xs[r] = ys[r] - ratios[r] * prev
        prev = xs[r]
    return xs


def _prep_kernel(cs, vac_ref, pore_ref, lab_ref, cot_ref, bx_lo, bx_hi, gy_lo, gy_hi, gz_lo, gz_hi,
                 fac_ref, loc_ref, rows_ref):
    m = vac_ref.shape[0]
    zero = jnp.zeros(vac_ref.shape[1:], F32)
    mobs = [1.0 + 2.0 * pore_ref[r].astype(F32) for r in range(m)]
    labs = [lab_ref[r].astype(F32) for r in range(m)]
    m_ext = [bx_lo[0]] + mobs + [bx_hi[0]]
    l_ext = [bx_lo[1]] + labs + [bx_hi[1]]
    w_ext = [0.5 * (1.0 + x) for x in m_ext]
    faces = [face_value(m_ext[k], m_ext[k + 1], l_ext[k], l_ext[k + 1]) for k in range(m + 1)]
    bands = {"f": ([], [], []), "a": ([], [], [])}
    for r in range(m):
        bf, ff = faces[r], faces[r + 1]
        w = w_ext[r + 1]
        main = 1.0 + cs * w * (bf + ff)
        bands["f"][0].append(-cs * bf * w_ext[r])
        bands["f"][1].append(main)
        bands["f"][2].append(-cs * ff * w_ext[r + 2])
        bands["a"][0].append(-cs * bf * w)
        bands["a"][1].append(main)
        bands["a"][2].append(-cs * ff * w)

    src_f = []
    for i in range(m):
        mob, lab, mob_n, fc = _geo_row(i, pore_ref, lab_ref, gy_lo, gy_hi, gz_lo, gz_hi)
        v = vac_ref[i]
        u = w_ext[i + 1] * v
        v_n = _neighbours(v, gy_lo[2, i], gy_hi[2, i], gz_lo[2, i], gz_hi[2, i])
        u_n = [0.5 * (1.0 + mn) * vn for mn, vn in zip(mob_n, v_n)]
        src_f.append(v + cross_rate * (1.0 * _flux(u, u_n, fc)))
    src_a = [cot_ref[r] for r in range(m)]

    for c, key, src in ((0, "f", src_f), (1, "a", src_a)):
        lower, main, upper = bands[key]
        pivots, ratios = [], []
        prev = None
        for r in range(m - 1):
            piv = main[r] if prev is None else main[r] - lower[r] * prev
            rat = upper[r] / piv
            pivots.append(piv)
            ratios.append(rat)
            prev = rat
        left_src = [lower[0]] + [None] * (m - 1)
        right_src = [None] * (m - 2) + [upper[m - 2], None]
        left = _sweep(m, lower, pivots, ratios, left_src)
        right = _sweep(m, lower, pivots, ratios, right_src)
        local = _sweep(m, lower, pivots, ratios, src[: m - 1] + [None])
        for r in range(m):
            fac_ref[c, 0, r] = lower[r]
            fac_ref[c, 1, r] = ratios[r] if r < m - 1 else zero
            fac_ref[c, 2, r] = pivots[r] if r < m - 1 else zero + 1.0
            fac_ref[c, 3, r] = left[r] if r < m - 1 else zero
            fac_ref[c, 4, r] = right[r] if r < m - 1 else zero - 1.0
            loc_ref[c, r] = local[r] if r < m - 1 else zero
        last_lower = lower[m - 1]
        rows_ref[c, 0] = last_lower * left[m - 2]
        rows_ref[c, 1] = main[m - 1] - last_lower * right[m - 2]
        rows_ref[c, 2] = upper[m - 1]
        rows_ref[c, 3] = left[0]
        rows_ref[c, 4] = right[0]
        rows_ref[c, 5] = src[m - 1] - last_lower * local[m - 2]
        rows_ref[c, 6] = local[0]


def _reduced_solve(gs, gv, voff, c, n):
    g = [[gs[p, c, k] for k in range(5)] for p in range(n)]
    lower = [-g[p][0] for p in range(n)]
    main = [g[p][1] - g[p][2] * g[(p + 1) % n][3] for p in range(n)]
    upper = [-g[p][2] * g[(p + 1) % n][4] for p in range(n)]
    src = [gv[p, c, voff] - g[p][2] * gv[(p + 1) % n, c, voff + 1] for p in range(n)]
    k_in = n - 1
    pivots, ratios = [], []
    prev = None
    for r in range(k_in):
        piv = main[r] if prev is None else main[r] - lower[r] * prev
        rat = upper[r] / piv
        pivots.append(piv)
        ratios.append(rat)
        prev = rat

    def apply(source):
        ys = []
        prev = None
        for r in range(k_in):
            num = source[r] if prev is None else source[r] - lower[r] * prev
            ys.append(num / pivots[r])
            prev = ys[-1]
        xs = [None] * k_in
        prev = None
        for r in range(k_in - 1, -1, -1):
            xs[r] = ys[r] if prev is None else ys[r] - ratios[r] * prev
            prev = xs[r]
        return xs

    coupling = []
    for r in range(k_in):
        term = None
        if r == 0:
            term = lower[0]
        if r == k_in - 1:
            term = upper[k_in - 1] if term is None else term + upper[k_in - 1]
        coupling.append(term if term is not None else jnp.zeros_like(lower[0]))
    linked = apply(coupling)
    closing = main[k_in] - lower[k_in] * linked[k_in - 1] - upper[k_in] * linked[0]
    inner = apply(src[:k_in])
    sep = (src[k_in] - lower[k_in] * inner[k_in - 1] - upper[k_in] * inner[0]) / closing
    return [inner[r] - linked[r] * sep for r in range(k_in)] + [sep]


def _combine_kernel(voff, stacked, pos_ref, gs_ref, gv_ref, fac_ref, loc_ref, *refs):
    if stacked:
        out_ref, sep_ref = refs
        outs = (out_ref.at[0], out_ref.at[1])
    else:
        out0, out1, sep_ref = refs
        outs = (out0, out1)
    n = gs_ref.shape[0]
    m = loc_ref.shape[1]
    p = pos_ref[0]
    for c in range(2):
        seps = _reduced_solve(gs_ref, gv_ref, voff, c, n)
        for q in range(n):
            sep_ref[q] = seps[q]
        own = sep_ref[p]
        prior = sep_ref[(p + n - 1) % n]
        for r in range(m):
            outs[c][r] = loc_ref[c, r] - fac_ref[c, 3, r] * prior - fac_ref[c, 4, r] * own


def _second_kernel(pore_ref, lab_ref, fa_ref, fac_ref, gy_lo, gy_hi, gz_lo, gz_hi,
                   hy_lo, hy_hi, hz_lo, hz_hi, loc_ref, vals_ref):
    m = pore_ref.shape[0]
    srcs = ([], [])
    for i in range(m):
        mob, lab, mob_n, fc = _geo_row(i, pore_ref, lab_ref, gy_lo, gy_hi, gz_lo, gz_hi)
        w = 0.5 * (1.0 + mob)
        f1 = fa_ref[0, i]
        f_n = _neighbours(f1, hy_lo[0, i], hy_hi[0, i], hz_lo[0, i], hz_hi[0, i])
        u_n = [0.5 * (1.0 + mn) * fn for mn, fn in zip(mob_n, f_n)]
        srcs[0].append(f1 + cross_rate * (1.0 * _flux(w * f1, u_n, fc)))
        a1 = fa_ref[1, i]
        a_n = _neighbours(a1, hy_lo[1, i], hy_hi[1, i], hz_lo[1, i], hz_hi[1, i])
        srcs[1].append(a1 + cross_rate * (w * _flux(a1, a_n, fc)))
    zero = jnp.zeros(pore_ref.shape[1:], F32)
    for c in range(2):
        lower = [fac_ref[c, 0, r] for r in range(m)]
        ratios = [fac_ref[c, 1, r] for r in range(m - 1)]
        pivots = [fac_ref[c, 2, r] for r in range(m - 1)]
        src = srcs[c]
        local = _sweep(m, lower, pivots, ratios, src[: m - 1] + [None])
        for r in range(m):
            loc_ref[c, r] = local[r] if r < m - 1 else zero
        vals_ref[c, 0] = src[m - 1] - lower[m - 1] * local[m - 2]
        vals_ref[c, 1] = local[0]


def _gradient_kernel(pore_ref, lab_ref, a2_ref, gy_lo, gy_hi, gz_lo, gz_hi,
                     hy_lo, hy_hi, hz_lo, hz_hi, out_ref):
    m = pore_ref.shape[0]
    for i in range(m):
        mob, lab, mob_n, fc = _geo_row(i, pore_ref, lab_ref, gy_lo, gy_hi, gz_lo, gz_hi)
        w = 0.5 * (1.0 + mob)
        a2 = a2_ref[i]
        a_n = _neighbours(a2, hy_lo[0, i], hy_hi[0, i], hz_lo[0, i], hz_hi[0, i])
        out_ref[i] = a2 + cross_rate * (w * _flux(a2, a_n, fc))


def _halo_pairs(axis, periodic):
    count = lax.axis_size(axis)
    forward = [(i, i + 1) for i in range(count - 1)]
    if periodic:
        forward.append((count - 1, 0))
    backward = [(t, s) for s, t in forward]
    return forward, backward


def _exchange(first, last, axis, periodic):
    forward, backward = _halo_pairs(axis, periodic)
    lo = lax.ppermute(last, axis, forward)
    hi = lax.ppermute(first, axis, backward)
    return lo, hi


def _yz_halos(stack):
    y = stack.shape[2]
    z = stack.shape[3]
    gy_lo, gy_hi = _exchange(stack[:, :, 0:1, :], stack[:, :, y - 1 : y, :], "gy", False)
    gz_lo, gz_hi = _exchange(stack[:, :, :, 0:1], stack[:, :, :, z - 1 : z], "gz", False)
    return gy_lo, gy_hi, gz_lo, gz_hi


def shards(vacancy, grain_label, pore_mask, cotangent):
    m, ny, nz = vacancy.shape
    n_blk = lax.axis_size("blk")
    cycle_step = float((m * n_blk) ** 2 // 64)
    shape = jax.ShapeDtypeStruct((m, ny, nz), F32)

    mobility = 1.0 + 2.0 * pore_mask.astype(F32)
    labels = grain_label.astype(F32)
    geo0 = jnp.stack([mobility[0], labels[0]])
    geo1 = jnp.stack([mobility[m - 1], labels[m - 1]])
    bx_lo, bx_hi = _exchange(geo0, geo1, "blk", True)
    gy_lo, gy_hi, gz_lo, gz_hi = _yz_halos(jnp.stack([mobility, labels, vacancy]))

    fac, loc, rows = pl.pallas_call(
        lambda *r: _prep_kernel(cycle_step, *r),
        out_shape=(
            jax.ShapeDtypeStruct((2, 5, m, ny, nz), F32),
            jax.ShapeDtypeStruct((2, m, ny, nz), F32),
            jax.ShapeDtypeStruct((2, 7, ny, nz), F32),
        ),
        in_specs=[_vmem()] * 10,
        out_specs=(_vmem(), _vmem(), _vmem()),
    )(vacancy, pore_mask, grain_label, cotangent, bx_lo, bx_hi, gy_lo, gy_hi, gz_lo, gz_hi)

    gathered = lax.all_gather(rows, "blk", axis=0, tiled=False)
    pos = jnp.reshape(lax.axis_index("blk"), (1,)).astype(jnp.int32)

    fa = pl.pallas_call(
        lambda *r: _combine_kernel(5, True, *r),
        out_shape=jax.ShapeDtypeStruct((2, m, ny, nz), F32),
        in_specs=[_smem()] + [_vmem()] * 4,
        out_specs=_vmem(),
        scratch_shapes=[pltpu.VMEM((n_blk, ny, nz), F32)],
    )(pos, gathered, gathered, fac, loc)

    hy_lo, hy_hi, hz_lo, hz_hi = _yz_halos(fa)
    loc2, vals2 = pl.pallas_call(
        _second_kernel,
        out_shape=(
            jax.ShapeDtypeStruct((2, m, ny, nz), F32),
            jax.ShapeDtypeStruct((2, 2, ny, nz), F32),
        ),
        in_specs=[_vmem()] * 12,
        out_specs=(_vmem(), _vmem()),
    )(pore_mask, grain_label, fa, fac, gy_lo, gy_hi, gz_lo, gz_hi, hy_lo, hy_hi, hz_lo, hz_hi)

    gathered2 = lax.all_gather(vals2, "blk", axis=0, tiled=False)
    final_field, adjoint_two = pl.pallas_call(
        lambda *r: _combine_kernel(0, False, *r),
        out_shape=(shape, shape),
        in_specs=[_smem()] + [_vmem()] * 4,
        out_specs=(_vmem(), _vmem()),
        scratch_shapes=[pltpu.VMEM((n_blk, ny, nz), F32)],
    )(pos, gathered, gathered2, fac, loc2)

    a2_lo, a2_hi, a2z_lo, a2z_hi = _yz_halos(adjoint_two[None])
    gradient = pl.pallas_call(
        _gradient_kernel,
        out_shape=shape,
        in_specs=[_vmem()] * 11,
        out_specs=_vmem(),
    )(pore_mask, grain_label, adjoint_two, gy_lo, gy_hi, gz_lo, gz_hi, a2_lo, a2_hi, a2z_lo, a2z_hi)
    return (final_field, gradient)


def solution(mesh):
    in_specs = (
        P("blk", "gy", "gz"),
        P("blk", "gy", "gz"),
        P("blk", "gy", "gz"),
        P("blk", "gy", "gz"),
    )
    out_specs = (P("blk", "gy", "gz"), P("blk", "gy", "gz"))
    return jax.shard_map(shards, mesh=mesh, in_specs=in_specs, out_specs=out_specs, check_vma=False)
```

profile of v0, /device:TPU:0, one launch (start us, length us, event | category | flops | bytes accessed | tf_op | source)
XLA Modules:
  0.0 113.2 jit_solution(5150399402180813738)
XLA Ops:
  0.7 1.2 %convert_bitcast_fusion = (f32[1,32,16,256]{3,2,1,0:T(8,128)S(1)}, f32[32,16,256]{2,1,0:T(8,128)S(1)}) fusion(s32[32,16,256]{2,1,0:T(8,128)} %lab_ref.3), kind=kLoop, calls=%fused_computation.6 | loop fusion | flops 131072 | bytes 1572864 | tf_op jit(solution)/shard_map/stack | solution.py:299
  1.9 0.1 fusion
  2.0 3.0 %collective-permute-start = (f32[2,16,256]{2,1,0:T(8,128)S(1)}, f32[2,16,256]{2,1,0:T(8,128)S(1)}, u32[]{:S(2)}, u32[]{:S(2)}) collective-permute-start(f32[2,16,256]{2,1,0:T(8,128)S(1)} %pad_maximum_fusion.3), channel_id=1, source_target_pairs={{0,16},{16,0},{1,17},{17,1},{2,18},{18,2},{3,19},{19,3},{4,20},{20... | collective-permute-start | bytes 98312 | tf_op jit(solution)/shard_map/ppermute | solution.py:275
  5.0 0.1 collective-permute-start.1
  5.1 0.1 pad_maximum_fusion.1
  5.2 1.3 %collective-permute-start.3 = (f32[3,32,1,256]{3,2,1,0:T(1,128)S(1)}, f32[3,32,1,256]{3,2,1,0:T(1,128)S(1)}, u32[]{:S(2)}, u32[]{:S(2)}) collective-permute-start(f32[3,32,1,256]{3,2,1,0:T(1,128)S(1)} %get-tuple-element.18), channel_id=1, source_target_pairs={{4,0},{8,4},{12,8},{5,1},{9,5},{13,9},{6,2},{10,6},{14,10},{7,3},{... | collective-permute-start | bytes 294920 | tf_op jit(solution)/shard_map/ppermute | solution.py:276
  6.5 3.0 %collective-permute-start.2 = (f32[3,32,1,256]{3,2,1,0:T(1,128)S(1)}, f32[3,32,1,256]{3,2,1,0:T(1,128)S(1)}, u32[]{:S(2)}, u32[]{:S(2)}) collective-permute-start(f32[3,32,1,256]{3,2,1,0:T(1,128)S(1)} %get-tuple-element.19), channel_id=1, source_target_pairs={{0,4},{4,8},{8,12},{1,5},{5,9},{9,13},{2,6},{6,10},{10,14},{3,7},{... | collective-permute-start | bytes 294920 | tf_op jit(solution)/shard_map/ppermute | solution.py:275
  9.6 0.1 pad_maximum_fusion
  9.7 0.3 fusion.1
  10.0 0.4 copy.7
  10.4 1.3 %collective-permute-start.5 = (f32[3,32,16,1]{1,2,3,0:T(8,128)S(1)}, f32[3,32,16,1]{1,2,3,0:T(8,128)S(1)}, u32[]{:S(2)}, u32[]{:S(2)}) collective-permute-start(f32[3,32,16,1]{1,2,3,0:T(8,128)S(1)} %copy.7), channel_id=1, source_target_pairs={{1,0},{2,1},{3,2},{5,4},{6,5},{7,6},{9,8},{10,9},{11,10},{13,12},{... | collective-permute-start | bytes 18440 | tf_op jit(solution)/shard_map/ppermute | solution.py:276
  11.7 0.4 copy.6
  12.1 4.0 %collective-permute-done.5 = f32[3,32,16,1]{1,2,3,0:T(8,128)S(1)} collective-permute-done((f32[3,32,16,1]{1,2,3,0:T(8,128)S(1)}, f32[3,32,16,1]{1,2,3,0:T(8,128)S(1)}, u32[]{:S(2)}, u32[]{:S(2)}) %collective-permute-start.5) | collective-permute-done | bytes 6176 | tf_op jit(solution)/shard_map/ppermute | solution.py:276
  16.1 4.0 %collective-permute-start.4 = (f32[3,32,16,1]{1,2,3,0:T(8,128)S(1)}, f32[3,32,16,1]{1,2,3,0:T(8,128)S(1)}, u32[]{:S(2)}, u32[]{:S(2)}) collective-permute-start(f32[3,32,16,1]{1,2,3,0:T(8,128)S(1)} %copy.6), channel_id=1, source_target_pairs={{0,1},{1,2},{2,3},{4,5},{5,6},{6,7},{8,9},{9,10},{10,11},{12,13},{... | collective-permute-start | bytes 18440 | tf_op jit(solution)/shard_map/ppermute | solution.py:275
  20.1 1.3 %copy.9.r_9_.gz_hi = f32[3,32,16,1]{3,2,1,0:T(8,128)} copy(f32[3,32,16,1]{1,2,3,0:T(8,128)S(1)} %collective-permute-done.5) | data formatting | bytes 12288 | tf_op jit(solution)/shard_map/ppermute | solution.py:276
  21.5 0.2 collective-permute-done.4
  21.6 1.3 %copy.8.r_8_.gz_lo = f32[3,32,16,1]{3,2,1,0:T(8,128)} copy(f32[3,32,16,1]{1,2,3,0:T(8,128)S(1)} %collective-permute-done.4) | data formatting | bytes 12288 | tf_op jit(solution)/shard_map/ppermute | solution.py:275
  23.0 0.6 copy-done.10
  23.6 0.0 copy-done.2
  23.6 0.6 copy-done.3
  24.3 7.5 %shard_map.59 = (f32[2,5,32,16,256]{4,3,2,1,0:T(8,128)}, f32[2,32,16,256]{3,2,1,0:T(8,128)}, f32[2,7,16,256]{3,2,1,0:T(8,128)}) custom-call(f32[32,16,256]{2,1,0:T(8,128)} %r_0_.1, s32[32,16,256]{2,1,0:T(8,128)} %pore_ref.3, s32[32,16,256]{2,1,0:T(8,128)} %lab_ref.3, f32[32,16,256]{2,1,0:T(8,128)} %r_3_.1, f32[2,16,256]{2,1,0:T(8,128)} %copy-done.10, ...), custom_call_target="tpu_custom_call" | custom-call | tf_op jit(solution)/shard_map/pallas_call | solution.py:301
  31.8 10.7 %all-gather = f32[4,7,16,256]{3,2,1,0:T(8,128)} all-gather(f32[2,7,16,256]{3,2,1,0:T(8,128)} %get-tuple-element.9), channel_id=2, replica_groups=mesh['blk'=2,'gy'=4,'gz'=4] {'blk'}, dimensions={0}, use_global_device_ids=true | all-gather | bytes 688128 | tf_op jit(solution)/shard_map/all_gather | solution.py:312
  42.5 4.2 %shard_map.60.fa_ref = f32[2,32,16,256]{3,2,1,0:T(8,128)} custom-call(s32[1]{0:T(128)} %bitcast.r_0_, f32[2,2,7,16,256]{4,3,2,1,0:T(8,128)} %bitcast.9, f32[2,2,7,16,256]{4,3,2,1,0:T(8,128)} %bitcast.10, f32[2,5,32,16,256]{4,3,2,1,0:T(8,128)} %get-tuple-element.10.r_3_.fac_ref, f32[2,32,16,256]{3,2,1,0:T(8,128)} %get-tuple-element.11.r_4_), custom_call_target="tpu_custom_call" | custom-call | tf_op jit(solution)/shard_map/pallas_call | solution.py:315
  46.7 1.3 %fusion.3 = (f32[2,32,1,256]{3,2,1,0:T(1,128)S(1)}, f32[2,32,1,256]{3,2,1,0:T(1,128)S(1)}) fusion(f32[2,32,16,256]{3,2,1,0:T(8,128)} %shard_map.60.fa_ref), kind=kLoop, calls=%fused_computation.10 | loop fusion | bytes 262144 | tf_op jit(solution)/shard_map/slice | solution.py:283
  48.0 1.3 %collective-permute-start.7 = (f32[2,32,1,256]{3,2,1,0:T(1,128)S(1)}, f32[2,32,1,256]{3,2,1,0:T(1,128)S(1)}, u32[]{:S(2)}, u32[]{:S(2)}) collective-permute-start(f32[2,32,1,256]{3,2,1,0:T(1,128)S(1)} %get-tuple-element.22), channel_id=1, source_target_pairs={{4,0},{8,4},{12,8},{5,1},{9,5},{13,9},{6,2},{10,6},{14,10},{7,3},{... | collective-permute-start | bytes 196616 | tf_op jit(solution)/shard_map/ppermute | solution.py:276
  49.3 3.0 %collective-permute-start.6 = (f32[2,32,1,256]{3,2,1,0:T(1,128)S(1)}, f32[2,32,1,256]{3,2,1,0:T(1,128)S(1)}, u32[]{:S(2)}, u32[]{:S(2)}) collective-permute-start(f32[2,32,1,256]{3,2,1,0:T(1,128)S(1)} %get-tuple-element.23), channel_id=1, source_target_pairs={{0,4},{4,8},{8,12},{1,5},{5,9},{9,13},{2,6},{6,10},{10,14},{3,7},{... | collective-permute-start | bytes 196616 | tf_op jit(solution)/shard_map/ppermute | solution.py:275
  52.4 1.4 %fusion.2 = (f32[2,32,16,1]{3,2,1,0:T(8,128)S(1)}, f32[2,32,16,1]{3,2,1,0:T(8,128)S(1)}) fusion(f32[2,32,16,256]{3,2,1,0:T(8,128)} %shard_map.60.fa_ref), kind=kLoop, calls=%fused_computation.9 | loop fusion | bytes 16384 | tf_op jit(solution)/shard_map/slice | solution.py:284
  53.8 1.3 %collective-permute-start.9 = (f32[2,32,16,1]{3,2,1,0:T(8,128)S(1)}, f32[2,32,16,1]{3,2,1,0:T(8,128)S(1)}, u32[]{:S(2)}, u32[]{:S(2)}) collective-permute-start(f32[2,32,16,1]{3,2,1,0:T(8,128)S(1)} %get-tuple-element.20), channel_id=1, source_target_pairs={{1,0},{2,1},{3,2},{5,4},{6,5},{7,6},{9,8},{10,9},{11,10},{13,12},{... | collective-permute-start | bytes 12296 | tf_op jit(solution)/shard_map/ppermute | solution.py:276
  55.1 4.6 %collective-permute-start.8 = (f32[2,32,16,1]{3,2,1,0:T(8,128)S(1)}, f32[2,32,16,1]{3,2,1,0:T(8,128)S(1)}, u32[]{:S(2)}, u32[]{:S(2)}) collective-permute-start(f32[2,32,16,1]{3,2,1,0:T(8,128)S(1)} %get-tuple-element.21), channel_id=1, source_target_pairs={{0,1},{1,2},{2,3},{4,5},{5,6},{6,7},{8,9},{9,10},{10,11},{12,13},{... | collective-permute-start | bytes 12296 | tf_op jit(solution)/shard_map/ppermute | solution.py:275
  59.6 10.2 %collective-permute-done.9.hz_hi = f32[2,32,16,1]{3,2,1,0:T(8,128)S(1)} collective-permute-done((f32[2,32,16,1]{3,2,1,0:T(8,128)S(1)}, f32[2,32,16,1]{3,2,1,0:T(8,128)S(1)}, u32[]{:S(2)}, u32[]{:S(2)}) %collective-permute-start.9) | collective-permute-done | bytes 4128 | tf_op jit(solution)/shard_map/ppermute | solution.py:276
  69.8 1.2 %collective-permute-done.8.hz_lo = f32[2,32,16,1]{3,2,1,0:T(8,128)S(1)} collective-permute-done((f32[2,32,16,1]{3,2,1,0:T(8,128)S(1)}, f32[2,32,16,1]{3,2,1,0:T(8,128)S(1)}, u32[]{:S(2)}, u32[]{:S(2)}) %collective-permute-start.8) | collective-permute-done | bytes 4128 | tf_op jit(solution)/shard_map/ppermute | solution.py:275
  71.0 0.8 copy-done.5
  71.8 0.6 copy-done.9
  72.4 7.2 %shard_map.61 = (f32[2,32,16,256]{3,2,1,0:T(8,128)}, f32[2,2,16,256]{3,2,1,0:T(8,128)}) custom-call(s32[32,16,256]{2,1,0:T(8,128)} %pore_ref.3, s32[32,16,256]{2,1,0:T(8,128)} %lab_ref.3, f32[2,32,16,256]{3,2,1,0:T(8,128)} %shard_map.60.fa_ref, f32[2,5,32,16,256]{4,3,2,1,0:T(8,128)} %get-tuple-element.10.r_3_.fac_ref, f32[3,32,1,256]{3,2,1,0:T(1,128)} %copy-done.3, ...), custom_call_target="tpu_custom_call" | custom-call | tf_op jit(solution)/shard_map/pallas_call | solution.py:324
  79.7 5.2 %all-gather.1 = f32[4,2,16,256]{3,2,1,0:T(8,128)} all-gather(f32[2,2,16,256]{3,2,1,0:T(8,128)} %get-tuple-element.12), channel_id=3, replica_groups=mesh['blk'=2,'gy'=4,'gz'=4] {'blk'}, dimensions={0}, use_global_device_ids=true | all-gather | bytes 196608 | tf_op jit(solution)/shard_map/all_gather | solution.py:334
  84.9 4.0 %shard_map.62 = (f32[32,16,256]{2,1,0:T(8,128)}, f32[32,16,256]{2,1,0:T(8,128)}) custom-call(s32[1]{0:T(128)} %bitcast.r_0_, f32[2,2,7,16,256]{4,3,2,1,0:T(8,128)} %bitcast.11, f32[2,2,2,16,256]{4,3,2,1,0:T(8,128)} %bitcast.16, f32[2,5,32,16,256]{4,3,2,1,0:T(8,128)} %get-tuple-element.10.r_3_.fac_ref, f32[2,32,16,256]{3,2,1,0:T(8,128)} %get-tuple-element.13.r_4_), custom_call_target="tpu_custom_call" | custom-call | tf_op jit(solution)/shard_map/pallas_call | solution.py:335
  88.9 1.1 fusion.5
  90.0 1.3 %collective-permute-start.11 = (f32[1,32,1,256]{3,2,1,0:T(1,128)S(1)}, f32[1,32,1,256]{3,2,1,0:T(1,128)S(1)}, u32[]{:S(2)}, u32[]{:S(2)}) collective-permute-start(f32[1,32,1,256]{3,2,1,0:T(1,128)S(1)} %get-tuple-element.26), channel_id=1, source_target_pairs={{4,0},{8,4},{12,8},{5,1},{9,5},{13,9},{6,2},{10,6},{14,10},{7,3},{... | collective-permute-start | bytes 98312 | tf_op jit(solution)/shard_map/ppermute | solution.py:276
  91.3 3.0 %collective-permute-start.10 = (f32[1,32,1,256]{3,2,1,0:T(1,128)S(1)}, f32[1,32,1,256]{3,2,1,0:T(1,128)S(1)}, u32[]{:S(2)}, u32[]{:S(2)}) collective-permute-start(f32[1,32,1,256]{3,2,1,0:T(1,128)S(1)} %get-tuple-element.27), channel_id=1, source_target_pairs={{0,4},{4,8},{8,12},{1,5},{5,9},{9,13},{2,6},{6,10},{10,14},{3,7},{... | collective-permute-start | bytes 98312 | tf_op jit(solution)/shard_map/ppermute | solution.py:275
  94.4 1.2 %fusion.4 = (f32[1,32,16,1]{3,2,1,0:T(8,128)S(1)}, f32[1,32,16,1]{3,2,1,0:T(8,128)S(1)}) fusion(f32[1,32,16,256]{3,2,1,0:T(8,128)} %bitcast.15), kind=kLoop, calls=%fused_computation.11 | loop fusion | bytes 8192 | tf_op jit(solution)/shard_map/slice | solution.py:284
  95.5 1.3 %collective-permute-start.13 = (f32[1,32,16,1]{3,2,1,0:T(8,128)S(1)}, f32[1,32,16,1]{3,2,1,0:T(8,128)S(1)}, u32[]{:S(2)}, u32[]{:S(2)}) collective-permute-start(f32[1,32,16,1]{3,2,1,0:T(8,128)S(1)} %get-tuple-element.24), channel_id=1, source_target_pairs={{1,0},{2,1},{3,2},{5,4},{6,5},{7,6},{9,8},{10,9},{11,10},{13,12},{... | collective-permute-start | bytes 6152 | tf_op jit(solution)/shard_map/ppermute | solution.py:276
  96.8 5.0 %collective-permute-start.12 = (f32[1,32,16,1]{3,2,1,0:T(8,128)S(1)}, f32[1,32,16,1]{3,2,1,0:T(8,128)S(1)}, u32[]{:S(2)}, u32[]{:S(2)}) collective-permute-start(f32[1,32,16,1]{3,2,1,0:T(8,128)S(1)} %get-tuple-element.25), channel_id=1, source_target_pairs={{0,1},{1,2},{2,3},{4,5},{5,6},{6,7},{8,9},{9,10},{10,11},{12,13},{... | collective-permute-start | bytes 6152 | tf_op jit(solution)/shard_map/ppermute | solution.py:275
  101.9 4.5 %collective-permute-done.13.hz_hi = f32[1,32,16,1]{3,2,1,0:T(8,128)S(1)} collective-permute-done((f32[1,32,16,1]{3,2,1,0:T(8,128)S(1)}, f32[1,32,16,1]{3,2,1,0:T(8,128)S(1)}, u32[]{:S(2)}, u32[]{:S(2)}) %collective-permute-start.13) | collective-permute-done | bytes 2080 | tf_op jit(solution)/shard_map/ppermute | solution.py:276
  106.4 1.2 %collective-permute-done.12.hz_lo = f32[1,32,16,1]{3,2,1,0:T(8,128)S(1)} collective-permute-done((f32[1,32,16,1]{3,2,1,0:T(8,128)S(1)}, f32[1,32,16,1]{3,2,1,0:T(8,128)S(1)}, u32[]{:S(2)}, u32[]{:S(2)}) %collective-permute-start.12) | collective-permute-done | bytes 2080 | tf_op jit(solution)/shard_map/ppermute | solution.py:275
  107.6 0.7 copy-done.7
  108.3 0.0 copy-done.12
  108.3 0.6 copy-done.13
  108.9 4.4 %shard_map.63 = f32[32,16,256]{2,1,0:T(8,128)} custom-call(s32[32,16,256]{2,1,0:T(8,128)} %pore_ref.3, s32[32,16,256]{2,1,0:T(8,128)} %lab_ref.3, f32[32,16,256]{2,1,0:T(8,128)} %get-tuple-element.15.a2_ref, f32[3,32,1,256]{3,2,1,0:T(1,128)} %copy-done.3, f32[3,32,1,256]{3,2,1,0:T(1,128)} %copy-done.2, f32[3,32,16,1]{3,2,1,0:T(8,128)} %copy.8.r_8_.gz_lo, ...), custom_call_target="tpu_custom_call" | custom-call | tf_op jit(solution)/shard_map/pallas_call | solution.py:344
  (31 shorter events, 0.1 us)
Async XLA Ops:
  0.6 1.2 %copy-start = (s32[32,16,256]{2,1,0:T(8,128)S(1)}, s32[32,16,256]{2,1,0:T(8,128)}, u32[]{:S(2)}) copy-start(s32[32,16,256]{2,1,0:T(8,128)} %pore_ref.3) | copy-start | bytes 1572868
  0.6 4.5 %copy-start.1 = (f32[32,16,256]{2,1,0:T(8,128)S(1)}, f32[32,16,256]{2,1,0:T(8,128)}, u32[]{:S(2)}) copy-start(f32[32,16,256]{2,1,0:T(8,128)} %r_0_.1) | copy-start | bytes 1572868
  2.0 21.0 %collective-permute-start = (f32[2,16,256]{2,1,0:T(8,128)S(1)}, f32[2,16,256]{2,1,0:T(8,128)S(1)}, u32[]{:S(2)}, u32[]{:S(2)}) collective-permute-start(f32[2,16,256]{2,1,0:T(8,128)S(1)} %pad_maximum_fusion.3), channel_id=1, source_target_pairs={{0,16},{16,0},{1,17},{17,1},{2,18},{18,2},{3,19},{19,3},{4,20},{20... | collective-permute-start | bytes 98312 | tf_op jit(solution)/shard_map/ppermute | solution.py:275
  5.0 18.0 %collective-permute-start.1 = (f32[2,16,256]{2,1,0:T(8,128)S(1)}, f32[2,16,256]{2,1,0:T(8,128)S(1)}, u32[]{:S(2)}, u32[]{:S(2)}) collective-permute-start(f32[2,16,256]{2,1,0:T(8,128)S(1)} %pad_maximum_fusion.4), channel_id=1, source_target_pairs={{16,0},{0,16},{17,1},{1,17},{18,2},{2,18},{19,3},{3,19},{20,4},{4,... | collective-permute-start | bytes 98312 | tf_op jit(solution)/shard_map/ppermute | solution.py:276
  5.2 17.7 %collective-permute-start.3 = (f32[3,32,1,256]{3,2,1,0:T(1,128)S(1)}, f32[3,32,1,256]{3,2,1,0:T(1,128)S(1)}, u32[]{:S(2)}, u32[]{:S(2)}) collective-permute-start(f32[3,32,1,256]{3,2,1,0:T(1,128)S(1)} %get-tuple-element.18), channel_id=1, source_target_pairs={{4,0},{8,4},{12,8},{5,1},{9,5},{13,9},{6,2},{10,6},{14,10},{7,3},{... | collective-permute-start | bytes 294920 | tf_op jit(solution)/shard_map/ppermute | solution.py:276
  6.5 16.5 %collective-permute-start.2 = (f32[3,32,1,256]{3,2,1,0:T(1,128)S(1)}, f32[3,32,1,256]{3,2,1,0:T(1,128)S(1)}, u32[]{:S(2)}, u32[]{:S(2)}) collective-permute-start(f32[3,32,1,256]{3,2,1,0:T(1,128)S(1)} %get-tuple-element.19), channel_id=1, source_target_pairs={{0,4},{4,8},{8,12},{1,5},{5,9},{9,13},{2,6},{6,10},{10,14},{3,7},{... | collective-permute-start | bytes 294920 | tf_op jit(solution)/shard_map/ppermute | solution.py:275
  10.4 5.7 %collective-permute-start.5 = (f32[3,32,16,1]{1,2,3,0:T(8,128)S(1)}, f32[3,32,16,1]{1,2,3,0:T(8,128)S(1)}, u32[]{:S(2)}, u32[]{:S(2)}) collective-permute-start(f32[3,32,16,1]{1,2,3,0:T(8,128)S(1)} %copy.7), channel_id=1, source_target_pairs={{1,0},{2,1},{3,2},{5,4},{6,5},{7,6},{9,8},{10,9},{11,10},{13,12},{... | collective-permute-start | bytes 18440 | tf_op jit(solution)/shard_map/ppermute | solution.py:276
  16.1 5.5 %collective-permute-start.4 = (f32[3,32,16,1]{1,2,3,0:T(8,128)S(1)}, f32[3,32,16,1]{1,2,3,0:T(8,128)S(1)}, u32[]{:S(2)}, u32[]{:S(2)}) collective-permute-start(f32[3,32,16,1]{1,2,3,0:T(8,128)S(1)} %copy.6), channel_id=1, source_target_pairs={{0,1},{1,2},{2,3},{4,5},{5,6},{6,7},{8,9},{9,10},{10,11},{12,13},{... | collective-permute-start | bytes 18440 | tf_op jit(solution)/shard_map/ppermute | solution.py:275
  23.0 0.6 copy-start.10
  23.0 0.6 copy-start.11
  23.0 0.6 copy-start.2
  23.6 0.6 copy-start.3
  48.0 23.0 %collective-permute-start.7 = (f32[2,32,1,256]{3,2,1,0:T(1,128)S(1)}, f32[2,32,1,256]{3,2,1,0:T(1,128)S(1)}, u32[]{:S(2)}, u32[]{:S(2)}) collective-permute-start(f32[2,32,1,256]{3,2,1,0:T(1,128)S(1)} %get-tuple-element.22), channel_id=1, source_target_pairs={{4,0},{8,4},{12,8},{5,1},{9,5},{13,9},{6,2},{10,6},{14,10},{7,3},{... | collective-permute-start | bytes 196616 | tf_op jit(solution)/shard_map/ppermute | solution.py:276
  49.3 21.7 %collective-permute-start.6 = (f32[2,32,1,256]{3,2,1,0:T(1,128)S(1)}, f32[2,32,1,256]{3,2,1,0:T(1,128)S(1)}, u32[]{:S(2)}, u32[]{:S(2)}) collective-permute-start(f32[2,32,1,256]{3,2,1,0:T(1,128)S(1)} %get-tuple-element.23), channel_id=1, source_target_pairs={{0,4},{4,8},{8,12},{1,5},{5,9},{9,13},{2,6},{6,10},{10,14},{3,7},{... | collective-permute-start | bytes 196616 | tf_op jit(solution)/shard_map/ppermute | solution.py:275
  53.8 16.1 %collective-permute-start.9 = (f32[2,32,16,1]{3,2,1,0:T(8,128)S(1)}, f32[2,32,16,1]{3,2,1,0:T(8,128)S(1)}, u32[]{:S(2)}, u32[]{:S(2)}) collective-permute-start(f32[2,32,16,1]{3,2,1,0:T(8,128)S(1)} %get-tuple-element.20), channel_id=1, source_target_pairs={{1,0},{2,1},{3,2},{5,4},{6,5},{7,6},{9,8},{10,9},{11,10},{13,12},{... | collective-permute-start | bytes 12296 | tf_op jit(solution)/shard_map/ppermute | solution.py:276
  55.1 15.9 %collective-permute-start.8 = (f32[2,32,16,1]{3,2,1,0:T(8,128)S(1)}, f32[2,32,16,1]{3,2,1,0:T(8,128)S(1)}, u32[]{:S(2)}, u32[]{:S(2)}) collective-permute-start(f32[2,32,16,1]{3,2,1,0:T(8,128)S(1)} %get-tuple-element.21), channel_id=1, source_target_pairs={{0,1},{1,2},{2,3},{4,5},{5,6},{6,7},{8,9},{9,10},{10,11},{12,13},{... | collective-permute-start | bytes 12296 | tf_op jit(solution)/shard_map/ppermute | solution.py:275
  69.8 1.2 %copy-start.4 = (f32[2,32,16,1]{3,2,1,0:T(8,128)}, f32[2,32,16,1]{3,2,1,0:T(8,128)S(1)}, u32[]{:S(2)}) copy-start(f32[2,32,16,1]{3,2,1,0:T(8,128)S(1)} %collective-permute-done.9.hz_hi) | copy-start | bytes 12292
  71.0 0.8 copy-start.5
  71.0 0.8 copy-start.8
  71.8 0.6 copy-start.9
  90.0 17.6 %collective-permute-start.11 = (f32[1,32,1,256]{3,2,1,0:T(1,128)S(1)}, f32[1,32,1,256]{3,2,1,0:T(1,128)S(1)}, u32[]{:S(2)}, u32[]{:S(2)}) collective-permute-start(f32[1,32,1,256]{3,2,1,0:T(1,128)S(1)} %get-tuple-element.26), channel_id=1, source_target_pairs={{4,0},{8,4},{12,8},{5,1},{9,5},{13,9},{6,2},{10,6},{14,10},{7,3},{... | collective-permute-start | bytes 98312 | tf_op jit(solution)/shard_map/ppermute | solution.py:276
  91.3 16.3 %collective-permute-start.10 = (f32[1,32,1,256]{3,2,1,0:T(1,128)S(1)}, f32[1,32,1,256]{3,2,1,0:T(1,128)S(1)}, u32[]{:S(2)}, u32[]{:S(2)}) collective-permute-start(f32[1,32,1,256]{3,2,1,0:T(1,128)S(1)} %get-tuple-element.27), channel_id=1, source_target_pairs={{0,4},{4,8},{8,12},{1,5},{5,9},{9,13},{2,6},{6,10},{10,14},{3,7},{... | collective-permute-start | bytes 98312 | tf_op jit(solution)/shard_map/ppermute | solution.py:275
  95.5 10.9 %collective-permute-start.13 = (f32[1,32,16,1]{3,2,1,0:T(8,128)S(1)}, f32[1,32,16,1]{3,2,1,0:T(8,128)S(1)}, u32[]{:S(2)}, u32[]{:S(2)}) collective-permute-start(f32[1,32,16,1]{3,2,1,0:T(8,128)S(1)} %get-tuple-element.24), channel_id=1, source_target_pairs={{1,0},{2,1},{3,2},{5,4},{6,5},{7,6},{9,8},{10,9},{11,10},{13,12},{... | collective-permute-start | bytes 6152 | tf_op jit(solution)/shard_map/ppermute | solution.py:276
  96.8 10.7 %collective-permute-start.12 = (f32[1,32,16,1]{3,2,1,0:T(8,128)S(1)}, f32[1,32,16,1]{3,2,1,0:T(8,128)S(1)}, u32[]{:S(2)}, u32[]{:S(2)}) collective-permute-start(f32[1,32,16,1]{3,2,1,0:T(8,128)S(1)} %get-tuple-element.25), channel_id=1, source_target_pairs={{0,1},{1,2},{2,3},{4,5},{5,6},{6,7},{8,9},{9,10},{10,11},{12,13},{... | collective-permute-start | bytes 6152 | tf_op jit(solution)/shard_map/ppermute | solution.py:275
  106.4 1.2 %copy-start.6 = (f32[1,32,16,1]{3,2,1,0:T(8,128)}, f32[1,32,16,1]{3,2,1,0:T(8,128)S(1)}, u32[]{:S(2)}) copy-start(f32[1,32,16,1]{3,2,1,0:T(8,128)S(1)} %collective-permute-done.13.hz_hi) | copy-start | bytes 6148
  107.6 0.7 copy-start.7
  107.6 0.7 copy-start.12
  108.3 0.6 copy-start.13
where the time goes:
time: 114 us; the launch traced here: 113 us
  starting transfers between devices  33.6 us (29%)
  Pallas kernels  27.4 us (24%)
  waiting for transfers between devices  21.3 us (19%)
  blocking collectives  16 us (14%)
  local copies, waits for them, and re-layouts  12.6 us (11%)
  other arithmetic  1.54 us (1%)
    ppermute x7, starting transfers between devices, _exchange(): lo = lax.ppermute(last, axis, forward)  25.7 us
    ppermute x7, waiting for transfers between devices, _exchange(): hi = lax.ppermute(first, axis, backward)  18.7 us
    all_gather x1, blocking collectives, shards(): gathered = lax.all_gather(rows, 'blk', axis=0, tiled=False)  10.7 us
    ppermute x7, starting transfers between devices, _exchange(): hi = lax.ppermute(first, axis, backward)  7.83 us
    pallas_call x1, Pallas kernels, shards(): pl.pallas_call(lambda *r: _prep_kernel(cycle_step, *r), out_shape=(jax.Sh...  7.54 us
    pallas_call x1, Pallas kernels, shards(): pl.pallas_call(_second_kernel, out_shape=(jax.ShapeDtypeStruct((2, m, ny,...  7.24 us
    all_gather x1, blocking collectives, shards(): gathered2 = lax.all_gather(vals2, 'blk', axis=0, tiled=False)  5.24 us
    pallas_call x1, Pallas kernels, shards(): pl.pallas_call(_gradient_kernel, out_shape=shape, in_specs=[_vmem()] * 11...  4.36 us
  transfers between devices with their start and end apart: 14, of which 6 were waited for; matrix products, arithmetic and copies ran while one was open for 6% of the time, Pallas kernels for 0%

commit v1 on v0

--- a/solution.py
+++ b/solution.py
@@ -60,11 +60,15 @@
     return total
 
 
+def _yrow(ref, c, i):
+    return ref[c, pl.ds(i, 1), :]
+
+
 def _geo_row(i, pore_ref, lab_ref, gy_lo, gy_hi, gz_lo, gz_hi):
     mob = 1.0 + 2.0 * pore_ref[i].astype(F32)
     lab = lab_ref[i].astype(F32)
-    mob_n = _neighbours(mob, gy_lo[0, i], gy_hi[0, i], gz_lo[0, i], gz_hi[0, i])
-    lab_n = _neighbours(lab, gy_lo[1, i], gy_hi[1, i], gz_lo[1, i], gz_hi[1, i])
+    mob_n = _neighbours(mob, _yrow(gy_lo, 0, i), _yrow(gy_hi, 0, i), gz_lo[0, i], gz_hi[0, i])
+    lab_n = _neighbours(lab, _yrow(gy_lo, 1, i), _yrow(gy_hi, 1, i), gz_lo[1, i], gz_hi[1, i])
     return mob, lab, mob_n, _faces(mob, lab, mob_n, lab_n)
 
 
@@ -121,7 +125,7 @@
         mob, lab, mob_n, fc = _geo_row(i, pore_ref, lab_ref, gy_lo, gy_hi, gz_lo, gz_hi)
         v = vac_ref[i]
         u = w_ext[i + 1] * v
-        v_n = _neighbours(v, gy_lo[2, i], gy_hi[2, i], gz_lo[2, i], gz_hi[2, i])
+        v_n = _neighbours(v, _yrow(gy_lo, 2, i), _yrow(gy_hi, 2, i), gz_lo[2, i], gz_hi[2, i])
         u_n = [0.5 * (1.0 + mn) * vn for mn, vn in zip(mob_n, v_n)]
         src_f.append(v + cross_rate * (1.0 * _flux(u, u_n, fc)))
     src_a = [cot_ref[r] for r in range(m)]
@@ -231,11 +235,11 @@
         mob, lab, mob_n, fc = _geo_row(i, pore_ref, lab_ref, gy_lo, gy_hi, gz_lo, gz_hi)
         w = 0.5 * (1.0 + mob)
         f1 = fa_ref[0, i]
-        f_n = _neighbours(f1, hy_lo[0, i], hy_hi[0, i], hz_lo[0, i], hz_hi[0, i])
+        f_n = _neighbours(f1, _yrow(hy_lo, 0, i), _yrow(hy_hi, 0, i), hz_lo[0, i], hz_hi[0, i])
         u_n = [0.5 * (1.0 + mn) * fn for mn, fn in zip(mob_n, f_n)]
         srcs[0].append(f1 + cross_rate * (1.0 * _flux(w * f1, u_n, fc)))
         a1 = fa_ref[1, i]
-        a_n = _neighbours(a1, hy_lo[1, i], hy_hi[1, i], hz_lo[1, i], hz_hi[1, i])
+        a_n = _neighbours(a1, _yrow(hy_lo, 1, i), _yrow(hy_hi, 1, i), hz_lo[1, i], hz_hi[1, i])
         srcs[1].append(a1 + cross_rate * (w * _flux(a1, a_n, fc)))
     zero = jnp.zeros(pore_ref.shape[1:], F32)
     for c in range(2):
@@ -257,7 +261,7 @@
         mob, lab, mob_n, fc = _geo_row(i, pore_ref, lab_ref, gy_lo, gy_hi, gz_lo, gz_hi)
         w = 0.5 * (1.0 + mob)
         a2 = a2_ref[i]
-        a_n = _neighbours(a2, hy_lo[0, i], hy_hi[0, i], hz_lo[0, i], hz_hi[0, i])
+        a_n = _neighbours(a2, _yrow(hy_lo, 0, i), _yrow(hy_hi, 0, i), hz_lo[0, i], hz_hi[0, i])
         out_ref[i] = a2 + cross_rate * (w * _flux(a2, a_n, fc))
 
 
@@ -277,12 +281,16 @@
     return lo, hi
 
 
-def _yz_halos(stack):
-    y = stack.shape[2]
-    z = stack.shape[3]
-    gy_lo, gy_hi = _exchange(stack[:, :, 0:1, :], stack[:, :, y - 1 : y, :], "gy", False)
-    gz_lo, gz_hi = _exchange(stack[:, :, :, 0:1], stack[:, :, :, z - 1 : z], "gz", False)
-    return gy_lo, gy_hi, gz_lo, gz_hi
+def _yz_halos(fields):
+    y = fields[0].shape[1]
+    z = fields[0].shape[2]
+    gy_lo, gy_hi = _exchange(
+        jnp.stack([f[:, 0, :] for f in fields]), jnp.stack([f[:, y - 1, :] for f in fields]), "gy", False
+    )
+    gz_lo, gz_hi = _exchange(
+        jnp.stack([f[:, :, 0] for f in fields]), jnp.stack([f[:, :, z - 1] for f in fields]), "gz", False
+    )
+    return gy_lo, gy_hi, gz_lo[..., None], gz_hi[..., None]
 
 
 def shards(vacancy, grain_label, pore_mask, cotangent):
@@ -296,7 +304,7 @@
     geo0 = jnp.stack([mobility[0], labels[0]])
     geo1 = jnp.stack([mobility[m - 1], labels[m - 1]])
     bx_lo, bx_hi = _exchange(geo0, geo1, "blk", True)
-    gy_lo, gy_hi, gz_lo, gz_hi = _yz_halos(jnp.stack([mobility, labels, vacancy]))
+    gy_lo, gy_hi, gz_lo, gz_hi = _yz_halos([mobility, labels, vacancy])
 
     fac, loc, rows = pl.pallas_call(
         lambda *r: _prep_kernel(cycle_step, *r),
@@ -320,7 +328,7 @@
         scratch_shapes=[pltpu.VMEM((n_blk, ny, nz), F32)],
     )(pos, gathered, gathered, fac, loc)
 
-    hy_lo, hy_hi, hz_lo, hz_hi = _yz_halos(fa)
+    hy_lo, hy_hi, hz_lo, hz_hi = _yz_halos([fa[0], fa[1]])
     loc2, vals2 = pl.pallas_call(
         _second_kernel,
         out_shape=(
@@ -340,7 +348,7 @@
         scratch_shapes=[pltpu.VMEM((n_blk, ny, nz), F32)],
     )(pos, gathered, gathered2, fac, loc2)
 
-    a2_lo, a2_hi, a2z_lo, a2z_hi = _yz_halos(adjoint_two[None])
+    a2_lo, a2_hi, a2z_lo, a2z_hi = _yz_halos([adjoint_two])
     gradient = pl.pallas_call(
         _gradient_kernel,
         out_shape=shape,

time: 114 us -> 105 us (0.921)
  the two profiles are of different devices: /device:TPU:0 before, /device:TPU:28 now
where the time goes in v1:
time: 105 us; the launch traced here: 104 us
  starting transfers between devices  30 us (29%)
  Pallas kernels  27.4 us (26%)
  local copies, waits for them, and re-layouts  18.3 us (17%)
  blocking collectives  14.5 us (14%)
  waiting for transfers between devices  10.9 us (10%)
  other arithmetic  2.31 us (2%)
    ppermute x7, starting transfers between devices, _exchange(): hi = lax.ppermute(first, axis, backward)  18.3 us
    ppermute x7, starting transfers between devices, _exchange(): lo = lax.ppermute(last, axis, forward)  11.7 us
    ppermute x7, waiting for transfers between devices, _exchange(): lo = lax.ppermute(last, axis, forward)  9.98 us
    all_gather x1, blocking collectives, shards(): gathered = lax.all_gather(rows, 'blk', axis=0, tiled=False)  9.27 us
    pallas_call x1, Pallas kernels, shards(): pl.pallas_call(lambda *r: _prep_kernel(cycle_step, *r), out_shape=(jax.Sh...  7.54 us
    pallas_call x1, Pallas kernels, shards(): pl.pallas_call(_second_kernel, out_shape=(jax.ShapeDtypeStruct((2, m, ny,...  7.23 us
    broadcast_in_dim x6, local copies, waits for them, and re-layouts, _yz_halos(): return (gy_lo, gy_hi, gz_lo[..., None], gz_hi[..., None])  6.58 us
    all_gather x1, blocking collectives, shards(): gathered2 = lax.all_gather(vals2, 'blk', axis=0, tiled=False)  5.24 us
  transfers between devices with their start and end apart: 14, of which 4 were waited for; matrix products, arithmetic and copies ran while one was open for 10% of the time, Pallas kernels for 0%

profile of v1, /device:TPU:28, one launch (start us, length us, event | category | flops | bytes accessed | tf_op | source)
XLA Modules:
  0.0 104.4 jit_solution(4459421954314932142)
XLA Ops:
  0.6 1.1 %convert_element_type.7 = f32[32,16,256]{2,1,0:T(8,128)S(1)} convert(s32[32,16,256]{2,1,0:T(8,128)} %lab_ref.3) | non-fusion elementwise | flops 131072 | bytes 1048576 | tf_op jit(solution)/shard_map/convert_element_type | solution.py:303
  1.8 1.1 %multiply_add_fusion = f32[32,16,256]{2,1,0:T(8,128)S(1)} fusion(s32[32,16,256]{2,1,0:T(8,128)} %pore_ref.3), kind=kLoop, calls=%fused_computation.2 | loop fusion | flops 393216 | bytes 1048576 | tf_op jit(solution)/shard_map/add | solution.py:302
  2.9 1.6 %collective-permute-start = (f32[2,16,256]{2,1,0:T(8,128)S(1)}, f32[2,16,256]{2,1,0:T(8,128)S(1)}, u32[]{:S(2)}, u32[]{:S(2)}) collective-permute-start(f32[2,16,256]{2,1,0:T(8,128)S(1)} %pad_maximum_fusion.4), channel_id=1, source_target_pairs={{0,16},{16,0},{1,17},{17,1},{2,18},{18,2},{3,19},{19,3},{4,20},{20... | collective-permute-start | bytes 98312 | tf_op jit(solution)/shard_map/ppermute | solution.py:279
  4.5 0.5 collective-permute-start.1
  5.1 1.1 %fusion.10 = (f32[32,1,256]{2,1,0:T(1,128)S(1)}, f32[32,1,256]{2,1,0:T(1,128)S(1)}) fusion(f32[32,16,256]{2,1,0:T(8,128)} %r_0_.1), kind=kLoop, calls=%fused_computation.35 | loop fusion | bytes 131072 | tf_op jit(solution)/shard_map/slice | solution.py:288
  6.3 1.9 %collective-permute-start.2 = (f32[3,32,256]{2,1,0:T(8,128)S(1)}, f32[3,32,256]{2,1,0:T(8,128)S(1)}, u32[]{:S(2)}, u32[]{:S(2)}) collective-permute-start(f32[3,32,256]{2,1,0:T(8,128)S(1)} %pad_maximum_fusion), channel_id=1, source_target_pairs={{0,4},{4,8},{8,12},{1,5},{5,9},{9,13},{2,6},{6,10},{10,14},{3,7},{... | collective-permute-start | bytes 294920 | tf_op jit(solution)/shard_map/ppermute | solution.py:279
  8.2 3.6 %collective-permute-start.3 = (f32[3,32,256]{2,1,0:T(8,128)S(1)}, f32[3,32,256]{2,1,0:T(8,128)S(1)}, u32[]{:S(2)}, u32[]{:S(2)}) collective-permute-start(f32[3,32,256]{2,1,0:T(8,128)S(1)} %pad_maximum_fusion.1), channel_id=1, source_target_pairs={{4,0},{8,4},{12,8},{5,1},{9,5},{13,9},{6,2},{10,6},{14,10},{7,3},{... | collective-permute-start | bytes 294920 | tf_op jit(solution)/shard_map/ppermute | solution.py:280
  12.3 0.2 copy.208
  12.9 2.3 %collective-permute-start.5 = (f32[3,32,16]{1,2,0:T(8,128)S(1)}, f32[3,32,16]{1,2,0:T(8,128)S(1)}, u32[]{:S(2)}, u32[]{:S(2)}) collective-permute-start(f32[3,32,16]{1,2,0:T(8,128)S(1)} %pad_maximum_fusion.7), channel_id=1, source_target_pairs={{1,0},{2,1},{3,2},{5,4},{6,5},{7,6},{9,8},{10,9},{11,10},{13,12},{... | collective-permute-start | bytes 18440 | tf_op jit(solution)/shard_map/ppermute | solution.py:280
  15.2 0.2 copy.205
  15.8 0.9 collective-permute-done.5
  16.7 1.3 %collective-permute-start.4 = (f32[3,32,16]{1,2,0:T(8,128)S(1)}, f32[3,32,16]{1,2,0:T(8,128)S(1)}, u32[]{:S(2)}, u32[]{:S(2)}) collective-permute-start(f32[3,32,16]{1,2,0:T(8,128)S(1)} %pad_maximum_fusion.6), channel_id=1, source_target_pairs={{0,1},{1,2},{2,3},{4,5},{5,6},{6,7},{8,9},{9,10},{10,11},{12,13},{... | collective-permute-start | bytes 18440 | tf_op jit(solution)/shard_map/ppermute | solution.py:279
  18.0 1.3 %copy.211.r_9_.gz_hi = f32[3,32,16,1]{3,2,1,0:T(8,128)} copy(f32[3,32,16,1]{1,2,3,0:T(8,128)S(1)} %bitcast.75) | data formatting | bytes 12288 | tf_op jit(solution)/shard_map/broadcast_in_dim | solution.py:293
  19.3 3.4 %collective-permute-done.4 = f32[3,32,16]{1,2,0:T(8,128)S(1)} collective-permute-done((f32[3,32,16]{1,2,0:T(8,128)S(1)}, f32[3,32,16]{1,2,0:T(8,128)S(1)}, u32[]{:S(2)}, u32[]{:S(2)}) %collective-permute-start.4) | collective-permute-done | bytes 6176 | tf_op jit(solution)/shard_map/ppermute | solution.py:279
  22.7 1.3 %copy.210.r_8_.gz_lo = f32[3,32,16,1]{3,2,1,0:T(8,128)} copy(f32[3,32,16,1]{1,2,3,0:T(8,128)S(1)} %bitcast.76) | data formatting | bytes 12288 | tf_op jit(solution)/shard_map/broadcast_in_dim | solution.py:293
  24.1 0.6 copy-done.5
  24.7 0.6 copy-done.2
  25.4 7.5 %shard_map.59 = (f32[2,5,32,16,256]{4,3,2,1,0:T(8,128)}, f32[2,32,16,256]{3,2,1,0:T(8,128)}, f32[2,7,16,256]{3,2,1,0:T(8,128)}) custom-call(f32[32,16,256]{2,1,0:T(8,128)} %r_0_.1, s32[32,16,256]{2,1,0:T(8,128)} %pore_ref.3, s32[32,16,256]{2,1,0:T(8,128)} %lab_ref.3, f32[32,16,256]{2,1,0:T(8,128)} %r_3_.1, f32[2,16,256]{2,1,0:T(8,128)} %copy-done.5, ...), custom_call_target="tpu_custom_call" | custom-call | tf_op jit(solution)/shard_map/pallas_call | solution.py:309
  32.9 9.3 %all-gather = f32[4,7,16,256]{3,2,1,0:T(8,128)} all-gather(f32[2,7,16,256]{3,2,1,0:T(8,128)} %get-tuple-element.9), channel_id=2, replica_groups=mesh['blk'=2,'gy'=4,'gz'=4] {'blk'}, dimensions={0}, use_global_device_ids=true | all-gather | bytes 688128 | tf_op jit(solution)/shard_map/all_gather | solution.py:320
  42.2 4.2 %shard_map.60.fa_ref = f32[2,32,16,256]{3,2,1,0:T(8,128)} custom-call(s32[1]{0:T(128)} %bitcast.r_0_, f32[2,2,7,16,256]{4,3,2,1,0:T(8,128)} %bitcast.55, f32[2,2,7,16,256]{4,3,2,1,0:T(8,128)} %bitcast.56, f32[2,5,32,16,256]{4,3,2,1,0:T(8,128)} %get-tuple-element.10.r_3_.fac_ref, f32[2,32,16,256]{3,2,1,0:T(8,128)} %get-tuple-element.11.r_4_), custom_call_target="tpu_custom_call" | custom-call | tf_op jit(solution)/shard_map/pallas_call | solution.py:323
  46.4 1.3 %slice_bitcast_fusion.1 = (f32[32,16,256]{2,1,0:T(8,128)S(1)}, f32[32,16,256]{2,1,0:T(8,128)S(1)}) fusion(f32[2,32,16,256]{3,2,1,0:T(8,128)} %shard_map.60.fa_ref), kind=kLoop, calls=%fused_computation.1 | loop fusion | bytes 2097152 | tf_op jit(solution)/shard_map/squeeze | solution.py:331
  48.0 0.2 copy.214
  48.8 3.9 %collective-permute-start.9 = (f32[2,32,16]{1,2,0:T(8,128)S(1)}, f32[2,32,16]{1,2,0:T(8,128)S(1)}, u32[]{:S(2)}, u32[]{:S(2)}) collective-permute-start(f32[2,32,16]{1,2,0:T(8,128)S(1)} %pad_maximum_fusion.9), channel_id=1, source_target_pairs={{1,0},{2,1},{3,2},{5,4},{6,5},{7,6},{9,8},{10,9},{11,10},{13,12},{... | collective-permute-start | bytes 12296 | tf_op jit(solution)/shard_map/ppermute | solution.py:280
  52.7 1.9 %collective-permute-start.6 = (f32[2,32,256]{2,1,0:T(8,128)S(1)}, f32[2,32,256]{2,1,0:T(8,128)S(1)}, u32[]{:S(2)}, u32[]{:S(2)}) collective-permute-start(f32[2,32,256]{2,1,0:T(8,128)S(1)} %pad_maximum_fusion.2), channel_id=1, source_target_pairs={{0,4},{4,8},{8,12},{1,5},{5,9},{9,13},{2,6},{6,10},{10,14},{3,7},{... | collective-permute-start | bytes 196616 | tf_op jit(solution)/shard_map/ppermute | solution.py:279
  54.7 3.6 %collective-permute-start.7 = (f32[2,32,256]{2,1,0:T(8,128)S(1)}, f32[2,32,256]{2,1,0:T(8,128)S(1)}, u32[]{:S(2)}, u32[]{:S(2)}) collective-permute-start(f32[2,32,256]{2,1,0:T(8,128)S(1)} %pad_maximum_fusion.3), channel_id=1, source_target_pairs={{4,0},{8,4},{12,8},{5,1},{9,5},{13,9},{6,2},{10,6},{14,10},{7,3},{... | collective-permute-start | bytes 196616 | tf_op jit(solution)/shard_map/ppermute | solution.py:280
  58.3 1.3 %collective-permute-start.8 = (f32[2,32,16]{1,2,0:T(8,128)S(1)}, f32[2,32,16]{1,2,0:T(8,128)S(1)}, u32[]{:S(2)}, u32[]{:S(2)}) collective-permute-start(f32[2,32,16]{1,2,0:T(8,128)S(1)} %pad_maximum_fusion.8), channel_id=1, source_target_pairs={{0,1},{1,2},{2,3},{4,5},{5,6},{6,7},{8,9},{9,10},{10,11},{12,13},{... | collective-permute-start | bytes 12296 | tf_op jit(solution)/shard_map/ppermute | solution.py:279
  59.7 1.1 %copy.219.hz_hi = f32[2,32,16,1]{3,2,1,0:T(8,128)} copy(f32[2,32,16,1]{1,2,3,0:T(8,128)S(1)} %bitcast.77) | data formatting | bytes 8192 | tf_op jit(solution)/shard_map/broadcast_in_dim | solution.py:293
  60.7 3.2 %collective-permute-done.8 = f32[2,32,16]{1,2,0:T(8,128)S(1)} collective-permute-done((f32[2,32,16]{1,2,0:T(8,128)S(1)}, f32[2,32,16]{1,2,0:T(8,128)S(1)}, u32[]{:S(2)}, u32[]{:S(2)}) %collective-permute-start.8) | collective-permute-done | bytes 4128 | tf_op jit(solution)/shard_map/ppermute | solution.py:279
  64.0 1.1 %copy.218.hz_lo = f32[2,32,16,1]{3,2,1,0:T(8,128)} copy(f32[2,32,16,1]{1,2,3,0:T(8,128)S(1)} %bitcast.78) | data formatting | bytes 8192 | tf_op jit(solution)/shard_map/broadcast_in_dim | solution.py:293
  65.1 0.6 copy-done.3
  65.7 0.6 copy-done.4
  66.3 7.2 %shard_map.61 = (f32[2,32,16,256]{3,2,1,0:T(8,128)}, f32[2,2,16,256]{3,2,1,0:T(8,128)}) custom-call(s32[32,16,256]{2,1,0:T(8,128)} %pore_ref.3, s32[32,16,256]{2,1,0:T(8,128)} %lab_ref.3, f32[2,32,16,256]{3,2,1,0:T(8,128)} %shard_map.60.fa_ref, f32[2,5,32,16,256]{4,3,2,1,0:T(8,128)} %get-tuple-element.10.r_3_.fac_ref, f32[3,32,256]{2,1,0:T(8,128)} %copy-done.1, ...), custom_call_target="tpu_custom_call" | custom-call | tf_op jit(solution)/shard_map/pallas_call | solution.py:332
  73.5 5.2 %all-gather.1 = f32[4,2,16,256]{3,2,1,0:T(8,128)} all-gather(f32[2,2,16,256]{3,2,1,0:T(8,128)} %get-tuple-element.12), channel_id=3, replica_groups=mesh['blk'=2,'gy'=4,'gz'=4] {'blk'}, dimensions={0}, use_global_device_ids=true | all-gather | bytes 196608 | tf_op jit(solution)/shard_map/all_gather | solution.py:342
  78.8 4.0 %shard_map.62 = (f32[32,16,256]{2,1,0:T(8,128)}, f32[32,16,256]{2,1,0:T(8,128)}) custom-call(s32[1]{0:T(128)} %bitcast.r_0_, f32[2,2,7,16,256]{4,3,2,1,0:T(8,128)} %bitcast.57, f32[2,2,2,16,256]{4,3,2,1,0:T(8,128)} %bitcast.58, f32[2,5,32,16,256]{4,3,2,1,0:T(8,128)} %get-tuple-element.10.r_3_.fac_ref, f32[2,32,16,256]{3,2,1,0:T(8,128)} %get-tuple-element.13.r_4_), custom_call_target="tpu_custom_call" | custom-call | tf_op jit(solution)/shard_map/pallas_call | solution.py:343
  82.8 1.3 %copy.220 = f32[32,16,256]{2,0,1:T(8,128)S(1)} copy(f32[32,16,256]{2,1,0:T(8,128)} %get-tuple-element.15.a2_ref) | data formatting | bytes 1048576 | tf_op jit(solution)/shard_map/pallas_call | solution.py:343
  84.2 1.9 %collective-permute-start.11 = (f32[1,32,256]{2,1,0:T(8,128)S(1)}, f32[1,32,256]{2,1,0:T(8,128)S(1)}, u32[]{:S(2)}, u32[]{:S(2)}) collective-permute-start(f32[1,32,256]{2,1,0:T(8,128)S(1)} %get-tuple-element.20), channel_id=1, source_target_pairs={{4,0},{8,4},{12,8},{5,1},{9,5},{13,9},{6,2},{10,6},{14,10},{7,3},{... | collective-permute-start | bytes 98312 | tf_op jit(solution)/shard_map/ppermute | solution.py:280
  86.1 2.4 %collective-permute-start.10 = (f32[1,32,256]{2,1,0:T(8,128)S(1)}, f32[1,32,256]{2,1,0:T(8,128)S(1)}, u32[]{:S(2)}, u32[]{:S(2)}) collective-permute-start(f32[1,32,256]{2,1,0:T(8,128)S(1)} %get-tuple-element.21), channel_id=1, source_target_pairs={{0,4},{4,8},{8,12},{1,5},{5,9},{9,13},{2,6},{6,10},{10,14},{3,7},{... | collective-permute-start | bytes 98312 | tf_op jit(solution)/shard_map/ppermute | solution.py:279
  88.5 1.2 %fusion = (f32[32,16,1]{2,1,0:T(8,128)S(1)}, f32[32,16,1]{2,1,0:T(8,128)S(1)}) fusion(f32[32,16,256]{2,1,0:T(8,128)} %get-tuple-element.15.a2_ref), kind=kLoop, calls=%fused_computation.25 | loop fusion | bytes 8192 | tf_op jit(solution)/shard_map/slice | solution.py:291
  89.7 0.2 copy.223
  89.9 2.4 %collective-permute-start.13 = (f32[1,32,16]{1,2,0:T(8,128)S(1)}, f32[1,32,16]{1,2,0:T(8,128)S(1)}, u32[]{:S(2)}, u32[]{:S(2)}) collective-permute-start(f32[1,32,16]{1,2,0:T(8,128)S(1)} %bitcast.79), channel_id=1, source_target_pairs={{1,0},{2,1},{3,2},{5,4},{6,5},{7,6},{9,8},{10,9},{11,10},{13,12},{... | collective-permute-start | bytes 6152 | tf_op jit(solution)/shard_map/ppermute | solution.py:280
  92.2 0.2 copy.222
  92.4 1.3 %collective-permute-start.12 = (f32[1,32,16]{1,2,0:T(8,128)S(1)}, f32[1,32,16]{1,2,0:T(8,128)S(1)}, u32[]{:S(2)}, u32[]{:S(2)}) collective-permute-start(f32[1,32,16]{1,2,0:T(8,128)S(1)} %bitcast.81), channel_id=1, source_target_pairs={{0,1},{1,2},{2,3},{4,5},{5,6},{6,7},{8,9},{9,10},{10,11},{12,13},{... | collective-permute-start | bytes 6152 | tf_op jit(solution)/shard_map/ppermute | solution.py:279
  93.7 0.9 copy.227.hz_hi
  94.6 3.4 %collective-permute-done.12 = f32[1,32,16]{1,2,0:T(8,128)S(1)} collective-permute-done((f32[1,32,16]{1,2,0:T(8,128)S(1)}, f32[1,32,16]{1,2,0:T(8,128)S(1)}, u32[]{:S(2)}, u32[]{:S(2)}) %collective-permute-start.12) | collective-permute-done | bytes 2080 | tf_op jit(solution)/shard_map/ppermute | solution.py:279
  98.0 0.9 copy.226.hz_lo
  98.8 0.6 copy-done.7
  99.4 0.6 copy-done.8
  100.0 4.4 %shard_map.63 = f32[32,16,256]{2,1,0:T(8,128)} custom-call(s32[32,16,256]{2,1,0:T(8,128)} %pore_ref.3, s32[32,16,256]{2,1,0:T(8,128)} %lab_ref.3, f32[32,16,256]{2,1,0:T(8,128)} %get-tuple-element.15.a2_ref, f32[3,32,256]{2,1,0:T(8,128)} %copy-done.1, f32[3,32,256]{2,1,0:T(8,128)} %copy-done.2, f32[3,32,16,1]{3,2,1,0:T(8,128)} %copy.210.r_8_.gz_lo, ...), custom_call_target="tpu_custom_call" | custom-call | tf_op jit(solution)/shard_map/pallas_call | solution.py:352
  (58 shorter events, 2.4 us)
Async XLA Ops:
  0.6 11.5 %copy-start = (f32[32,16,256]{2,1,0:T(8,128)S(1)}, f32[32,16,256]{2,1,0:T(8,128)}, u32[]{:S(2)}) copy-start(f32[32,16,256]{2,1,0:T(8,128)} %r_0_.1) | copy-start | bytes 1572868
  2.9 21.1 %collective-permute-start = (f32[2,16,256]{2,1,0:T(8,128)S(1)}, f32[2,16,256]{2,1,0:T(8,128)S(1)}, u32[]{:S(2)}, u32[]{:S(2)}) collective-permute-start(f32[2,16,256]{2,1,0:T(8,128)S(1)} %pad_maximum_fusion.4), channel_id=1, source_target_pairs={{0,16},{16,0},{1,17},{17,1},{2,18},{18,2},{3,19},{19,3},{4,20},{20... | collective-permute-start | bytes 98312 | tf_op jit(solution)/shard_map/ppermute | solution.py:279
  4.5 19.6 %collective-permute-start.1 = (f32[2,16,256]{2,1,0:T(8,128)S(1)}, f32[2,16,256]{2,1,0:T(8,128)S(1)}, u32[]{:S(2)}, u32[]{:S(2)}) collective-permute-start(f32[2,16,256]{2,1,0:T(8,128)S(1)} %pad_maximum_fusion.5), channel_id=1, source_target_pairs={{16,0},{0,16},{17,1},{1,17},{18,2},{2,18},{19,3},{3,19},{20,4},{4,... | collective-permute-start | bytes 98312 | tf_op jit(solution)/shard_map/ppermute | solution.py:280
  6.3 17.8 %collective-permute-start.2 = (f32[3,32,256]{2,1,0:T(8,128)S(1)}, f32[3,32,256]{2,1,0:T(8,128)S(1)}, u32[]{:S(2)}, u32[]{:S(2)}) collective-permute-start(f32[3,32,256]{2,1,0:T(8,128)S(1)} %pad_maximum_fusion), channel_id=1, source_target_pairs={{0,4},{4,8},{8,12},{1,5},{5,9},{9,13},{2,6},{6,10},{10,14},{3,7},{... | collective-permute-start | bytes 294920 | tf_op jit(solution)/shard_map/ppermute | solution.py:279
  8.2 15.9 %collective-permute-start.3 = (f32[3,32,256]{2,1,0:T(8,128)S(1)}, f32[3,32,256]{2,1,0:T(8,128)S(1)}, u32[]{:S(2)}, u32[]{:S(2)}) collective-permute-start(f32[3,32,256]{2,1,0:T(8,128)S(1)} %pad_maximum_fusion.1), channel_id=1, source_target_pairs={{4,0},{8,4},{12,8},{5,1},{9,5},{13,9},{6,2},{10,6},{14,10},{7,3},{... | collective-permute-start | bytes 294920 | tf_op jit(solution)/shard_map/ppermute | solution.py:280
  12.9 3.9 %collective-permute-start.5 = (f32[3,32,16]{1,2,0:T(8,128)S(1)}, f32[3,32,16]{1,2,0:T(8,128)S(1)}, u32[]{:S(2)}, u32[]{:S(2)}) collective-permute-start(f32[3,32,16]{1,2,0:T(8,128)S(1)} %pad_maximum_fusion.7), channel_id=1, source_target_pairs={{1,0},{2,1},{3,2},{5,4},{6,5},{7,6},{9,8},{10,9},{11,10},{13,12},{... | collective-permute-start | bytes 18440 | tf_op jit(solution)/shard_map/ppermute | solution.py:280
  16.7 6.0 %collective-permute-start.4 = (f32[3,32,16]{1,2,0:T(8,128)S(1)}, f32[3,32,16]{1,2,0:T(8,128)S(1)}, u32[]{:S(2)}, u32[]{:S(2)}) collective-permute-start(f32[3,32,16]{1,2,0:T(8,128)S(1)} %pad_maximum_fusion.6), channel_id=1, source_target_pairs={{0,1},{1,2},{2,3},{4,5},{5,6},{6,7},{8,9},{9,10},{10,11},{12,13},{... | collective-permute-start | bytes 18440 | tf_op jit(solution)/shard_map/ppermute | solution.py:279
  24.1 0.6 copy-start.5
  24.1 0.6 copy-start.6
  24.1 0.6 copy-start.1
  24.7 0.6 copy-start.2
  48.8 10.9 %collective-permute-start.9 = (f32[2,32,16]{1,2,0:T(8,128)S(1)}, f32[2,32,16]{1,2,0:T(8,128)S(1)}, u32[]{:S(2)}, u32[]{:S(2)}) collective-permute-start(f32[2,32,16]{1,2,0:T(8,128)S(1)} %pad_maximum_fusion.9), channel_id=1, source_target_pairs={{1,0},{2,1},{3,2},{5,4},{6,5},{7,6},{9,8},{10,9},{11,10},{13,12},{... | collective-permute-start | bytes 12296 | tf_op jit(solution)/shard_map/ppermute | solution.py:280
  52.7 12.3 %collective-permute-start.6 = (f32[2,32,256]{2,1,0:T(8,128)S(1)}, f32[2,32,256]{2,1,0:T(8,128)S(1)}, u32[]{:S(2)}, u32[]{:S(2)}) collective-permute-start(f32[2,32,256]{2,1,0:T(8,128)S(1)} %pad_maximum_fusion.2), channel_id=1, source_target_pairs={{0,4},{4,8},{8,12},{1,5},{5,9},{9,13},{2,6},{6,10},{10,14},{3,7},{... | collective-permute-start | bytes 196616 | tf_op jit(solution)/shard_map/ppermute | solution.py:279
  54.7 10.4 %collective-permute-start.7 = (f32[2,32,256]{2,1,0:T(8,128)S(1)}, f32[2,32,256]{2,1,0:T(8,128)S(1)}, u32[]{:S(2)}, u32[]{:S(2)}) collective-permute-start(f32[2,32,256]{2,1,0:T(8,128)S(1)} %pad_maximum_fusion.3), channel_id=1, source_target_pairs={{4,0},{8,4},{12,8},{5,1},{9,5},{13,9},{6,2},{10,6},{14,10},{7,3},{... | collective-permute-start | bytes 196616 | tf_op jit(solution)/shard_map/ppermute | solution.py:280
  58.3 5.6 %collective-permute-start.8 = (f32[2,32,16]{1,2,0:T(8,128)S(1)}, f32[2,32,16]{1,2,0:T(8,128)S(1)}, u32[]{:S(2)}, u32[]{:S(2)}) collective-permute-start(f32[2,32,16]{1,2,0:T(8,128)S(1)} %pad_maximum_fusion.8), channel_id=1, source_target_pairs={{0,1},{1,2},{2,3},{4,5},{5,6},{6,7},{8,9},{9,10},{10,11},{12,13},{... | collective-permute-start | bytes 12296 | tf_op jit(solution)/shard_map/ppermute | solution.py:279
  65.1 0.6 copy-start.3
  65.7 0.6 copy-start.4
  84.2 14.6 %collective-permute-start.11 = (f32[1,32,256]{2,1,0:T(8,128)S(1)}, f32[1,32,256]{2,1,0:T(8,128)S(1)}, u32[]{:S(2)}, u32[]{:S(2)}) collective-permute-start(f32[1,32,256]{2,1,0:T(8,128)S(1)} %get-tuple-element.20), channel_id=1, source_target_pairs={{4,0},{8,4},{12,8},{5,1},{9,5},{13,9},{6,2},{10,6},{14,10},{7,3},{... | collective-permute-start | bytes 98312 | tf_op jit(solution)/shard_map/ppermute | solution.py:280
  86.1 12.7 %collective-permute-start.10 = (f32[1,32,256]{2,1,0:T(8,128)S(1)}, f32[1,32,256]{2,1,0:T(8,128)S(1)}, u32[]{:S(2)}, u32[]{:S(2)}) collective-permute-start(f32[1,32,256]{2,1,0:T(8,128)S(1)} %get-tuple-element.21), channel_id=1, source_target_pairs={{0,4},{4,8},{8,12},{1,5},{5,9},{9,13},{2,6},{6,10},{10,14},{3,7},{... | collective-permute-start | bytes 98312 | tf_op jit(solution)/shard_map/ppermute | solution.py:279
  89.9 3.8 %collective-permute-start.13 = (f32[1,32,16]{1,2,0:T(8,128)S(1)}, f32[1,32,16]{1,2,0:T(8,128)S(1)}, u32[]{:S(2)}, u32[]{:S(2)}) collective-permute-start(f32[1,32,16]{1,2,0:T(8,128)S(1)} %bitcast.79), channel_id=1, source_target_pairs={{1,0},{2,1},{3,2},{5,4},{6,5},{7,6},{9,8},{10,9},{11,10},{13,12},{... | collective-permute-start | bytes 6152 | tf_op jit(solution)/shard_map/ppermute | solution.py:280
  92.4 5.5 %collective-permute-start.12 = (f32[1,32,16]{1,2,0:T(8,128)S(1)}, f32[1,32,16]{1,2,0:T(8,128)S(1)}, u32[]{:S(2)}, u32[]{:S(2)}) collective-permute-start(f32[1,32,16]{1,2,0:T(8,128)S(1)} %bitcast.81), channel_id=1, source_target_pairs={{0,1},{1,2},{2,3},{4,5},{5,6},{6,7},{8,9},{9,10},{10,11},{12,13},{... | collective-permute-start | bytes 6152 | tf_op jit(solution)/shard_map/ppermute | solution.py:279
  98.8 0.6 copy-start.7
  99.4 0.6 copy-start.8

commit v2 on v0

--- a/solution.py
+++ b/solution.py
@@ -60,11 +60,28 @@
     return total
 
 
+def _yrow(ref, c, i):
+    return ref[c, pl.ds(i, 1), :]
+
+
+def _zcol(ref, c, i):
+    return ref[c, :, pl.ds(i, 1)]
+
+
+def _write_edges(edges, c, r, val):
+    y_first, y_last, z_first, z_last = edges
+    ny, nz = val.shape
+    y_first[c, pl.ds(r, 1), :] = val[0:1, :]
+    y_last[c, pl.ds(r, 1), :] = val[ny - 1 : ny, :]
+    z_first[c, :, pl.ds(r, 1)] = val[:, 0:1]
+    z_last[c, :, pl.ds(r, 1)] = val[:, nz - 1 : nz]
+
+
 def _geo_row(i, pore_ref, lab_ref, gy_lo, gy_hi, gz_lo, gz_hi):
     mob = 1.0 + 2.0 * pore_ref[i].astype(F32)
     lab = lab_ref[i].astype(F32)
-    mob_n = _neighbours(mob, gy_lo[0, i], gy_hi[0, i], gz_lo[0, i], gz_hi[0, i])
-    lab_n = _neighbours(lab, gy_lo[1, i], gy_hi[1, i], gz_lo[1, i], gz_hi[1, i])
+    mob_n = _neighbours(mob, _yrow(gy_lo, 0, i), _yrow(gy_hi, 0, i), _zcol(gz_lo, 0, i), _zcol(gz_hi, 0, i))
+    lab_n = _neighbours(lab, _yrow(gy_lo, 1, i), _yrow(gy_hi, 1, i), _zcol(gz_lo, 1, i), _zcol(gz_hi, 1, i))
     return mob, lab, mob_n, _faces(mob, lab, mob_n, lab_n)
 
 
@@ -121,7 +138,7 @@
         mob, lab, mob_n, fc = _geo_row(i, pore_ref, lab_ref, gy_lo, gy_hi, gz_lo, gz_hi)
         v = vac_ref[i]
         u = w_ext[i + 1] * v
-        v_n = _neighbours(v, gy_lo[2, i], gy_hi[2, i], gz_lo[2, i], gz_hi[2, i])
+        v_n = _neighbours(v, _yrow(gy_lo, 2, i), _yrow(gy_hi, 2, i), _zcol(gz_lo, 2, i), _zcol(gz_hi, 2, i))
         u_n = [0.5 * (1.0 + mn) * vn for mn, vn in zip(mob_n, v_n)]
         src_f.append(v + cross_rate * (1.0 * _flux(u, u_n, fc)))
     src_a = [cot_ref[r] for r in range(m)]
@@ -203,13 +220,15 @@
     return [inner[r] - linked[r] * sep for r in range(k_in)] + [sep]
 
 
-def _combine_kernel(voff, stacked, pos_ref, gs_ref, gv_ref, fac_ref, loc_ref, *refs):
+def _combine_kernel(voff, stacked, edge_of, pos_ref, gs_ref, gv_ref, fac_ref, loc_ref, *refs):
     if stacked:
-        out_ref, sep_ref = refs
+        out_ref = refs[0]
         outs = (out_ref.at[0], out_ref.at[1])
+        rest = refs[1:]
     else:
-        out0, out1, sep_ref = refs
-        outs = (out0, out1)
+        outs = refs[:2]
+        rest = refs[2:]
+    edges, sep_ref = rest[:4], rest[4]
     n = gs_ref.shape[0]
     m = loc_ref.shape[1]
     p = pos_ref[0]
@@ -220,7 +239,26 @@
         own = sep_ref[p]
         prior = sep_ref[(p + n - 1) % n]
         for r in range(m):
-            outs[c][r] = loc_ref[c, r] - fac_ref[c, 3, r] * prior - fac_ref[c, 4, r] * own
+            val = loc_ref[c, r] - fac_ref[c, 3, r] * prior - fac_ref[c, 4, r] * own
+            outs[c][r] = val
+            if c in edge_of:
+                _write_edges(edges, edge_of[c], r, val)
+
+
+def _edge_kernel(vac_ref, pore_ref, lab_ref, y_first, y_last, z_first, z_last, bx_first, bx_last):
+    m = vac_ref.shape[0]
+    edges = (y_first, y_last, z_first, z_last)
+    for r in range(m):
+        mob = 1.0 + 2.0 * pore_ref[r].astype(F32)
+        lab = lab_ref[r].astype(F32)
+        for c, val in enumerate((mob, lab, vac_ref[r])):
+            _write_edges(edges, c, r, val)
+        if r == 0:
+            bx_first[0] = mob
+            bx_first[1] = lab
+        if r == m - 1:
+            bx_last[0] = mob
+            bx_last[1] = lab
 
 
 def _second_kernel(pore_ref, lab_ref, fa_ref, fac_ref, gy_lo, gy_hi, gz_lo, gz_hi,
@@ -231,11 +269,11 @@
         mob, lab, mob_n, fc = _geo_row(i, pore_ref, lab_ref, gy_lo, gy_hi, gz_lo, gz_hi)
         w = 0.5 * (1.0 + mob)
         f1 = fa_ref[0, i]
-        f_n = _neighbours(f1, hy_lo[0, i], hy_hi[0, i], hz_lo[0, i], hz_hi[0, i])
+        f_n = _neighbours(f1, _yrow(hy_lo, 0, i), _yrow(hy_hi, 0, i), _zcol(hz_lo, 0, i), _zcol(hz_hi, 0, i))
         u_n = [0.5 * (1.0 + mn) * fn for mn, fn in zip(mob_n, f_n)]
         srcs[0].append(f1 + cross_rate * (1.0 * _flux(w * f1, u_n, fc)))
         a1 = fa_ref[1, i]
-        a_n = _neighbours(a1, hy_lo[1, i], hy_hi[1, i], hz_lo[1, i], hz_hi[1, i])
+        a_n = _neighbours(a1, _yrow(hy_lo, 1, i), _yrow(hy_hi, 1, i), _zcol(hz_lo, 1, i), _zcol(hz_hi, 1, i))
         srcs[1].append(a1 + cross_rate * (w * _flux(a1, a_n, fc)))
     zero = jnp.zeros(pore_ref.shape[1:], F32)
     for c in range(2):
@@ -257,7 +295,7 @@
         mob, lab, mob_n, fc = _geo_row(i, pore_ref, lab_ref, gy_lo, gy_hi, gz_lo, gz_hi)
         w = 0.5 * (1.0 + mob)
         a2 = a2_ref[i]
-        a_n = _neighbours(a2, hy_lo[0, i], hy_hi[0, i], hz_lo[0, i], hz_hi[0, i])
+        a_n = _neighbours(a2, _yrow(hy_lo, 0, i), _yrow(hy_hi, 0, i), _zcol(hz_lo, 0, i), _zcol(hz_hi, 0, i))
         out_ref[i] = a2 + cross_rate * (w * _flux(a2, a_n, fc))
 
 
@@ -277,11 +315,18 @@
     return lo, hi
 
 
-def _yz_halos(stack):
-    y = stack.shape[2]
-    z = stack.shape[3]
-    gy_lo, gy_hi = _exchange(stack[:, :, 0:1, :], stack[:, :, y - 1 : y, :], "gy", False)
-    gz_lo, gz_hi = _exchange(stack[:, :, :, 0:1], stack[:, :, :, z - 1 : z], "gz", False)
+def _edge_shapes(chans, m, ny, nz):
+    return (
+        jax.ShapeDtypeStruct((chans, m, nz), F32),
+        jax.ShapeDtypeStruct((chans, m, nz), F32),
+        jax.ShapeDtypeStruct((chans, ny, m), F32),
+        jax.ShapeDtypeStruct((chans, ny, m), F32),
+    )
+
+
+def _yz_halos(y_first, y_last, z_first, z_last):
+    gy_lo, gy_hi = _exchange(y_first, y_last, "gy", False)
+    gz_lo, gz_hi = _exchange(z_first, z_last, "gz", False)
     return gy_lo, gy_hi, gz_lo, gz_hi
 
 
@@ -291,12 +336,14 @@
     cycle_step = float((m * n_blk) ** 2 // 64)
     shape = jax.ShapeDtypeStruct((m, ny, nz), F32)
 
-    mobility = 1.0 + 2.0 * pore_mask.astype(F32)
-    labels = grain_label.astype(F32)
-    geo0 = jnp.stack([mobility[0], labels[0]])
-    geo1 = jnp.stack([mobility[m - 1], labels[m - 1]])
-    bx_lo, bx_hi = _exchange(geo0, geo1, "blk", True)
-    gy_lo, gy_hi, gz_lo, gz_hi = _yz_halos(jnp.stack([mobility, labels, vacancy]))
+    outs = pl.pallas_call(
+        _edge_kernel,
+        out_shape=_edge_shapes(3, m, ny, nz) + (jax.ShapeDtypeStruct((2, ny, nz), F32),) * 2,
+        in_specs=[_vmem()] * 3,
+        out_specs=tuple(_vmem() for _ in range(6)),
+    )(vacancy, pore_mask, grain_label)
+    bx_lo, bx_hi = _exchange(outs[4], outs[5], "blk", True)
+    gy_lo, gy_hi, gz_lo, gz_hi = _yz_halos(*outs[:4])
 
     fac, loc, rows = pl.pallas_call(
         lambda *r: _prep_kernel(cycle_step, *r),
@@ -312,15 +359,16 @@
     gathered = lax.all_gather(rows, "blk", axis=0, tiled=False)
     pos = jnp.reshape(lax.axis_index("blk"), (1,)).astype(jnp.int32)
 
-    fa = pl.pallas_call(
-        lambda *r: _combine_kernel(5, True, *r),
-        out_shape=jax.ShapeDtypeStruct((2, m, ny, nz), F32),
+    outs = pl.pallas_call(
+        lambda *r: _combine_kernel(5, True, {0: 0, 1: 1}, *r),
+        out_shape=(jax.ShapeDtypeStruct((2, m, ny, nz), F32),) + _edge_shapes(2, m, ny, nz),
         in_specs=[_smem()] + [_vmem()] * 4,
-        out_specs=_vmem(),
+        out_specs=tuple(_vmem() for _ in range(5)),
         scratch_shapes=[pltpu.VMEM((n_blk, ny, nz), F32)],
     )(pos, gathered, gathered, fac, loc)
-
-    hy_lo, hy_hi, hz_lo, hz_hi = _yz_halos(fa)
+    fa = outs[0]
+
+    hy_lo, hy_hi, hz_lo, hz_hi = _yz_halos(*outs[1:])
     loc2, vals2 = pl.pallas_call(
         _second_kernel,
         out_shape=(
@@ -332,15 +380,16 @@
     )(pore_mask, grain_label, fa, fac, gy_lo, gy_hi, gz_lo, gz_hi, hy_lo, hy_hi, hz_lo, hz_hi)
 
     gathered2 = lax.all_gather(vals2, "blk", axis=0, tiled=False)
-    final_field, adjoint_two = pl.pallas_call(
-        lambda *r: _combine_kernel(0, False, *r),
-        out_shape=(shape, shape),
+    outs = pl.pallas_call(
+        lambda *r: _combine_kernel(0, False, {1: 0}, *r),
+        out_shape=(shape, shape) + _edge_shapes(1, m, ny, nz),
         in_specs=[_smem()] + [_vmem()] * 4,
-        out_specs=(_vmem(), _vmem()),
+        out_specs=tuple(_vmem() for _ in range(6)),
         scratch_shapes=[pltpu.VMEM((n_blk, ny, nz), F32)],
     )(pos, gathered, gathered2, fac, loc2)
-
-    a2_lo, a2_hi, a2z_lo, a2z_hi = _yz_halos(adjoint_two[None])
+    final_field, adjoint_two = outs[:2]
+
+    a2_lo, a2_hi, a2z_lo, a2z_hi = _yz_halos(*outs[2:])
     gradient = pl.pallas_call(
         _gradient_kernel,
         out_shape=shape,

time: 114 us -> 96.2 us (0.84)
  the two profiles are of different devices: /device:TPU:0 before, /device:TPU:4 now
where the time goes in v2:
time: 96.2 us; the launch traced here: 95.5 us
  starting transfers between devices  33.5 us (35%)
  Pallas kernels  28.5 us (30%)
  waiting for transfers between devices  15.6 us (16%)
  blocking collectives  14.5 us (15%)
  local copies, waits for them, and re-layouts  2.54 us (3%)
    ppermute x7, starting transfers between devices, _exchange(): lo = lax.ppermute(last, axis, forward)  18.2 us
    ppermute x7, starting transfers between devices, _exchange(): hi = lax.ppermute(first, axis, backward)  15.3 us
    ppermute x7, waiting for transfers between devices, _exchange(): hi = lax.ppermute(first, axis, backward)  13.3 us
    all_gather x1, blocking collectives, shards(): gathered = lax.all_gather(rows, 'blk', axis=0, tiled=False)  9.3 us
    pallas_call x1, Pallas kernels, shards(): pl.pallas_call(lambda *r: _prep_kernel(cycle_step, *r), out_shape=(jax.Sh...  7.14 us
    pallas_call x1, Pallas kernels, shards(): pl.pallas_call(_second_kernel, out_shape=(jax.ShapeDtypeStruct((2, m, ny,...  6.59 us
    all_gather x1, blocking collectives, shards(): gathered2 = lax.all_gather(vals2, 'blk', axis=0, tiled=False)  5.24 us
    pallas_call x1, Pallas kernels, shards(): pl.pallas_call(lambda *r: _combine_kernel(5, True, {0: 0, 1: 1}, *r), out...  4.35 us
  transfers between devices with their start and end apart: 14, of which 6 were waited for; matrix products, arithmetic and copies ran while one was open for 0% of the time, Pallas kernels for 0%

profile of v2, /device:TPU:4, one launch (start us, length us, event | category | flops | bytes accessed | tf_op | source)
XLA Modules:
  0.0 95.5 jit_solution(3248094963124832847)
XLA Ops:
  0.6 2.4 %shard_map.59 = (f32[3,32,256]{2,1,0:T(8,128)}, f32[3,32,256]{2,1,0:T(8,128)}, f32[3,16,32]{2,1,0:T(8,128)}, f32[3,16,32]{2,1,0:T(8,128)}, f32[2,16,256]{2,1,0:T(8,128)}, /*index=5*/f32[2,16,256]{2,1,0:T(8,128)}) custom-call(f32[32,16,256]{2,1,0:T(8,128)} %r_0_.1, s32[32,16,256]{2,1,0:T(8,128)} %pore_ref.5, s32[32,16,256]{2,1,0:T(8,128)} %lab_ref.5), custom_call_target="tpu_custom_call" | custom-call | tf_op jit(solution)/shard_map/pallas_call | solution.py:339
  3.1 1.9 %collective-permute-start.2 = (f32[3,32,256]{2,1,0:T(8,128)}, f32[3,32,256]{2,1,0:T(8,128)S(1)}, u32[]{:S(2)}, u32[]{:S(2)}) collective-permute-start(f32[3,32,256]{2,1,0:T(8,128)} %get-tuple-element.26), channel_id=1, source_target_pairs={{0,4},{4,8},{8,12},{1,5},{5,9},{9,13},{2,6},{6,10},{10,14},{3,7},{... | collective-permute-start | bytes 294920 | tf_op jit(solution)/shard_map/ppermute | solution.py:313
  5.0 3.6 %collective-permute-start.3 = (f32[3,32,256]{2,1,0:T(8,128)}, f32[3,32,256]{2,1,0:T(8,128)S(1)}, u32[]{:S(2)}, u32[]{:S(2)}) collective-permute-start(f32[3,32,256]{2,1,0:T(8,128)} %get-tuple-element.27), channel_id=1, source_target_pairs={{4,0},{8,4},{12,8},{5,1},{9,5},{13,9},{6,2},{10,6},{14,10},{7,3},{... | collective-permute-start | bytes 294920 | tf_op jit(solution)/shard_map/ppermute | solution.py:314
  8.6 1.6 %collective-permute-start = (f32[2,16,256]{2,1,0:T(8,128)}, f32[2,16,256]{2,1,0:T(8,128)S(1)}, u32[]{:S(2)}, u32[]{:S(2)}) collective-permute-start(f32[2,16,256]{2,1,0:T(8,128)} %get-tuple-element.24), channel_id=1, source_target_pairs={{0,16},{16,0},{1,17},{17,1},{2,18},{18,2},{3,19},{19,3},{4,20},{20... | collective-permute-start | bytes 98312 | tf_op jit(solution)/shard_map/ppermute | solution.py:313
  10.2 0.5 collective-permute-start.1
  10.7 3.5 %collective-permute-start.4 = (f32[3,16,32]{2,1,0:T(8,128)}, f32[3,16,32]{2,1,0:T(8,128)S(1)}, u32[]{:S(2)}, u32[]{:S(2)}) collective-permute-start(f32[3,16,32]{2,1,0:T(8,128)} %get-tuple-element.28), channel_id=1, source_target_pairs={{0,1},{1,2},{2,3},{4,5},{5,6},{6,7},{8,9},{9,10},{10,11},{12,13},{... | collective-permute-start | bytes 18440 | tf_op jit(solution)/shard_map/ppermute | solution.py:313
  14.2 1.7 %collective-permute-done.4.r_8_.gz_lo = f32[3,16,32]{2,1,0:T(8,128)S(1)} collective-permute-done((f32[3,16,32]{2,1,0:T(8,128)}, f32[3,16,32]{2,1,0:T(8,128)S(1)}, u32[]{:S(2)}, u32[]{:S(2)}) %collective-permute-start.4) | collective-permute-done | bytes 6176 | tf_op jit(solution)/shard_map/ppermute | solution.py:313
  15.9 1.3 %collective-permute-start.5 = (f32[3,16,32]{2,1,0:T(8,128)}, f32[3,16,32]{2,1,0:T(8,128)S(1)}, u32[]{:S(2)}, u32[]{:S(2)}) collective-permute-start(f32[3,16,32]{2,1,0:T(8,128)} %get-tuple-element.29), channel_id=1, source_target_pairs={{1,0},{2,1},{3,2},{5,4},{6,5},{7,6},{9,8},{10,9},{11,10},{13,12},{... | collective-permute-start | bytes 18440 | tf_op jit(solution)/shard_map/ppermute | solution.py:314
  17.2 4.9 %collective-permute-done.5.r_9_.gz_hi = f32[3,16,32]{2,1,0:T(8,128)S(1)} collective-permute-done((f32[3,16,32]{2,1,0:T(8,128)}, f32[3,16,32]{2,1,0:T(8,128)S(1)}, u32[]{:S(2)}, u32[]{:S(2)}) %collective-permute-start.5) | collective-permute-done | bytes 6176 | tf_op jit(solution)/shard_map/ppermute | solution.py:314
  22.1 0.0 collective-permute-done.r_4_
  22.1 0.0 collective-permute-done.1.r_5_
  22.2 0.0 collective-permute-done.2.r_6_.gy_lo
  22.2 0.0 collective-permute-done.3.r_7_.gy_hi
  22.2 0.6 copy-done.3
  22.8 0.0 copy-done.6
  22.8 0.0 copy-done.7
  22.8 0.1 copy-done
  22.8 0.6 copy-done.1
  23.5 7.1 %shard_map.60 = (f32[2,5,32,16,256]{4,3,2,1,0:T(8,128)}, f32[2,32,16,256]{3,2,1,0:T(8,128)}, f32[2,7,16,256]{3,2,1,0:T(8,128)}) custom-call(f32[32,16,256]{2,1,0:T(8,128)} %r_0_.1, s32[32,16,256]{2,1,0:T(8,128)} %pore_ref.5, s32[32,16,256]{2,1,0:T(8,128)} %lab_ref.5, f32[32,16,256]{2,1,0:T(8,128)} %r_3_.1, f32[2,16,256]{2,1,0:T(8,128)} %copy-done.6, ...), custom_call_target="tpu_custom_call" | custom-call | tf_op jit(solution)/shard_map/pallas_call | solution.py:348
  30.6 9.3 %all-gather = f32[4,7,16,256]{3,2,1,0:T(8,128)} all-gather(f32[2,7,16,256]{3,2,1,0:T(8,128)} %get-tuple-element.30), channel_id=2, replica_groups=mesh['blk'=2,'gy'=4,'gz'=4] {'blk'}, dimensions={0}, use_global_device_ids=true | all-gather | bytes 688128 | tf_op jit(solution)/shard_map/all_gather | solution.py:359
  39.9 4.3 %shard_map.61 = (f32[2,32,16,256]{3,2,1,0:T(8,128)}, f32[2,32,256]{2,1,0:T(8,128)}, f32[2,32,256]{2,1,0:T(8,128)}, f32[2,16,32]{2,1,0:T(8,128)}, f32[2,16,32]{2,1,0:T(8,128)}) custom-call(s32[1]{0:T(128)} %bitcast.r_0_, f32[2,2,7,16,256]{4,3,2,1,0:T(8,128)} %bitcast.3, f32[2,2,7,16,256]{4,3,2,1,0:T(8,128)} %bitcast.4, ...), custom_call_target="tpu_custom_call" | custom-call | tf_op jit(solution)/shard_map/pallas_call | solution.py:362
  44.3 1.9 %collective-permute-start.6 = (f32[2,32,256]{2,1,0:T(8,128)}, f32[2,32,256]{2,1,0:T(8,128)S(1)}, u32[]{:S(2)}, u32[]{:S(2)}) collective-permute-start(f32[2,32,256]{2,1,0:T(8,128)} %get-tuple-element.34), channel_id=1, source_target_pairs={{0,4},{4,8},{8,12},{1,5},{5,9},{9,13},{2,6},{6,10},{10,14},{3,7},{... | collective-permute-start | bytes 196616 | tf_op jit(solution)/shard_map/ppermute | solution.py:313
  46.2 3.6 %collective-permute-start.7 = (f32[2,32,256]{2,1,0:T(8,128)}, f32[2,32,256]{2,1,0:T(8,128)S(1)}, u32[]{:S(2)}, u32[]{:S(2)}) collective-permute-start(f32[2,32,256]{2,1,0:T(8,128)} %get-tuple-element.35), channel_id=1, source_target_pairs={{4,0},{8,4},{12,8},{5,1},{9,5},{13,9},{6,2},{10,6},{14,10},{7,3},{... | collective-permute-start | bytes 196616 | tf_op jit(solution)/shard_map/ppermute | solution.py:314
  49.8 3.9 %collective-permute-start.8 = (f32[2,16,32]{2,1,0:T(8,128)}, f32[2,16,32]{2,1,0:T(8,128)S(1)}, u32[]{:S(2)}, u32[]{:S(2)}) collective-permute-start(f32[2,16,32]{2,1,0:T(8,128)} %get-tuple-element.36), channel_id=1, source_target_pairs={{0,1},{1,2},{2,3},{4,5},{5,6},{6,7},{8,9},{9,10},{10,11},{12,13},{... | collective-permute-start | bytes 12296 | tf_op jit(solution)/shard_map/ppermute | solution.py:313
  53.8 1.3 %collective-permute-start.9 = (f32[2,16,32]{2,1,0:T(8,128)}, f32[2,16,32]{2,1,0:T(8,128)S(1)}, u32[]{:S(2)}, u32[]{:S(2)}) collective-permute-start(f32[2,16,32]{2,1,0:T(8,128)} %get-tuple-element.37), channel_id=1, source_target_pairs={{1,0},{2,1},{3,2},{5,4},{6,5},{7,6},{9,8},{10,9},{11,10},{13,12},{... | collective-permute-start | bytes 12296 | tf_op jit(solution)/shard_map/ppermute | solution.py:314
  55.1 0.3 collective-permute-done.8.hz_lo
  55.4 4.2 %collective-permute-done.9.hz_hi = f32[2,16,32]{2,1,0:T(8,128)S(1)} collective-permute-done((f32[2,16,32]{2,1,0:T(8,128)}, f32[2,16,32]{2,1,0:T(8,128)S(1)}, u32[]{:S(2)}, u32[]{:S(2)}) %collective-permute-start.9) | collective-permute-done | bytes 4128 | tf_op jit(solution)/shard_map/ppermute | solution.py:314
  59.6 0.0 collective-permute-done.6.hy_lo
  59.6 0.0 collective-permute-done.7.hy_hi
  59.6 0.0 copy-start.5
  59.6 0.6 copy-done.11
  60.2 0.0 copy-done.4
  60.2 0.0 copy-done.5
  60.3 6.6 %shard_map.62 = (f32[2,32,16,256]{3,2,1,0:T(8,128)}, f32[2,2,16,256]{3,2,1,0:T(8,128)}) custom-call(s32[32,16,256]{2,1,0:T(8,128)} %pore_ref.5, s32[32,16,256]{2,1,0:T(8,128)} %lab_ref.5, f32[2,32,16,256]{3,2,1,0:T(8,128)} %get-tuple-element.33.fa_ref, f32[2,5,32,16,256]{4,3,2,1,0:T(8,128)} %get-tuple-element.31.r_3_.fac_ref, f32[3,32,256]{2,1,0:T(8,128)} %copy-done, ...), custom_call_target="tpu_custom_call" | custom-call | tf_op jit(solution)/shard_map/pallas_call | solution.py:372
  66.9 5.2 %all-gather.1 = f32[4,2,16,256]{3,2,1,0:T(8,128)} all-gather(f32[2,2,16,256]{3,2,1,0:T(8,128)} %get-tuple-element.38), channel_id=3, replica_groups=mesh['blk'=2,'gy'=4,'gz'=4] {'blk'}, dimensions={0}, use_global_device_ids=true | all-gather | bytes 196608 | tf_op jit(solution)/shard_map/all_gather | solution.py:382
  72.1 4.1 %shard_map.63 = (f32[32,16,256]{2,1,0:T(8,128)}, f32[32,16,256]{2,1,0:T(8,128)}, f32[1,32,256]{2,1,0:T(8,128)}, f32[1,32,256]{2,1,0:T(8,128)}, f32[1,16,32]{2,1,0:T(8,128)}, /*index=5*/f32[1,16,32]{2,1,0:T(8,128)}) custom-call(s32[1]{0:T(128)} %bitcast.r_0_, f32[2,2,7,16,256]{4,3,2,1,0:T(8,128)} %bitcast.5, f32[2,2,2,16,256]{4,3,2,1,0:T(8,128)} %bitcast.6, ...), custom_call_target="tpu_custom_call" | custom-call | tf_op jit(solution)/shard_map/pallas_call | solution.py:383
  76.2 1.9 %collective-permute-start.10 = (f32[1,32,256]{2,1,0:T(8,128)}, f32[1,32,256]{2,1,0:T(8,128)S(1)}, u32[]{:S(2)}, u32[]{:S(2)}) collective-permute-start(f32[1,32,256]{2,1,0:T(8,128)} %get-tuple-element.42), channel_id=1, source_target_pairs={{0,4},{4,8},{8,12},{1,5},{5,9},{9,13},{2,6},{6,10},{10,14},{3,7},{... | collective-permute-start | bytes 98312 | tf_op jit(solution)/shard_map/ppermute | solution.py:313
  78.1 3.6 %collective-permute-start.11 = (f32[1,32,256]{2,1,0:T(8,128)}, f32[1,32,256]{2,1,0:T(8,128)S(1)}, u32[]{:S(2)}, u32[]{:S(2)}) collective-permute-start(f32[1,32,256]{2,1,0:T(8,128)} %get-tuple-element.43), channel_id=1, source_target_pairs={{4,0},{8,4},{12,8},{5,1},{9,5},{13,9},{6,2},{10,6},{14,10},{7,3},{... | collective-permute-start | bytes 98312 | tf_op jit(solution)/shard_map/ppermute | solution.py:314
  81.8 3.5 %collective-permute-start.12 = (f32[1,16,32]{2,1,0:T(8,128)}, f32[1,16,32]{2,1,0:T(8,128)S(1)}, u32[]{:S(2)}, u32[]{:S(2)}) collective-permute-start(f32[1,16,32]{2,1,0:T(8,128)} %get-tuple-element.44), channel_id=1, source_target_pairs={{0,1},{1,2},{2,3},{4,5},{5,6},{6,7},{8,9},{9,10},{10,11},{12,13},{... | collective-permute-start | bytes 6152 | tf_op jit(solution)/shard_map/ppermute | solution.py:313
  85.3 1.3 %collective-permute-start.13 = (f32[1,16,32]{2,1,0:T(8,128)}, f32[1,16,32]{2,1,0:T(8,128)S(1)}, u32[]{:S(2)}, u32[]{:S(2)}) collective-permute-start(f32[1,16,32]{2,1,0:T(8,128)} %get-tuple-element.45), channel_id=1, source_target_pairs={{1,0},{2,1},{3,2},{5,4},{6,5},{7,6},{9,8},{10,9},{11,10},{13,12},{... | collective-permute-start | bytes 6152 | tf_op jit(solution)/shard_map/ppermute | solution.py:314
  86.6 0.3 collective-permute-done.12.hz_lo
  86.8 4.2 %collective-permute-done.13.hz_hi = f32[1,16,32]{2,1,0:T(8,128)S(1)} collective-permute-done((f32[1,16,32]{2,1,0:T(8,128)}, f32[1,16,32]{2,1,0:T(8,128)S(1)}, u32[]{:S(2)}, u32[]{:S(2)}) %collective-permute-start.13) | collective-permute-done | bytes 2080 | tf_op jit(solution)/shard_map/ppermute | solution.py:314
  91.0 0.0 collective-permute-done.10.hy_lo
  91.0 0.0 collective-permute-done.11.hy_hi
  91.1 0.6 copy-done.13
  91.6 0.0 copy-done.8
  91.7 0.0 copy-done.9
  91.7 3.8 %shard_map.64 = f32[32,16,256]{2,1,0:T(8,128)} custom-call(s32[32,16,256]{2,1,0:T(8,128)} %pore_ref.5, s32[32,16,256]{2,1,0:T(8,128)} %lab_ref.5, f32[32,16,256]{2,1,0:T(8,128)} %get-tuple-element.41.a2_ref, f32[3,32,256]{2,1,0:T(8,128)} %copy-done, f32[3,32,256]{2,1,0:T(8,128)} %copy-done.1, f32[3,16,32]{2,1,0:T(8,128)} %copy-done.2, ...), custom_call_target="tpu_custom_call" | custom-call | tf_op jit(solution)/shard_map/pallas_call | solution.py:393
  (16 shorter events, 0.0 us)
Async XLA Ops:
  3.1 19.1 %collective-permute-start.2 = (f32[3,32,256]{2,1,0:T(8,128)}, f32[3,32,256]{2,1,0:T(8,128)S(1)}, u32[]{:S(2)}, u32[]{:S(2)}) collective-permute-start(f32[3,32,256]{2,1,0:T(8,128)} %get-tuple-element.26), channel_id=1, source_target_pairs={{0,4},{4,8},{8,12},{1,5},{5,9},{9,13},{2,6},{6,10},{10,14},{3,7},{... | collective-permute-start | bytes 294920 | tf_op jit(solution)/shard_map/ppermute | solution.py:313
  5.0 17.2 %collective-permute-start.3 = (f32[3,32,256]{2,1,0:T(8,128)}, f32[3,32,256]{2,1,0:T(8,128)S(1)}, u32[]{:S(2)}, u32[]{:S(2)}) collective-permute-start(f32[3,32,256]{2,1,0:T(8,128)} %get-tuple-element.27), channel_id=1, source_target_pairs={{4,0},{8,4},{12,8},{5,1},{9,5},{13,9},{6,2},{10,6},{14,10},{7,3},{... | collective-permute-start | bytes 294920 | tf_op jit(solution)/shard_map/ppermute | solution.py:314
  8.6 13.5 %collective-permute-start = (f32[2,16,256]{2,1,0:T(8,128)}, f32[2,16,256]{2,1,0:T(8,128)S(1)}, u32[]{:S(2)}, u32[]{:S(2)}) collective-permute-start(f32[2,16,256]{2,1,0:T(8,128)} %get-tuple-element.24), channel_id=1, source_target_pairs={{0,16},{16,0},{1,17},{17,1},{2,18},{18,2},{3,19},{19,3},{4,20},{20... | collective-permute-start | bytes 98312 | tf_op jit(solution)/shard_map/ppermute | solution.py:313
  10.2 11.9 %collective-permute-start.1 = (f32[2,16,256]{2,1,0:T(8,128)}, f32[2,16,256]{2,1,0:T(8,128)S(1)}, u32[]{:S(2)}, u32[]{:S(2)}) collective-permute-start(f32[2,16,256]{2,1,0:T(8,128)} %get-tuple-element.25), channel_id=1, source_target_pairs={{16,0},{0,16},{17,1},{1,17},{18,2},{2,18},{19,3},{3,19},{20,4},{4,... | collective-permute-start | bytes 98312 | tf_op jit(solution)/shard_map/ppermute | solution.py:314
  10.7 5.2 %collective-permute-start.4 = (f32[3,16,32]{2,1,0:T(8,128)}, f32[3,16,32]{2,1,0:T(8,128)S(1)}, u32[]{:S(2)}, u32[]{:S(2)}) collective-permute-start(f32[3,16,32]{2,1,0:T(8,128)} %get-tuple-element.28), channel_id=1, source_target_pairs={{0,1},{1,2},{2,3},{4,5},{5,6},{6,7},{8,9},{9,10},{10,11},{12,13},{... | collective-permute-start | bytes 18440 | tf_op jit(solution)/shard_map/ppermute | solution.py:313
  15.9 6.3 %copy-start.2 = (f32[3,16,32]{2,1,0:T(8,128)}, f32[3,16,32]{2,1,0:T(8,128)S(1)}, u32[]{:S(2)}) copy-start(f32[3,16,32]{2,1,0:T(8,128)S(1)} %collective-permute-done.4.r_8_.gz_lo) | copy-start | bytes 18436
  15.9 6.2 %collective-permute-start.5 = (f32[3,16,32]{2,1,0:T(8,128)}, f32[3,16,32]{2,1,0:T(8,128)S(1)}, u32[]{:S(2)}, u32[]{:S(2)}) collective-permute-start(f32[3,16,32]{2,1,0:T(8,128)} %get-tuple-element.29), channel_id=1, source_target_pairs={{1,0},{2,1},{3,2},{5,4},{6,5},{7,6},{9,8},{10,9},{11,10},{13,12},{... | collective-permute-start | bytes 18440 | tf_op jit(solution)/shard_map/ppermute | solution.py:314
  22.1 0.6 copy-start.3
  22.1 0.6 copy-start.6
  22.2 0.6 copy-start.7
  22.2 0.7 copy-start
  22.8 0.6 copy-start.1
  44.3 15.3 %collective-permute-start.6 = (f32[2,32,256]{2,1,0:T(8,128)}, f32[2,32,256]{2,1,0:T(8,128)S(1)}, u32[]{:S(2)}, u32[]{:S(2)}) collective-permute-start(f32[2,32,256]{2,1,0:T(8,128)} %get-tuple-element.34), channel_id=1, source_target_pairs={{0,4},{4,8},{8,12},{1,5},{5,9},{9,13},{2,6},{6,10},{10,14},{3,7},{... | collective-permute-start | bytes 196616 | tf_op jit(solution)/shard_map/ppermute | solution.py:313
  46.2 13.4 %collective-permute-start.7 = (f32[2,32,256]{2,1,0:T(8,128)}, f32[2,32,256]{2,1,0:T(8,128)S(1)}, u32[]{:S(2)}, u32[]{:S(2)}) collective-permute-start(f32[2,32,256]{2,1,0:T(8,128)} %get-tuple-element.35), channel_id=1, source_target_pairs={{4,0},{8,4},{12,8},{5,1},{9,5},{13,9},{6,2},{10,6},{14,10},{7,3},{... | collective-permute-start | bytes 196616 | tf_op jit(solution)/shard_map/ppermute | solution.py:314
  49.8 5.6 %collective-permute-start.8 = (f32[2,16,32]{2,1,0:T(8,128)}, f32[2,16,32]{2,1,0:T(8,128)S(1)}, u32[]{:S(2)}, u32[]{:S(2)}) collective-permute-start(f32[2,16,32]{2,1,0:T(8,128)} %get-tuple-element.36), channel_id=1, source_target_pairs={{0,1},{1,2},{2,3},{4,5},{5,6},{6,7},{8,9},{9,10},{10,11},{12,13},{... | collective-permute-start | bytes 12296 | tf_op jit(solution)/shard_map/ppermute | solution.py:313
  53.8 5.8 %collective-permute-start.9 = (f32[2,16,32]{2,1,0:T(8,128)}, f32[2,16,32]{2,1,0:T(8,128)S(1)}, u32[]{:S(2)}, u32[]{:S(2)}) collective-permute-start(f32[2,16,32]{2,1,0:T(8,128)} %get-tuple-element.37), channel_id=1, source_target_pairs={{1,0},{2,1},{3,2},{5,4},{6,5},{7,6},{9,8},{10,9},{11,10},{13,12},{... | collective-permute-start | bytes 12296 | tf_op jit(solution)/shard_map/ppermute | solution.py:314
  55.4 4.2 %copy-start.10 = (f32[2,16,32]{2,1,0:T(8,128)}, f32[2,16,32]{2,1,0:T(8,128)S(1)}, u32[]{:S(2)}) copy-start(f32[2,16,32]{2,1,0:T(8,128)S(1)} %collective-permute-done.8.hz_lo) | copy-start | bytes 12292
  59.6 0.6 copy-start.11
  59.6 0.6 copy-start.4
  59.6 0.6 copy-start.5
  76.2 14.8 %collective-permute-start.10 = (f32[1,32,256]{2,1,0:T(8,128)}, f32[1,32,256]{2,1,0:T(8,128)S(1)}, u32[]{:S(2)}, u32[]{:S(2)}) collective-permute-start(f32[1,32,256]{2,1,0:T(8,128)} %get-tuple-element.42), channel_id=1, source_target_pairs={{0,4},{4,8},{8,12},{1,5},{5,9},{9,13},{2,6},{6,10},{10,14},{3,7},{... | collective-permute-start | bytes 98312 | tf_op jit(solution)/shard_map/ppermute | solution.py:313
  78.1 12.9 %collective-permute-start.11 = (f32[1,32,256]{2,1,0:T(8,128)}, f32[1,32,256]{2,1,0:T(8,128)S(1)}, u32[]{:S(2)}, u32[]{:S(2)}) collective-permute-start(f32[1,32,256]{2,1,0:T(8,128)} %get-tuple-element.43), channel_id=1, source_target_pairs={{4,0},{8,4},{12,8},{5,1},{9,5},{13,9},{6,2},{10,6},{14,10},{7,3},{... | collective-permute-start | bytes 98312 | tf_op jit(solution)/shard_map/ppermute | solution.py:314
  81.8 5.1 %collective-permute-start.12 = (f32[1,16,32]{2,1,0:T(8,128)}, f32[1,16,32]{2,1,0:T(8,128)S(1)}, u32[]{:S(2)}, u32[]{:S(2)}) collective-permute-start(f32[1,16,32]{2,1,0:T(8,128)} %get-tuple-element.44), channel_id=1, source_target_pairs={{0,1},{1,2},{2,3},{4,5},{5,6},{6,7},{8,9},{9,10},{10,11},{12,13},{... | collective-permute-start | bytes 6152 | tf_op jit(solution)/shard_map/ppermute | solution.py:313
  85.3 5.8 %collective-permute-start.13 = (f32[1,16,32]{2,1,0:T(8,128)}, f32[1,16,32]{2,1,0:T(8,128)S(1)}, u32[]{:S(2)}, u32[]{:S(2)}) collective-permute-start(f32[1,16,32]{2,1,0:T(8,128)} %get-tuple-element.45), channel_id=1, source_target_pairs={{1,0},{2,1},{3,2},{5,4},{6,5},{7,6},{9,8},{10,9},{11,10},{13,12},{... | collective-permute-start | bytes 6152 | tf_op jit(solution)/shard_map/ppermute | solution.py:314
  86.8 4.2 %copy-start.12 = (f32[1,16,32]{2,1,0:T(8,128)}, f32[1,16,32]{2,1,0:T(8,128)S(1)}, u32[]{:S(2)}) copy-start(f32[1,16,32]{2,1,0:T(8,128)S(1)} %collective-permute-done.12.hz_lo) | copy-start | bytes 6148
  91.0 0.6 copy-start.13
  91.0 0.6 copy-start.8
  91.1 0.6 copy-start.9

commit v3 on v2

--- a/solution.py
+++ b/solution.py
@@ -4,6 +4,7 @@
 from jax.experimental import pallas as pl
 from jax.experimental.pallas import tpu as pltpu
 from jax.sharding import PartitionSpec as P
+
 
 cross_rate = 0.0125
 boundary_gain = 3.0
@@ -111,10 +112,9 @@
     return xs
 
 
-def _prep_kernel(cs, vac_ref, pore_ref, lab_ref, cot_ref, bx_lo, bx_hi, gy_lo, gy_hi, gz_lo, gz_hi,
-                 fac_ref, loc_ref, rows_ref):
-    m = vac_ref.shape[0]
-    zero = jnp.zeros(vac_ref.shape[1:], F32)
+def _factor_kernel(cs, pore_ref, lab_ref, bx_lo, bx_hi, fac_ref, lr_ref, rows_ref):
+    m = pore_ref.shape[0]
+    zero = jnp.zeros(pore_ref.shape[1:], F32)
     mobs = [1.0 + 2.0 * pore_ref[r].astype(F32) for r in range(m)]
     labs = [lab_ref[r].astype(F32) for r in range(m)]
     m_ext = [bx_lo[0]] + mobs + [bx_hi[0]]
@@ -133,17 +133,7 @@
         bands["a"][1].append(main)
         bands["a"][2].append(-cs * ff * w)
 
-    src_f = []
-    for i in range(m):
-        mob, lab, mob_n, fc = _geo_row(i, pore_ref, lab_ref, gy_lo, gy_hi, gz_lo, gz_hi)
-        v = vac_ref[i]
-        u = w_ext[i + 1] * v
-        v_n = _neighbours(v, _yrow(gy_lo, 2, i), _yrow(gy_hi, 2, i), _zcol(gz_lo, 2, i), _zcol(gz_hi, 2, i))
-        u_n = [0.5 * (1.0 + mn) * vn for mn, vn in zip(mob_n, v_n)]
-        src_f.append(v + cross_rate * (1.0 * _flux(u, u_n, fc)))
-    src_a = [cot_ref[r] for r in range(m)]
-
-    for c, key, src in ((0, "f", src_f), (1, "a", src_a)):
+    for c, key in ((0, "f"), (1, "a")):
         lower, main, upper = bands[key]
         pivots, ratios = [], []
         prev = None
@@ -157,30 +147,28 @@
         right_src = [None] * (m - 2) + [upper[m - 2], None]
         left = _sweep(m, lower, pivots, ratios, left_src)
         right = _sweep(m, lower, pivots, ratios, right_src)
-        local = _sweep(m, lower, pivots, ratios, src[: m - 1] + [None])
         for r in range(m):
             fac_ref[c, 0, r] = lower[r]
             fac_ref[c, 1, r] = ratios[r] if r < m - 1 else zero
             fac_ref[c, 2, r] = pivots[r] if r < m - 1 else zero + 1.0
-            fac_ref[c, 3, r] = left[r] if r < m - 1 else zero
-            fac_ref[c, 4, r] = right[r] if r < m - 1 else zero - 1.0
-            loc_ref[c, r] = local[r] if r < m - 1 else zero
+            lr_ref[c, 0, r] = left[r] if r < m - 1 else zero
+            lr_ref[c, 1, r] = right[r] if r < m - 1 else zero - 1.0
         last_lower = lower[m - 1]
         rows_ref[c, 0] = last_lower * left[m - 2]
         rows_ref[c, 1] = main[m - 1] - last_lower * right[m - 2]
         rows_ref[c, 2] = upper[m - 1]
         rows_ref[c, 3] = left[0]
         rows_ref[c, 4] = right[0]
-        rows_ref[c, 5] = src[m - 1] - last_lower * local[m - 2]
-        rows_ref[c, 6] = local[0]
-
-
-def _reduced_solve(gs, gv, voff, c, n):
-    g = [[gs[p, c, k] for k in range(5)] for p in range(n)]
+
+
+def _reduced_solve(gs, gv, voff, c, n, pos):
+    slot = [(pos - p + n) % n for p in range(n)]
+    g = [[gs[slot[p], c, k] for k in range(5)] for p in range(n)]
+    v = [[gv[slot[p], c, voff + k] for k in range(2)] for p in range(n)]
     lower = [-g[p][0] for p in range(n)]
     main = [g[p][1] - g[p][2] * g[(p + 1) % n][3] for p in range(n)]
     upper = [-g[p][2] * g[(p + 1) % n][4] for p in range(n)]
-    src = [gv[p, c, voff] - g[p][2] * gv[(p + 1) % n, c, voff + 1] for p in range(n)]
+    src = [v[p][0] - g[p][2] * v[(p + 1) % n][1] for p in range(n)]
     k_in = n - 1
     pivots, ratios = [], []
     prev = None
@@ -220,7 +208,7 @@
     return [inner[r] - linked[r] * sep for r in range(k_in)] + [sep]
 
 
-def _combine_kernel(voff, stacked, edge_of, pos_ref, gs_ref, gv_ref, fac_ref, loc_ref, *refs):
+def _combine_kernel(voff, stacked, edge_of, pos_ref, gs_ref, gv_ref, lr_ref, loc_ref, *refs):
     if stacked:
         out_ref = refs[0]
         outs = (out_ref.at[0], out_ref.at[1])
@@ -233,13 +221,13 @@
     m = loc_ref.shape[1]
     p = pos_ref[0]
     for c in range(2):
-        seps = _reduced_solve(gs_ref, gv_ref, voff, c, n)
+        seps = _reduced_solve(gs_ref, gv_ref, voff, c, n, p)
         for q in range(n):
             sep_ref[q] = seps[q]
         own = sep_ref[p]
         prior = sep_ref[(p + n - 1) % n]
         for r in range(m):
-            val = loc_ref[c, r] - fac_ref[c, 3, r] * prior - fac_ref[c, 4, r] * own
+            val = loc_ref[c, r] - lr_ref[c, 0, r] * prior - lr_ref[c, 1, r] * own
             outs[c][r] = val
             if c in edge_of:
                 _write_edges(edges, edge_of[c], r, val)
@@ -261,21 +249,9 @@
             bx_last[1] = lab
 
 
-def _second_kernel(pore_ref, lab_ref, fa_ref, fac_ref, gy_lo, gy_hi, gz_lo, gz_hi,
-                   hy_lo, hy_hi, hz_lo, hz_hi, loc_ref, vals_ref):
-    m = pore_ref.shape[0]
-    srcs = ([], [])
-    for i in range(m):
-        mob, lab, mob_n, fc = _geo_row(i, pore_ref, lab_ref, gy_lo, gy_hi, gz_lo, gz_hi)
-        w = 0.5 * (1.0 + mob)
-        f1 = fa_ref[0, i]
-        f_n = _neighbours(f1, _yrow(hy_lo, 0, i), _yrow(hy_hi, 0, i), _zcol(hz_lo, 0, i), _zcol(hz_hi, 0, i))
-        u_n = [0.5 * (1.0 + mn) * fn for mn, fn in zip(mob_n, f_n)]
-        srcs[0].append(f1 + cross_rate * (1.0 * _flux(w * f1, u_n, fc)))
-        a1 = fa_ref[1, i]
-        a_n = _neighbours(a1, _yrow(hy_lo, 1, i), _yrow(hy_hi, 1, i), _zcol(hz_lo, 1, i), _zcol(hz_hi, 1, i))
-        srcs[1].append(a1 + cross_rate * (w * _flux(a1, a_n, fc)))
-    zero = jnp.zeros(pore_ref.shape[1:], F32)
+def _local_solves(fac_ref, srcs, loc_ref, vals_ref):
+    m = loc_ref.shape[1]
+    zero = jnp.zeros(loc_ref.shape[2:], F32)
     for c in range(2):
         lower = [fac_ref[c, 0, r] for r in range(m)]
         ratios = [fac_ref[c, 1, r] for r in range(m - 1)]
@@ -288,11 +264,41 @@
         vals_ref[c, 1] = local[0]
 
 
+def _first_kernel(vac_ref, cot_ref, pore_ref, lab_ref, fac_ref, gy_lo, gy_hi, gz_lo, gz_hi, loc_ref, vals_ref):
+    m = pore_ref.shape[0]
+    srcs = ([], [cot_ref[r] for r in range(m)])
+    for i in range(m):
+        mob, _, mob_n, fc = _geo_row(i, pore_ref, lab_ref, gy_lo, gy_hi, gz_lo, gz_hi)
+        w = 0.5 * (1.0 + mob)
+        v = vac_ref[i]
+        v_n = _neighbours(v, _yrow(gy_lo, 2, i), _yrow(gy_hi, 2, i), _zcol(gz_lo, 2, i), _zcol(gz_hi, 2, i))
+        u_n = [0.5 * (1.0 + mn) * vn for mn, vn in zip(mob_n, v_n)]
+        srcs[0].append(v + cross_rate * (1.0 * _flux(w * v, u_n, fc)))
+    _local_solves(fac_ref, srcs, loc_ref, vals_ref)
+
+
+def _second_kernel(pore_ref, lab_ref, fa_ref, fac_ref, gy_lo, gy_hi, gz_lo, gz_hi,
+                   hy_lo, hy_hi, hz_lo, hz_hi, loc_ref, vals_ref):
+    m = pore_ref.shape[0]
+    srcs = ([], [])
+    for i in range(m):
+        mob, _, mob_n, fc = _geo_row(i, pore_ref, lab_ref, gy_lo, gy_hi, gz_lo, gz_hi)
+        w = 0.5 * (1.0 + mob)
+        f1 = fa_ref[0, i]
+        f_n = _neighbours(f1, _yrow(hy_lo, 0, i), _yrow(hy_hi, 0, i), _zcol(hz_lo, 0, i), _zcol(hz_hi, 0, i))
+        u_n = [0.5 * (1.0 + mn) * fn for mn, fn in zip(mob_n, f_n)]
+        srcs[0].append(f1 + cross_rate * (1.0 * _flux(w * f1, u_n, fc)))
+        a1 = fa_ref[1, i]
+        a_n = _neighbours(a1, _yrow(hy_lo, 1, i), _yrow(hy_hi, 1, i), _zcol(hz_lo, 1, i), _zcol(hz_hi, 1, i))
+        srcs[1].append(a1 + cross_rate * (w * _flux(a1, a_n, fc)))
+    _local_solves(fac_ref, srcs, loc_ref, vals_ref)
+
+
 def _gradient_kernel(pore_ref, lab_ref, a2_ref, gy_lo, gy_hi, gz_lo, gz_hi,
                      hy_lo, hy_hi, hz_lo, hz_hi, out_ref):
     m = pore_ref.shape[0]
     for i in range(m):
-        mob, lab, mob_n, fc = _geo_row(i, pore_ref, lab_ref, gy_lo, gy_hi, gz_lo, gz_hi)
+        mob, _, _, fc = _geo_row(i, pore_ref, lab_ref, gy_lo, gy_hi, gz_lo, gz_hi)
         w = 0.5 * (1.0 + mob)
         a2 = a2_ref[i]
         a_n = _neighbours(a2, _yrow(hy_lo, 0, i), _yrow(hy_hi, 0, i), _zcol(hz_lo, 0, i), _zcol(hz_hi, 0, i))
@@ -315,6 +321,26 @@
     return lo, hi
 
 
+def _first_call(m, ny, nz):
+    return pl.pallas_call(
+        _first_kernel,
+        out_shape=(
+            jax.ShapeDtypeStruct((2, m, ny, nz), F32),
+            jax.ShapeDtypeStruct((2, 2, ny, nz), F32),
+        ),
+        in_specs=[_vmem()] * 9,
+        out_specs=(_vmem(), _vmem()),
+    )
+
+
+def _gather_blk(x):
+    n = lax.axis_size("blk")
+    parts = [x]
+    for k in range(1, n):
+        parts.append(lax.ppermute(x, "blk", [(j, (j + k) % n) for j in range(n)]))
+    return jnp.stack(parts)
+
+
 def _edge_shapes(chans, m, ny, nz):
     return (
         jax.ShapeDtypeStruct((chans, m, nz), F32),
@@ -330,7 +356,7 @@
     return gy_lo, gy_hi, gz_lo, gz_hi
 
 
-def shards(vacancy, grain_label, pore_mask, cotangent):
+def _shards(vacancy, grain_label, pore_mask, cotangent):
     m, ny, nz = vacancy.shape
     n_blk = lax.axis_size("blk")
     cycle_step = float((m * n_blk) ** 2 // 64)
@@ -345,27 +371,31 @@
     bx_lo, bx_hi = _exchange(outs[4], outs[5], "blk", True)
     gy_lo, gy_hi, gz_lo, gz_hi = _yz_halos(*outs[:4])
 
-    fac, loc, rows = pl.pallas_call(
-        lambda *r: _prep_kernel(cycle_step, *r),
+    fac, lr, rows = pl.pallas_call(
+        lambda *r: _factor_kernel(cycle_step, *r),
         out_shape=(
-            jax.ShapeDtypeStruct((2, 5, m, ny, nz), F32),
-            jax.ShapeDtypeStruct((2, m, ny, nz), F32),
-            jax.ShapeDtypeStruct((2, 7, ny, nz), F32),
+            jax.ShapeDtypeStruct((2, 3, m, ny, nz), F32),
+            jax.ShapeDtypeStruct((2, 2, m, ny, nz), F32),
+            jax.ShapeDtypeStruct((2, 5, ny, nz), F32),
         ),
-        in_specs=[_vmem()] * 10,
+        in_specs=[_vmem()] * 4,
         out_specs=(_vmem(), _vmem(), _vmem()),
-    )(vacancy, pore_mask, grain_label, cotangent, bx_lo, bx_hi, gy_lo, gy_hi, gz_lo, gz_hi)
-
-    gathered = lax.all_gather(rows, "blk", axis=0, tiled=False)
+    )(pore_mask, grain_label, bx_lo, bx_hi)
+    gathered = _gather_blk(rows)
+
+    loc, vals = _first_call(m, ny, nz)(
+        vacancy, cotangent, pore_mask, grain_label, fac, gy_lo, gy_hi, gz_lo, gz_hi
+    )
+    gathered1 = _gather_blk(vals)
     pos = jnp.reshape(lax.axis_index("blk"), (1,)).astype(jnp.int32)
 
     outs = pl.pallas_call(
-        lambda *r: _combine_kernel(5, True, {0: 0, 1: 1}, *r),
+        lambda *r: _combine_kernel(0, True, {0: 0, 1: 1}, *r),
         out_shape=(jax.ShapeDtypeStruct((2, m, ny, nz), F32),) + _edge_shapes(2, m, ny, nz),
         in_specs=[_smem()] + [_vmem()] * 4,
         out_specs=tuple(_vmem() for _ in range(5)),
         scratch_shapes=[pltpu.VMEM((n_blk, ny, nz), F32)],
-    )(pos, gathered, gathered, fac, loc)
+    )(pos, gathered, gathered1, lr, loc)
     fa = outs[0]
 
     hy_lo, hy_hi, hz_lo, hz_hi = _yz_halos(*outs[1:])
@@ -379,14 +409,14 @@
         out_specs=(_vmem(), _vmem()),
     )(pore_mask, grain_label, fa, fac, gy_lo, gy_hi, gz_lo, gz_hi, hy_lo, hy_hi, hz_lo, hz_hi)
 
-    gathered2 = lax.all_gather(vals2, "blk", axis=0, tiled=False)
+    gathered2 = _gather_blk(vals2)
     outs = pl.pallas_call(
         lambda *r: _combine_kernel(0, False, {1: 0}, *r),
         out_shape=(shape, shape) + _edge_shapes(1, m, ny, nz),
         in_specs=[_smem()] + [_vmem()] * 4,
         out_specs=tuple(_vmem() for _ in range(6)),
         scratch_shapes=[pltpu.VMEM((n_blk, ny, nz), F32)],
-    )(pos, gathered, gathered2, fac, loc2)
+    )(pos, gathered, gathered2, lr, loc2)
     final_field, adjoint_two = outs[:2]
 
     a2_lo, a2_hi, a2z_lo, a2z_hi = _yz_halos(*outs[2:])
@@ -407,4 +437,4 @@
         P("blk", "gy", "gz"),
     )
     out_specs = (P("blk", "gy", "gz"), P("blk", "gy", "gz"))
-    return jax.shard_map(shards, mesh=mesh, in_specs=in_specs, out_specs=out_specs, check_vma=False)
+    return jax.shard_map(_shards, mesh=mesh, in_specs=in_specs, out_specs=out_specs, check_vma=False)

time: 96.2 us -> 89.5 us (0.930)
  the two profiles are of different devices: /device:TPU:4 before, /device:TPU:12 now
where the time goes in v3:
time: 89.5 us; the launch traced here: 89 us
  starting transfers between devices  39.2 us (44%)
  Pallas kernels  28.9 us (32%)
  waiting for transfers between devices  13.7 us (15%)
  other arithmetic  3.74 us (4%)
  local copies, waits for them, and re-layouts  2.47 us (3%)
  between operations  0.91 us (1%)
    ppermute x7, starting transfers between devices, _exchange(): hi = lax.ppermute(first, axis, backward)  18.5 us
    ppermute x7, starting transfers between devices, _exchange(): lo = lax.ppermute(last, axis, forward)  17.7 us
    ppermute x7, waiting for transfers between devices, _exchange(): hi = lax.ppermute(first, axis, backward)  6.85 us
    ppermute x3, waiting for transfers between devices, _gather_blk(): parts.append(lax.ppermute(x, 'blk', [(j, (j + k) % n) for j in range(n)]))  6.85 us
    pallas_call x1, Pallas kernels, _shards(): pl.pallas_call(_second_kernel, out_shape=(jax.ShapeDtypeStruct((2, m, ny,...  6.01 us
    pallas_call x1, Pallas kernels, _shards(): _first_call(m, ny, nz)  5.65 us
    pallas_call x1, Pallas kernels, _shards(): pl.pallas_call(lambda *r: _factor_kernel(cycle_step, *r), out_shape=(jax....  4.45 us
    pallas_call x1, Pallas kernels, _shards(): pl.pallas_call(_gradient_kernel, out_shape=shape, in_specs=[_vmem()] * 11...  3.84 us
  transfers between devices with their start and end apart: 17, of which 5 were waited for; matrix products, arithmetic and copies ran while one was open for 2% of the time, Pallas kernels for 5%

profile of v3, /device:TPU:12, one launch (start us, length us, event | category | flops | bytes accessed | tf_op | source)
XLA Modules:
  0.0 89.0 jit_solution(5118905539224293904)
XLA Ops:
  0.6 2.5 %shard_map.59 = (f32[3,32,256]{2,1,0:T(8,128)}, f32[3,32,256]{2,1,0:T(8,128)}, f32[3,16,32]{2,1,0:T(8,128)}, f32[3,16,32]{2,1,0:T(8,128)}, f32[2,16,256]{2,1,0:T(8,128)}, /*index=5*/f32[2,16,256]{2,1,0:T(8,128)}) custom-call(f32[32,16,256]{2,1,0:T(8,128)} %vac_ref.3, s32[32,16,256]{2,1,0:T(8,128)} %pore_ref.7, s32[32,16,256]{2,1,0:T(8,128)} %lab_ref.7), custom_call_target="tpu_custom_call" | custom-call | tf_op jit(solution)/shard_map/pallas_call | solution.py:365
  3.1 1.9 %collective-permute-start.3 = (f32[3,32,256]{2,1,0:T(8,128)}, f32[3,32,256]{2,1,0:T(8,128)S(1)}, u32[]{:S(2)}, u32[]{:S(2)}) collective-permute-start(f32[3,32,256]{2,1,0:T(8,128)} %get-tuple-element.30), channel_id=1, source_target_pairs={{0,4},{4,8},{8,12},{1,5},{5,9},{9,13},{2,6},{6,10},{10,14},{3,7},{... | collective-permute-start | bytes 294920 | tf_op jit(solution)/shard_map/ppermute | solution.py:319
  5.0 3.6 %collective-permute-start.4 = (f32[3,32,256]{2,1,0:T(8,128)}, f32[3,32,256]{2,1,0:T(8,128)S(1)}, u32[]{:S(2)}, u32[]{:S(2)}) collective-permute-start(f32[3,32,256]{2,1,0:T(8,128)} %get-tuple-element.31), channel_id=1, source_target_pairs={{4,0},{8,4},{12,8},{5,1},{9,5},{13,9},{6,2},{10,6},{14,10},{7,3},{... | collective-permute-start | bytes 294920 | tf_op jit(solution)/shard_map/ppermute | solution.py:320
  8.6 1.6 %collective-permute-start = (f32[2,16,256]{2,1,0:T(8,128)}, f32[2,16,256]{2,1,0:T(8,128)S(1)}, u32[]{:S(2)}, u32[]{:S(2)}) collective-permute-start(f32[2,16,256]{2,1,0:T(8,128)} %get-tuple-element.26), channel_id=1, source_target_pairs={{0,16},{16,0},{1,17},{17,1},{2,18},{18,2},{3,19},{19,3},{4,20},{20... | collective-permute-start | bytes 98312 | tf_op jit(solution)/shard_map/ppermute | solution.py:319
  10.2 0.5 collective-permute-start.1
  10.7 3.5 %collective-permute-start.5 = (f32[3,16,32]{2,1,0:T(8,128)}, f32[3,16,32]{2,1,0:T(8,128)S(1)}, u32[]{:S(2)}, u32[]{:S(2)}) collective-permute-start(f32[3,16,32]{2,1,0:T(8,128)} %get-tuple-element.32), channel_id=1, source_target_pairs={{0,1},{1,2},{2,3},{4,5},{5,6},{6,7},{8,9},{9,10},{10,11},{12,13},{... | collective-permute-start | bytes 18440 | tf_op jit(solution)/shard_map/ppermute | solution.py:319
  14.2 0.0 collective-permute-done.r_2_
  14.2 2.4 %collective-permute-start.6 = (f32[3,16,32]{2,1,0:T(8,128)}, f32[3,16,32]{2,1,0:T(8,128)S(1)}, u32[]{:S(2)}, u32[]{:S(2)}) collective-permute-start(f32[3,16,32]{2,1,0:T(8,128)} %get-tuple-element.33), channel_id=1, source_target_pairs={{1,0},{2,1},{3,2},{5,4},{6,5},{7,6},{9,8},{10,9},{11,10},{13,12},{... | collective-permute-start | bytes 18440 | tf_op jit(solution)/shard_map/ppermute | solution.py:320
  16.6 0.0 collective-permute-done.1.r_3_
  16.6 0.6 copy-done.10
  17.2 4.4 %shard_map.60 = (f32[2,3,32,16,256]{4,3,2,1,0:T(8,128)}, f32[2,2,32,16,256]{4,3,2,1,0:T(8,128)}, f32[2,5,16,256]{3,2,1,0:T(8,128)}) custom-call(s32[32,16,256]{2,1,0:T(8,128)} %pore_ref.7, s32[32,16,256]{2,1,0:T(8,128)} %lab_ref.7, f32[2,16,256]{2,1,0:T(8,128)} %copy-done.9, f32[2,16,256]{2,1,0:T(8,128)} %copy-done.10), custom_call_target="tpu_custom_call" | custom-call | tf_op jit(solution)/shard_map/pallas_call | solution.py:374
  21.7 0.0 collective-permute-done.3.gy_lo
  21.7 0.0 collective-permute-done.4.gy_hi
  21.7 0.5 copy-done.2
  22.3 0.0 copy-done.3
  22.3 0.0 copy-done
  22.3 0.0 copy-done.1
  22.4 5.6 %shard_map.61 = (f32[2,32,16,256]{3,2,1,0:T(8,128)}, f32[2,2,16,256]{3,2,1,0:T(8,128)}) custom-call(f32[32,16,256]{2,1,0:T(8,128)} %vac_ref.3, f32[32,16,256]{2,1,0:T(8,128)} %cot_ref.1, s32[32,16,256]{2,1,0:T(8,128)} %pore_ref.7, s32[32,16,256]{2,1,0:T(8,128)} %lab_ref.7, f32[2,3,32,16,256]{4,3,2,1,0:T(8,128)} %get-tuple-element.29.fac_ref, ...), custom_call_target="tpu_custom_call" | custom-call | tf_op jit(solution)/shard_map/pallas_call | solution.py:386
  28.0 1.5 %collective-permute-start.7 = (f32[2,2,16,256]{3,2,1,0:T(8,128)}, f32[2,2,16,256]{3,2,1,0:T(8,128)S(1)}, u32[]{:S(2)}, u32[]{:S(2)}) collective-permute-start(f32[2,2,16,256]{3,2,1,0:T(8,128)} %get-tuple-element.34), channel_id=1, source_target_pairs={{0,16},{16,0},{1,17},{17,1},{2,18},{18,2},{3,19},{19,3},{4,20},{20... | collective-permute-start | bytes 196616 | tf_op jit(solution)/shard_map/ppermute | solution.py:340
  29.5 0.5 collective-permute-start.2
  30.1 2.4 %collective-permute-done.7 = f32[2,2,16,256]{3,2,1,0:T(8,128)S(1)} collective-permute-done((f32[2,2,16,256]{3,2,1,0:T(8,128)}, f32[2,2,16,256]{3,2,1,0:T(8,128)S(1)}, u32[]{:S(2)}, u32[]{:S(2)}) %collective-permute-start.7) | collective-permute-done | bytes 65568 | tf_op jit(solution)/shard_map/ppermute | solution.py:340
  32.5 1.5 %pad_maximum_fusion.1.r_2_ = f32[2,2,2,16,256]{4,3,2,1,0:T(8,128)} fusion(f32[1,2,2,16,256]{4,3,2,1,0:T(8,128)S(1)} %bitcast.10, f32[1,2,2,16,256]{4,3,2,1,0:T(8,128)} %bitcast.9), kind=kLoop, calls=%fused_computation.1 | loop fusion | flops 32768 | bytes 262144 | tf_op jit(solution)/shard_map/stack | solution.py:341
  34.0 0.8 collective-permute-done.2
  34.9 0.7 pad_maximum_fusion.r_1_
  35.6 3.3 %shard_map.62 = (f32[2,32,16,256]{3,2,1,0:T(8,128)}, f32[2,32,256]{2,1,0:T(8,128)}, f32[2,32,256]{2,1,0:T(8,128)}, f32[2,16,32]{2,1,0:T(8,128)}, f32[2,16,32]{2,1,0:T(8,128)}) custom-call(s32[1]{0:T(128)} %bitcast.r_0_, f32[2,2,5,16,256]{4,3,2,1,0:T(8,128)} %pad_maximum_fusion.r_1_, f32[2,2,2,16,256]{4,3,2,1,0:T(8,128)} %pad_maximum_fusion.1.r_2_, ...), custom_call_target="tpu_custom_call" | custom-call | tf_op jit(solution)/shard_map/pallas_call | solution.py:392
  38.9 1.9 %collective-permute-start.8 = (f32[2,32,256]{2,1,0:T(8,128)}, f32[2,32,256]{2,1,0:T(8,128)S(1)}, u32[]{:S(2)}, u32[]{:S(2)}) collective-permute-start(f32[2,32,256]{2,1,0:T(8,128)} %get-tuple-element.38), channel_id=1, source_target_pairs={{0,4},{4,8},{8,12},{1,5},{5,9},{9,13},{2,6},{6,10},{10,14},{3,7},{... | collective-permute-start | bytes 196616 | tf_op jit(solution)/shard_map/ppermute | solution.py:319
  40.9 3.6 %collective-permute-start.9 = (f32[2,32,256]{2,1,0:T(8,128)}, f32[2,32,256]{2,1,0:T(8,128)S(1)}, u32[]{:S(2)}, u32[]{:S(2)}) collective-permute-start(f32[2,32,256]{2,1,0:T(8,128)} %get-tuple-element.39), channel_id=1, source_target_pairs={{4,0},{8,4},{12,8},{5,1},{9,5},{13,9},{6,2},{10,6},{14,10},{7,3},{... | collective-permute-start | bytes 196616 | tf_op jit(solution)/shard_map/ppermute | solution.py:320
  44.5 3.5 %collective-permute-start.10 = (f32[2,16,32]{2,1,0:T(8,128)}, f32[2,16,32]{2,1,0:T(8,128)S(1)}, u32[]{:S(2)}, u32[]{:S(2)}) collective-permute-start(f32[2,16,32]{2,1,0:T(8,128)} %get-tuple-element.40), channel_id=1, source_target_pairs={{0,1},{1,2},{2,3},{4,5},{5,6},{6,7},{8,9},{9,10},{10,11},{12,13},{... | collective-permute-start | bytes 12296 | tf_op jit(solution)/shard_map/ppermute | solution.py:319
  48.0 2.4 %collective-permute-start.11 = (f32[2,16,32]{2,1,0:T(8,128)}, f32[2,16,32]{2,1,0:T(8,128)S(1)}, u32[]{:S(2)}, u32[]{:S(2)}) collective-permute-start(f32[2,16,32]{2,1,0:T(8,128)} %get-tuple-element.41), channel_id=1, source_target_pairs={{1,0},{2,1},{3,2},{5,4},{6,5},{7,6},{9,8},{10,9},{11,10},{13,12},{... | collective-permute-start | bytes 12296 | tf_op jit(solution)/shard_map/ppermute | solution.py:320
  50.4 0.0 collective-permute-done.10.hz_lo
  50.4 3.5 %collective-permute-done.11.hz_hi = f32[2,16,32]{2,1,0:T(8,128)S(1)} collective-permute-done((f32[2,16,32]{2,1,0:T(8,128)}, f32[2,16,32]{2,1,0:T(8,128)S(1)}, u32[]{:S(2)}, u32[]{:S(2)}) %collective-permute-start.11) | collective-permute-done | bytes 4128 | tf_op jit(solution)/shard_map/ppermute | solution.py:320
  53.9 0.6 copy-done.12
  54.5 0.0 copy-done.5
  54.5 0.0 copy-done.6
  54.5 6.0 %shard_map.63 = (f32[2,32,16,256]{3,2,1,0:T(8,128)}, f32[2,2,16,256]{3,2,1,0:T(8,128)}) custom-call(s32[32,16,256]{2,1,0:T(8,128)} %pore_ref.7, s32[32,16,256]{2,1,0:T(8,128)} %lab_ref.7, f32[2,32,16,256]{3,2,1,0:T(8,128)} %get-tuple-element.37.fa_ref, f32[2,3,32,16,256]{4,3,2,1,0:T(8,128)} %get-tuple-element.29.fac_ref, f32[3,32,256]{2,1,0:T(8,128)} %copy-done, ...), custom_call_target="tpu_custom_call" | custom-call | tf_op jit(solution)/shard_map/pallas_call | solution.py:402
  60.5 0.9 %collective-permute-start.12 = (f32[2,2,16,256]{3,2,1,0:T(8,128)}, f32[2,2,16,256]{3,2,1,0:T(8,128)S(1)}, u32[]{:S(2)}, u32[]{:S(2)}) collective-permute-start(f32[2,2,16,256]{3,2,1,0:T(8,128)} %get-tuple-element.42), channel_id=1, source_target_pairs={{0,16},{16,0},{1,17},{17,1},{2,18},{18,2},{3,19},{19,3},{4,20},{20... | collective-permute-start | bytes 196616 | tf_op jit(solution)/shard_map/ppermute | solution.py:340
  61.4 3.6 %collective-permute-done.12 = f32[2,2,16,256]{3,2,1,0:T(8,128)S(1)} collective-permute-done((f32[2,2,16,256]{3,2,1,0:T(8,128)}, f32[2,2,16,256]{3,2,1,0:T(8,128)S(1)}, u32[]{:S(2)}, u32[]{:S(2)}) %collective-permute-start.12) | collective-permute-done | bytes 65568 | tf_op jit(solution)/shard_map/ppermute | solution.py:340
  65.0 1.5 %pad_maximum_fusion.2.r_2_ = f32[2,2,2,16,256]{4,3,2,1,0:T(8,128)} fusion(f32[1,2,2,16,256]{4,3,2,1,0:T(8,128)S(1)} %bitcast.12, f32[1,2,2,16,256]{4,3,2,1,0:T(8,128)} %bitcast.11), kind=kLoop, calls=%fused_computation.2 | loop fusion | flops 32768 | bytes 262144 | tf_op jit(solution)/shard_map/stack | solution.py:341
  66.5 3.2 %shard_map.64 = (f32[32,16,256]{2,1,0:T(8,128)}, f32[32,16,256]{2,1,0:T(8,128)}, f32[1,32,256]{2,1,0:T(8,128)}, f32[1,32,256]{2,1,0:T(8,128)}, f32[1,16,32]{2,1,0:T(8,128)}, /*index=5*/f32[1,16,32]{2,1,0:T(8,128)}) custom-call(s32[1]{0:T(128)} %bitcast.r_0_, f32[2,2,5,16,256]{4,3,2,1,0:T(8,128)} %pad_maximum_fusion.r_1_, ...), custom_call_target="tpu_custom_call" | custom-call | tf_op jit(solution)/shard_map/pallas_call | solution.py:413
  69.7 1.9 %collective-permute-start.13 = (f32[1,32,256]{2,1,0:T(8,128)}, f32[1,32,256]{2,1,0:T(8,128)S(1)}, u32[]{:S(2)}, u32[]{:S(2)}) collective-permute-start(f32[1,32,256]{2,1,0:T(8,128)} %get-tuple-element.46), channel_id=1, source_target_pairs={{0,4},{4,8},{8,12},{1,5},{5,9},{9,13},{2,6},{6,10},{10,14},{3,7},{... | collective-permute-start | bytes 98312 | tf_op jit(solution)/shard_map/ppermute | solution.py:319
  71.6 3.6 %collective-permute-start.14 = (f32[1,32,256]{2,1,0:T(8,128)}, f32[1,32,256]{2,1,0:T(8,128)S(1)}, u32[]{:S(2)}, u32[]{:S(2)}) collective-permute-start(f32[1,32,256]{2,1,0:T(8,128)} %get-tuple-element.47), channel_id=1, source_target_pairs={{4,0},{8,4},{12,8},{5,1},{9,5},{13,9},{6,2},{10,6},{14,10},{7,3},{... | collective-permute-start | bytes 98312 | tf_op jit(solution)/shard_map/ppermute | solution.py:320
  75.2 3.5 %collective-permute-start.15 = (f32[1,16,32]{2,1,0:T(8,128)}, f32[1,16,32]{2,1,0:T(8,128)S(1)}, u32[]{:S(2)}, u32[]{:S(2)}) collective-permute-start(f32[1,16,32]{2,1,0:T(8,128)} %get-tuple-element.48), channel_id=1, source_target_pairs={{0,1},{1,2},{2,3},{4,5},{5,6},{6,7},{8,9},{9,10},{10,11},{12,13},{... | collective-permute-start | bytes 6152 | tf_op jit(solution)/shard_map/ppermute | solution.py:319
  78.7 2.4 %collective-permute-start.16 = (f32[1,16,32]{2,1,0:T(8,128)}, f32[1,16,32]{2,1,0:T(8,128)S(1)}, u32[]{:S(2)}, u32[]{:S(2)}) collective-permute-start(f32[1,16,32]{2,1,0:T(8,128)} %get-tuple-element.49), channel_id=1, source_target_pairs={{1,0},{2,1},{3,2},{5,4},{6,5},{7,6},{9,8},{10,9},{11,10},{13,12},{... | collective-permute-start | bytes 6152 | tf_op jit(solution)/shard_map/ppermute | solution.py:320
  81.1 3.4 %collective-permute-done.16.hz_hi = f32[1,16,32]{2,1,0:T(8,128)S(1)} collective-permute-done((f32[1,16,32]{2,1,0:T(8,128)}, f32[1,16,32]{2,1,0:T(8,128)S(1)}, u32[]{:S(2)}, u32[]{:S(2)}) %collective-permute-start.16) | collective-permute-done | bytes 2080 | tf_op jit(solution)/shard_map/ppermute | solution.py:320
  84.5 0.6 copy-done.14
  85.1 0.0 copy-done.7
  85.1 0.0 copy-done.8
  85.1 3.8 %shard_map.65 = f32[32,16,256]{2,1,0:T(8,128)} custom-call(s32[32,16,256]{2,1,0:T(8,128)} %pore_ref.7, s32[32,16,256]{2,1,0:T(8,128)} %lab_ref.7, f32[32,16,256]{2,1,0:T(8,128)} %get-tuple-element.45.a2_ref, f32[3,32,256]{2,1,0:T(8,128)} %copy-done, f32[3,32,256]{2,1,0:T(8,128)} %copy-done.1, f32[3,16,32]{2,1,0:T(8,128)} %copy-done.2, ...), custom_call_target="tpu_custom_call" | custom-call | tf_op jit(solution)/shard_map/pallas_call | solution.py:423
  (26 shorter events, 0.1 us)
Async XLA Ops:
  3.1 18.6 %collective-permute-start.3 = (f32[3,32,256]{2,1,0:T(8,128)}, f32[3,32,256]{2,1,0:T(8,128)S(1)}, u32[]{:S(2)}, u32[]{:S(2)}) collective-permute-start(f32[3,32,256]{2,1,0:T(8,128)} %get-tuple-element.30), channel_id=1, source_target_pairs={{0,4},{4,8},{8,12},{1,5},{5,9},{9,13},{2,6},{6,10},{10,14},{3,7},{... | collective-permute-start | bytes 294920 | tf_op jit(solution)/shard_map/ppermute | solution.py:319
  5.0 16.7 %collective-permute-start.4 = (f32[3,32,256]{2,1,0:T(8,128)}, f32[3,32,256]{2,1,0:T(8,128)S(1)}, u32[]{:S(2)}, u32[]{:S(2)}) collective-permute-start(f32[3,32,256]{2,1,0:T(8,128)} %get-tuple-element.31), channel_id=1, source_target_pairs={{4,0},{8,4},{12,8},{5,1},{9,5},{13,9},{6,2},{10,6},{14,10},{7,3},{... | collective-permute-start | bytes 294920 | tf_op jit(solution)/shard_map/ppermute | solution.py:320
  8.6 5.6 %collective-permute-start = (f32[2,16,256]{2,1,0:T(8,128)}, f32[2,16,256]{2,1,0:T(8,128)S(1)}, u32[]{:S(2)}, u32[]{:S(2)}) collective-permute-start(f32[2,16,256]{2,1,0:T(8,128)} %get-tuple-element.26), channel_id=1, source_target_pairs={{0,16},{16,0},{1,17},{17,1},{2,18},{18,2},{3,19},{19,3},{4,20},{20... | collective-permute-start | bytes 98312 | tf_op jit(solution)/shard_map/ppermute | solution.py:319
  10.2 6.4 %collective-permute-start.1 = (f32[2,16,256]{2,1,0:T(8,128)}, f32[2,16,256]{2,1,0:T(8,128)S(1)}, u32[]{:S(2)}, u32[]{:S(2)}) collective-permute-start(f32[2,16,256]{2,1,0:T(8,128)} %get-tuple-element.27), channel_id=1, source_target_pairs={{16,0},{0,16},{17,1},{1,17},{18,2},{2,18},{19,3},{3,19},{20,4},{4,... | collective-permute-start | bytes 98312 | tf_op jit(solution)/shard_map/ppermute | solution.py:320
  10.7 10.9 %collective-permute-start.5 = (f32[3,16,32]{2,1,0:T(8,128)}, f32[3,16,32]{2,1,0:T(8,128)S(1)}, u32[]{:S(2)}, u32[]{:S(2)}) collective-permute-start(f32[3,16,32]{2,1,0:T(8,128)} %get-tuple-element.32), channel_id=1, source_target_pairs={{0,1},{1,2},{2,3},{4,5},{5,6},{6,7},{8,9},{9,10},{10,11},{12,13},{... | collective-permute-start | bytes 18440 | tf_op jit(solution)/shard_map/ppermute | solution.py:319
  14.2 2.4 %copy-start.9 = (f32[2,16,256]{2,1,0:T(8,128)}, f32[2,16,256]{2,1,0:T(8,128)S(1)}, u32[]{:S(2)}) copy-start(f32[2,16,256]{2,1,0:T(8,128)S(1)} %collective-permute-done.r_2_) | copy-start | bytes 98308
  14.2 7.4 %collective-permute-start.6 = (f32[3,16,32]{2,1,0:T(8,128)}, f32[3,16,32]{2,1,0:T(8,128)S(1)}, u32[]{:S(2)}, u32[]{:S(2)}) collective-permute-start(f32[3,16,32]{2,1,0:T(8,128)} %get-tuple-element.33), channel_id=1, source_target_pairs={{1,0},{2,1},{3,2},{5,4},{6,5},{7,6},{9,8},{10,9},{11,10},{13,12},{... | collective-permute-start | bytes 18440 | tf_op jit(solution)/shard_map/ppermute | solution.py:320
  16.6 0.6 copy-start.10
  21.7 7.9 %copy-start.4 = (f32[2,5,16,256]{3,2,1,0:T(8,128)S(1)}, f32[2,5,16,256]{3,2,1,0:T(8,128)}, u32[]{:S(2)}) copy-start(f32[2,5,16,256]{3,2,1,0:T(8,128)} %get-tuple-element.28) | copy-start | bytes 491524
  21.7 0.6 copy-start.2
  21.7 0.6 copy-start.3
  21.7 0.6 copy-start
  21.7 0.7 copy-start.1
  28.0 4.5 %collective-permute-start.7 = (f32[2,2,16,256]{3,2,1,0:T(8,128)}, f32[2,2,16,256]{3,2,1,0:T(8,128)S(1)}, u32[]{:S(2)}, u32[]{:S(2)}) collective-permute-start(f32[2,2,16,256]{3,2,1,0:T(8,128)} %get-tuple-element.34), channel_id=1, source_target_pairs={{0,16},{16,0},{1,17},{17,1},{2,18},{18,2},{3,19},{19,3},{4,20},{20... | collective-permute-start | bytes 196616 | tf_op jit(solution)/shard_map/ppermute | solution.py:340
  29.5 5.3 %collective-permute-start.2 = (f32[2,5,16,256]{3,2,1,0:T(8,128)S(1)}, f32[2,5,16,256]{3,2,1,0:T(8,128)S(1)}, u32[]{:S(2)}, u32[]{:S(2)}) collective-permute-start(f32[2,5,16,256]{3,2,1,0:T(8,128)S(1)} %copy-done.4), channel_id=1, source_target_pairs={{0,16},{16,0},{1,17},{17,1},{2,18},{18,2},{3,19},{19,3},{4,20},{20... | collective-permute-start | bytes 491528 | tf_op jit(solution)/shard_map/ppermute | solution.py:340
  38.9 14.9 %collective-permute-start.8 = (f32[2,32,256]{2,1,0:T(8,128)}, f32[2,32,256]{2,1,0:T(8,128)S(1)}, u32[]{:S(2)}, u32[]{:S(2)}) collective-permute-start(f32[2,32,256]{2,1,0:T(8,128)} %get-tuple-element.38), channel_id=1, source_target_pairs={{0,4},{4,8},{8,12},{1,5},{5,9},{9,13},{2,6},{6,10},{10,14},{3,7},{... | collective-permute-start | bytes 196616 | tf_op jit(solution)/shard_map/ppermute | solution.py:319
  40.9 13.0 %collective-permute-start.9 = (f32[2,32,256]{2,1,0:T(8,128)}, f32[2,32,256]{2,1,0:T(8,128)S(1)}, u32[]{:S(2)}, u32[]{:S(2)}) collective-permute-start(f32[2,32,256]{2,1,0:T(8,128)} %get-tuple-element.39), channel_id=1, source_target_pairs={{4,0},{8,4},{12,8},{5,1},{9,5},{13,9},{6,2},{10,6},{14,10},{7,3},{... | collective-permute-start | bytes 196616 | tf_op jit(solution)/shard_map/ppermute | solution.py:320
  44.5 5.9 %collective-permute-start.10 = (f32[2,16,32]{2,1,0:T(8,128)}, f32[2,16,32]{2,1,0:T(8,128)S(1)}, u32[]{:S(2)}, u32[]{:S(2)}) collective-permute-start(f32[2,16,32]{2,1,0:T(8,128)} %get-tuple-element.40), channel_id=1, source_target_pairs={{0,1},{1,2},{2,3},{4,5},{5,6},{6,7},{8,9},{9,10},{10,11},{12,13},{... | collective-permute-start | bytes 12296 | tf_op jit(solution)/shard_map/ppermute | solution.py:319
  48.0 5.8 %collective-permute-start.11 = (f32[2,16,32]{2,1,0:T(8,128)}, f32[2,16,32]{2,1,0:T(8,128)S(1)}, u32[]{:S(2)}, u32[]{:S(2)}) collective-permute-start(f32[2,16,32]{2,1,0:T(8,128)} %get-tuple-element.41), channel_id=1, source_target_pairs={{1,0},{2,1},{3,2},{5,4},{6,5},{7,6},{9,8},{10,9},{11,10},{13,12},{... | collective-permute-start | bytes 12296 | tf_op jit(solution)/shard_map/ppermute | solution.py:320
  50.4 3.5 %copy-start.11 = (f32[2,16,32]{2,1,0:T(8,128)}, f32[2,16,32]{2,1,0:T(8,128)S(1)}, u32[]{:S(2)}) copy-start(f32[2,16,32]{2,1,0:T(8,128)S(1)} %collective-permute-done.10.hz_lo) | copy-start | bytes 12292
  53.8 0.6 copy-start.12
  53.9 0.6 copy-start.5
  53.9 0.6 copy-start.6
  60.5 4.5 %collective-permute-start.12 = (f32[2,2,16,256]{3,2,1,0:T(8,128)}, f32[2,2,16,256]{3,2,1,0:T(8,128)S(1)}, u32[]{:S(2)}, u32[]{:S(2)}) collective-permute-start(f32[2,2,16,256]{3,2,1,0:T(8,128)} %get-tuple-element.42), channel_id=1, source_target_pairs={{0,16},{16,0},{1,17},{17,1},{2,18},{18,2},{3,19},{19,3},{4,20},{20... | collective-permute-start | bytes 196616 | tf_op jit(solution)/shard_map/ppermute | solution.py:340
  69.7 14.8 %collective-permute-start.13 = (f32[1,32,256]{2,1,0:T(8,128)}, f32[1,32,256]{2,1,0:T(8,128)S(1)}, u32[]{:S(2)}, u32[]{:S(2)}) collective-permute-start(f32[1,32,256]{2,1,0:T(8,128)} %get-tuple-element.46), channel_id=1, source_target_pairs={{0,4},{4,8},{8,12},{1,5},{5,9},{9,13},{2,6},{6,10},{10,14},{3,7},{... | collective-permute-start | bytes 98312 | tf_op jit(solution)/shard_map/ppermute | solution.py:319
  71.6 12.9 %collective-permute-start.14 = (f32[1,32,256]{2,1,0:T(8,128)}, f32[1,32,256]{2,1,0:T(8,128)S(1)}, u32[]{:S(2)}, u32[]{:S(2)}) collective-permute-start(f32[1,32,256]{2,1,0:T(8,128)} %get-tuple-element.47), channel_id=1, source_target_pairs={{4,0},{8,4},{12,8},{5,1},{9,5},{13,9},{6,2},{10,6},{14,10},{7,3},{... | collective-permute-start | bytes 98312 | tf_op jit(solution)/shard_map/ppermute | solution.py:320
  75.2 5.9 %collective-permute-start.15 = (f32[1,16,32]{2,1,0:T(8,128)}, f32[1,16,32]{2,1,0:T(8,128)S(1)}, u32[]{:S(2)}, u32[]{:S(2)}) collective-permute-start(f32[1,16,32]{2,1,0:T(8,128)} %get-tuple-element.48), channel_id=1, source_target_pairs={{0,1},{1,2},{2,3},{4,5},{5,6},{6,7},{8,9},{9,10},{10,11},{12,13},{... | collective-permute-start | bytes 6152 | tf_op jit(solution)/shard_map/ppermute | solution.py:319
  78.7 5.8 %collective-permute-start.16 = (f32[1,16,32]{2,1,0:T(8,128)}, f32[1,16,32]{2,1,0:T(8,128)S(1)}, u32[]{:S(2)}, u32[]{:S(2)}) collective-permute-start(f32[1,16,32]{2,1,0:T(8,128)} %get-tuple-element.49), channel_id=1, source_target_pairs={{1,0},{2,1},{3,2},{5,4},{6,5},{7,6},{9,8},{10,9},{11,10},{13,12},{... | collective-permute-start | bytes 6152 | tf_op jit(solution)/shard_map/ppermute | solution.py:320
  81.1 3.4 %copy-start.13 = (f32[1,16,32]{2,1,0:T(8,128)}, f32[1,16,32]{2,1,0:T(8,128)S(1)}, u32[]{:S(2)}) copy-start(f32[1,16,32]{2,1,0:T(8,128)S(1)} %collective-permute-done.15.hz_lo) | copy-start | bytes 6148
  84.5 0.6 copy-start.14
  84.5 0.6 copy-start.7
  84.5 0.6 copy-start.8

commit v4 on v3

--- a/solution.py
+++ b/solution.py
@@ -112,7 +112,8 @@
     return xs
 
 
-def _factor_kernel(cs, pore_ref, lab_ref, bx_lo, bx_hi, fac_ref, lr_ref, rows_ref):
+def _factor_kernel(cs, pore_ref, lab_ref, bx_lo, bx_hi, fac_f, fac_a, lr_f, lr_a, rows_ref):
+    facs, lrs = (fac_f, fac_a), (lr_f, lr_a)
     m = pore_ref.shape[0]
     zero = jnp.zeros(pore_ref.shape[1:], F32)
     mobs = [1.0 + 2.0 * pore_ref[r].astype(F32) for r in range(m)]
@@ -148,11 +149,11 @@
         left = _sweep(m, lower, pivots, ratios, left_src)
         right = _sweep(m, lower, pivots, ratios, right_src)
         for r in range(m):
-            fac_ref[c, 0, r] = lower[r]
-            fac_ref[c, 1, r] = ratios[r] if r < m - 1 else zero
-            fac_ref[c, 2, r] = pivots[r] if r < m - 1 else zero + 1.0
-            lr_ref[c, 0, r] = left[r] if r < m - 1 else zero
-            lr_ref[c, 1, r] = right[r] if r < m - 1 else zero - 1.0
+            facs[c][0, r] = lower[r]
+            facs[c][1, r] = ratios[r] if r < m - 1 else zero
+            facs[c][2, r] = pivots[r] if r < m - 1 else zero + 1.0
+            lrs[c][0, r] = left[r] if r < m - 1 else zero
+            lrs[c][1, r] = right[r] if r < m - 1 else zero - 1.0
         last_lower = lower[m - 1]
         rows_ref[c, 0] = last_lower * left[m - 2]
         rows_ref[c, 1] = main[m - 1] - last_lower * right[m - 2]
@@ -161,10 +162,11 @@
         rows_ref[c, 4] = right[0]
 
 
-def _reduced_solve(gs, gv, voff, c, n, pos):
+def _reduced_solve(gs, gv, voff, c, n, pos, cv=None):
+    cv = c if cv is None else cv
     slot = [(pos - p + n) % n for p in range(n)]
     g = [[gs[slot[p], c, k] for k in range(5)] for p in range(n)]
-    v = [[gv[slot[p], c, voff + k] for k in range(2)] for p in range(n)]
+    v = [[gv[slot[p], cv, voff + k] for k in range(2)] for p in range(n)]
     lower = [-g[p][0] for p in range(n)]
     main = [g[p][1] - g[p][2] * g[(p + 1) % n][3] for p in range(n)]
     upper = [-g[p][2] * g[(p + 1) % n][4] for p in range(n)]
@@ -206,31 +208,6 @@
     inner = apply(src[:k_in])
     sep = (src[k_in] - lower[k_in] * inner[k_in - 1] - upper[k_in] * inner[0]) / closing
     return [inner[r] - linked[r] * sep for r in range(k_in)] + [sep]
-
-
-def _combine_kernel(voff, stacked, edge_of, pos_ref, gs_ref, gv_ref, lr_ref, loc_ref, *refs):
-    if stacked:
-        out_ref = refs[0]
-        outs = (out_ref.at[0], out_ref.at[1])
-        rest = refs[1:]
-    else:
-        outs = refs[:2]
-        rest = refs[2:]
-    edges, sep_ref = rest[:4], rest[4]
-    n = gs_ref.shape[0]
-    m = loc_ref.shape[1]
-    p = pos_ref[0]
-    for c in range(2):
-        seps = _reduced_solve(gs_ref, gv_ref, voff, c, n, p)
-        for q in range(n):
-            sep_ref[q] = seps[q]
-        own = sep_ref[p]
-        prior = sep_ref[(p + n - 1) % n]
-        for r in range(m):
-            val = loc_ref[c, r] - lr_ref[c, 0, r] * prior - lr_ref[c, 1, r] * own
-            outs[c][r] = val
-            if c in edge_of:
-                _write_edges(edges, edge_of[c], r, val)
 
 
 def _edge_kernel(vac_ref, pore_ref, lab_ref, y_first, y_last, z_first, z_last, bx_first, bx_last):
@@ -249,49 +226,81 @@
             bx_last[1] = lab
 
 
-def _local_solves(fac_ref, srcs, loc_ref, vals_ref):
-    m = loc_ref.shape[1]
-    zero = jnp.zeros(loc_ref.shape[2:], F32)
-    for c in range(2):
-        lower = [fac_ref[c, 0, r] for r in range(m)]
-        ratios = [fac_ref[c, 1, r] for r in range(m - 1)]
-        pivots = [fac_ref[c, 2, r] for r in range(m - 1)]
-        src = srcs[c]
-        local = _sweep(m, lower, pivots, ratios, src[: m - 1] + [None])
-        for r in range(m):
-            loc_ref[c, r] = local[r] if r < m - 1 else zero
-        vals_ref[c, 0] = src[m - 1] - lower[m - 1] * local[m - 2]
-        vals_ref[c, 1] = local[0]
-
-
-def _first_kernel(vac_ref, cot_ref, pore_ref, lab_ref, fac_ref, gy_lo, gy_hi, gz_lo, gz_hi, loc_ref, vals_ref):
+def _solve_one(fac_ref, src, loc_ref, vals_ref):
+    m = loc_ref.shape[0]
+    zero = jnp.zeros(loc_ref.shape[1:], F32)
+    lower = [fac_ref[0, r] for r in range(m)]
+    ratios = [fac_ref[1, r] for r in range(m - 1)]
+    pivots = [fac_ref[2, r] for r in range(m - 1)]
+    local = _sweep(m, lower, pivots, ratios, src[: m - 1] + [None])
+    for r in range(m):
+        loc_ref[r] = local[r] if r < m - 1 else zero
+    vals_ref[0] = src[m - 1] - lower[m - 1] * local[m - 2]
+    vals_ref[1] = local[0]
+
+
+def _first_fwd_kernel(vac_ref, pore_ref, lab_ref, fac_ref, gy_lo, gy_hi, gz_lo, gz_hi, loc_ref, vals_ref):
     m = pore_ref.shape[0]
-    srcs = ([], [cot_ref[r] for r in range(m)])
+    src = []
     for i in range(m):
         mob, _, mob_n, fc = _geo_row(i, pore_ref, lab_ref, gy_lo, gy_hi, gz_lo, gz_hi)
         w = 0.5 * (1.0 + mob)
         v = vac_ref[i]
         v_n = _neighbours(v, _yrow(gy_lo, 2, i), _yrow(gy_hi, 2, i), _zcol(gz_lo, 2, i), _zcol(gz_hi, 2, i))
         u_n = [0.5 * (1.0 + mn) * vn for mn, vn in zip(mob_n, v_n)]
-        srcs[0].append(v + cross_rate * (1.0 * _flux(w * v, u_n, fc)))
-    _local_solves(fac_ref, srcs, loc_ref, vals_ref)
-
-
-def _second_kernel(pore_ref, lab_ref, fa_ref, fac_ref, gy_lo, gy_hi, gz_lo, gz_hi,
-                   hy_lo, hy_hi, hz_lo, hz_hi, loc_ref, vals_ref):
+        src.append(v + cross_rate * (1.0 * _flux(w * v, u_n, fc)))
+    _solve_one(fac_ref, src, loc_ref, vals_ref)
+
+
+def _first_adj_kernel(cot_ref, fac_ref, loc_ref, vals_ref):
+    _solve_one(fac_ref, [cot_ref[r] for r in range(cot_ref.shape[0])], loc_ref, vals_ref)
+
+
+def _second_one_kernel(ch, pore_ref, lab_ref, x_ref, fac_ref, gy_lo, gy_hi, gz_lo, gz_hi,
+                       hy_lo, hy_hi, hz_lo, hz_hi, loc_ref, vals_ref):
     m = pore_ref.shape[0]
-    srcs = ([], [])
+    src = []
     for i in range(m):
         mob, _, mob_n, fc = _geo_row(i, pore_ref, lab_ref, gy_lo, gy_hi, gz_lo, gz_hi)
         w = 0.5 * (1.0 + mob)
-        f1 = fa_ref[0, i]
-        f_n = _neighbours(f1, _yrow(hy_lo, 0, i), _yrow(hy_hi, 0, i), _zcol(hz_lo, 0, i), _zcol(hz_hi, 0, i))
-        u_n = [0.5 * (1.0 + mn) * fn for mn, fn in zip(mob_n, f_n)]
-        srcs[0].append(f1 + cross_rate * (1.0 * _flux(w * f1, u_n, fc)))
-        a1 = fa_ref[1, i]
-        a_n = _neighbours(a1, _yrow(hy_lo, 1, i), _yrow(hy_hi, 1, i), _zcol(hz_lo, 1, i), _zcol(hz_hi, 1, i))
-        srcs[1].append(a1 + cross_rate * (w * _flux(a1, a_n, fc)))
-    _local_solves(fac_ref, srcs, loc_ref, vals_ref)
+        x = x_ref[i]
+        x_n = _neighbours(x, _yrow(hy_lo, ch, i), _yrow(hy_hi, ch, i), _zcol(hz_lo, ch, i), _zcol(hz_hi, ch, i))
+        if ch == 0:
+            u_n = [0.5 * (1.0 + mn) * xn for mn, xn in zip(mob_n, x_n)]
+            src.append(x + cross_rate * (1.0 * _flux(w * x, u_n, fc)))
+        else:
+            src.append(x + cross_rate * (w * _flux(x, x_n, fc)))
+    _solve_one(fac_ref, src, loc_ref, vals_ref)
+
+
+def _combine_one_kernel(n, c, extra_edges, pos_ref, *refs):
+    gs_parts, gv_parts = refs[:n], refs[n : 2 * n]
+    refs = refs[2 * n :]
+    lr_ref, loc_ref = refs[0], refs[1]
+    refs = refs[2:]
+    if extra_edges:
+        other, refs = refs[:4], refs[4:]
+    out_ref, refs = refs[0], refs[1:]
+    edges = refs[:4] if len(refs) > 4 else None
+    sep_ref, gs_ref, gv_ref = refs[-3:]
+    for k in range(n):
+        gs_ref[k] = gs_parts[k][...]
+        gv_ref[k, 0] = gv_parts[k][...]
+    m = loc_ref.shape[0]
+    p = pos_ref[0]
+    seps = _reduced_solve(gs_ref, gv_ref, 0, c, n, p, cv=0)
+    for q in range(n):
+        sep_ref[q] = seps[q]
+    own = sep_ref[p]
+    prior = sep_ref[(p + n - 1) % n]
+    for r in range(m):
+        val = loc_ref[r] - lr_ref[0, r] * prior - lr_ref[1, r] * own
+        out_ref[r] = val
+        if edges is not None:
+            _write_edges(edges, 0, r, val)
+    if extra_edges:
+        for e_out, e_in in zip(edges, other):
+            e_out[1] = e_in[0]
 
 
 def _gradient_kernel(pore_ref, lab_ref, a2_ref, gy_lo, gy_hi, gz_lo, gz_hi,
@@ -321,24 +330,12 @@
     return lo, hi
 
 
-def _first_call(m, ny, nz):
-    return pl.pallas_call(
-        _first_kernel,
-        out_shape=(
-            jax.ShapeDtypeStruct((2, m, ny, nz), F32),
-            jax.ShapeDtypeStruct((2, 2, ny, nz), F32),
-        ),
-        in_specs=[_vmem()] * 9,
-        out_specs=(_vmem(), _vmem()),
-    )
-
-
 def _gather_blk(x):
     n = lax.axis_size("blk")
     parts = [x]
     for k in range(1, n):
         parts.append(lax.ppermute(x, "blk", [(j, (j + k) % n) for j in range(n)]))
-    return jnp.stack(parts)
+    return parts
 
 
 def _edge_shapes(chans, m, ny, nz):
@@ -371,55 +368,70 @@
     bx_lo, bx_hi = _exchange(outs[4], outs[5], "blk", True)
     gy_lo, gy_hi, gz_lo, gz_hi = _yz_halos(*outs[:4])
 
-    fac, lr, rows = pl.pallas_call(
+    fac_f, fac_a, lr_f, lr_a, rows = pl.pallas_call(
         lambda *r: _factor_kernel(cycle_step, *r),
-        out_shape=(
-            jax.ShapeDtypeStruct((2, 3, m, ny, nz), F32),
-            jax.ShapeDtypeStruct((2, 2, m, ny, nz), F32),
-            jax.ShapeDtypeStruct((2, 5, ny, nz), F32),
-        ),
+        out_shape=(jax.ShapeDtypeStruct((3, m, ny, nz), F32),) * 2
+        + (jax.ShapeDtypeStruct((2, m, ny, nz), F32),) * 2
+        + (jax.ShapeDtypeStruct((2, 5, ny, nz), F32),),
         in_specs=[_vmem()] * 4,
-        out_specs=(_vmem(), _vmem(), _vmem()),
+        out_specs=tuple(_vmem() for _ in range(5)),
     )(pore_mask, grain_label, bx_lo, bx_hi)
     gathered = _gather_blk(rows)
-
-    loc, vals = _first_call(m, ny, nz)(
-        vacancy, cotangent, pore_mask, grain_label, fac, gy_lo, gy_hi, gz_lo, gz_hi
-    )
-    gathered1 = _gather_blk(vals)
     pos = jnp.reshape(lax.axis_index("blk"), (1,)).astype(jnp.int32)
-
-    outs = pl.pallas_call(
-        lambda *r: _combine_kernel(0, True, {0: 0, 1: 1}, *r),
-        out_shape=(jax.ShapeDtypeStruct((2, m, ny, nz), F32),) + _edge_shapes(2, m, ny, nz),
-        in_specs=[_smem()] + [_vmem()] * 4,
-        out_specs=tuple(_vmem() for _ in range(5)),
-        scratch_shapes=[pltpu.VMEM((n_blk, ny, nz), F32)],
-    )(pos, gathered, gathered1, lr, loc)
-    fa = outs[0]
-
-    hy_lo, hy_hi, hz_lo, hz_hi = _yz_halos(*outs[1:])
-    loc2, vals2 = pl.pallas_call(
-        _second_kernel,
-        out_shape=(
-            jax.ShapeDtypeStruct((2, m, ny, nz), F32),
-            jax.ShapeDtypeStruct((2, 2, ny, nz), F32),
-        ),
-        in_specs=[_vmem()] * 12,
+    vals_shape = jax.ShapeDtypeStruct((2, ny, nz), F32)
+
+    loc_a, vals_a = pl.pallas_call(
+        _first_adj_kernel,
+        out_shape=(shape, vals_shape),
+        in_specs=[_vmem()] * 2,
         out_specs=(_vmem(), _vmem()),
-    )(pore_mask, grain_label, fa, fac, gy_lo, gy_hi, gz_lo, gz_hi, hy_lo, hy_hi, hz_lo, hz_hi)
-
-    gathered2 = _gather_blk(vals2)
-    outs = pl.pallas_call(
-        lambda *r: _combine_kernel(0, False, {1: 0}, *r),
-        out_shape=(shape, shape) + _edge_shapes(1, m, ny, nz),
-        in_specs=[_smem()] + [_vmem()] * 4,
-        out_specs=tuple(_vmem() for _ in range(6)),
-        scratch_shapes=[pltpu.VMEM((n_blk, ny, nz), F32)],
-    )(pos, gathered, gathered2, lr, loc2)
-    final_field, adjoint_two = outs[:2]
-
-    a2_lo, a2_hi, a2z_lo, a2z_hi = _yz_halos(*outs[2:])
+    )(cotangent, fac_a)
+    g_a1 = _gather_blk(vals_a)
+    loc_f, vals_f = pl.pallas_call(
+        _first_fwd_kernel,
+        out_shape=(shape, vals_shape),
+        in_specs=[_vmem()] * 8,
+        out_specs=(_vmem(), _vmem()),
+    )(vacancy, pore_mask, grain_label, fac_f, gy_lo, gy_hi, gz_lo, gz_hi)
+    g_f1 = _gather_blk(vals_f)
+
+    def combine(c, g_vals, lr, loc, edge_chans, other=None):
+        extra = other is not None
+        out_shape = (shape,) + (_edge_shapes(edge_chans, m, ny, nz) if edge_chans else ())
+        return pl.pallas_call(
+            lambda *r: _combine_one_kernel(n_blk, c, extra, *r),
+            out_shape=out_shape,
+            in_specs=[_smem()] + [_vmem()] * (2 * n_blk + 2 + (4 if extra else 0)),
+            out_specs=tuple(_vmem() for _ in out_shape),
+            scratch_shapes=[
+                pltpu.VMEM((n_blk, ny, nz), F32),
+                pltpu.VMEM((n_blk, 2, 5, ny, nz), F32),
+                pltpu.VMEM((n_blk, 1, 2, ny, nz), F32),
+            ],
+        )(pos, *gathered, *g_vals, lr, loc, *((other or ())))
+
+    a1_out = combine(1, g_a1, lr_a, loc_a, 1)
+    f1_out = combine(0, g_f1, lr_f, loc_f, 2, other=a1_out[1:])
+    adjoint_one, field_one = a1_out[0], f1_out[0]
+
+    hy_lo, hy_hi, hz_lo, hz_hi = _yz_halos(*f1_out[1:])
+
+    def second(ch, x, fac):
+        return pl.pallas_call(
+            lambda *r: _second_one_kernel(ch, *r),
+            out_shape=(shape, vals_shape),
+            in_specs=[_vmem()] * 12,
+            out_specs=(_vmem(), _vmem()),
+        )(pore_mask, grain_label, x, fac, gy_lo, gy_hi, gz_lo, gz_hi, hy_lo, hy_hi, hz_lo, hz_hi)
+
+    loc2_a, vals2_a = second(1, adjoint_one, fac_a)
+    g_a2 = _gather_blk(vals2_a)
+    loc2_f, vals2_f = second(0, field_one, fac_f)
+    g_f2 = _gather_blk(vals2_f)
+    a2_out = combine(1, g_a2, lr_a, loc2_a, 1)
+    adjoint_two = a2_out[0]
+    a2_lo, a2_hi, a2z_lo, a2z_hi = _yz_halos(*a2_out[1:])
+    final_field = combine(0, g_f2, lr_f, loc2_f, 0)[0]
     gradient = pl.pallas_call(
         _gradient_kernel,
         out_shape=shape,

time: 89.5 us -> 92.3 us (1.031)
  the two profiles are of different devices: /device:TPU:12 before, /device:TPU:4 now
where the time goes in v4:
time: 92.3 us; the launch traced here: 91.6 us
  starting transfers between devices  38.5 us (42%)
  Pallas kernels  37.1 us (40%)
  waiting for transfers between devices  10.1 us (11%)
  local copies, waits for them, and re-layouts  5.07 us (5%)
    ppermute x7, starting transfers between devices, _exchange(): lo = lax.ppermute(last, axis, forward)  17.7 us
    ppermute x7, starting transfers between devices, _exchange(): hi = lax.ppermute(first, axis, backward)  15.3 us
    pallas_call x4, Pallas kernels, combine(): pl.pallas_call(lambda *r: _combine_one_kernel(n_blk, c, extra, *r), out_s...  10.2 us
    pallas_call x2, Pallas kernels, second(): pl.pallas_call(lambda *r: _second_one_kernel(ch, *r), out_shape=(shape, v...  9.1 us
    ppermute x7, waiting for transfers between devices, _exchange(): hi = lax.ppermute(first, axis, backward)  7.33 us
    ppermute x5, starting transfers between devices, _gather_blk(): parts.append(lax.ppermute(x, 'blk', [(j, (j + k) % n) for j in range(n)]))  5.52 us
    unnamed x38, local copies, waits for them, and re-layouts  5.07 us
    pallas_call x1, Pallas kernels, _shards(): pl.pallas_call(_first_fwd_kernel, out_shape=(shape, vals_shape), in_specs...  4.55 us
  transfers between devices with their start and end apart: 19, of which 6 were waited for; matrix products, arithmetic and copies ran while one was open for 0% of the time, Pallas kernels for 21%

profile of v4, /device:TPU:4, one launch (start us, length us, event | category | flops | bytes accessed | tf_op | source)
XLA Modules:
  0.0 91.6 jit_solution(5328859204512518827)
XLA Ops:
  0.6 2.5 %shard_map.59 = (f32[3,32,256]{2,1,0:T(8,128)}, f32[3,32,256]{2,1,0:T(8,128)}, f32[3,16,32]{2,1,0:T(8,128)}, f32[3,16,32]{2,1,0:T(8,128)}, f32[2,16,256]{2,1,0:T(8,128)}, /*index=5*/f32[2,16,256]{2,1,0:T(8,128)}) custom-call(f32[32,16,256]{2,1,0:T(8,128)} %vac_ref.3, s32[32,16,256]{2,1,0:T(8,128)} %pore_ref.5, s32[32,16,256]{2,1,0:T(8,128)} %lab_ref.5), custom_call_target="tpu_custom_call" | custom-call | tf_op jit(solution)/shard_map/pallas_call | solution.py:362
  3.1 1.5 %collective-permute-start = (f32[2,16,256]{2,1,0:T(8,128)}, f32[2,16,256]{2,1,0:T(8,128)S(1)}, u32[]{:S(2)}, u32[]{:S(2)}) collective-permute-start(f32[2,16,256]{2,1,0:T(8,128)} %get-tuple-element.36), channel_id=1, source_target_pairs={{0,16},{16,0},{1,17},{17,1},{2,18},{18,2},{3,19},{19,3},{4,20},{20... | collective-permute-start | bytes 98312 | tf_op jit(solution)/shard_map/ppermute | solution.py:328
  4.6 0.5 collective-permute-start.1
  5.1 2.4 %collective-permute-done.r_2_ = f32[2,16,256]{2,1,0:T(8,128)S(1)} collective-permute-done((f32[2,16,256]{2,1,0:T(8,128)}, f32[2,16,256]{2,1,0:T(8,128)S(1)}, u32[]{:S(2)}, u32[]{:S(2)}) %collective-permute-start) | collective-permute-done | bytes 32800 | tf_op jit(solution)/shard_map/ppermute | solution.py:328
  7.5 1.2 %collective-permute-done.1.r_3_ = f32[2,16,256]{2,1,0:T(8,128)S(1)} collective-permute-done((f32[2,16,256]{2,1,0:T(8,128)}, f32[2,16,256]{2,1,0:T(8,128)S(1)}, u32[]{:S(2)}, u32[]{:S(2)}) %collective-permute-start.1) | collective-permute-done | bytes 32800 | tf_op jit(solution)/shard_map/ppermute | solution.py:329
  8.7 0.6 copy-done.16
  9.3 4.3 %shard_map.60 = (f32[3,32,16,256]{3,2,1,0:T(8,128)}, f32[3,32,16,256]{3,2,1,0:T(8,128)}, f32[2,32,16,256]{3,2,1,0:T(8,128)}, f32[2,32,16,256]{3,2,1,0:T(8,128)}, f32[2,5,16,256]{3,2,1,0:T(8,128)}) custom-call(s32[32,16,256]{2,1,0:T(8,128)} %pore_ref.5, s32[32,16,256]{2,1,0:T(8,128)} %lab_ref.5, f32[2,16,256]{2,1,0:T(8,128)} %copy-done.15, ...), custom_call_target="tpu_custom_call" | custom-call | tf_op jit(solution)/shard_map/pallas_call | solution.py:371
  13.7 0.6 collective-permute-start.2
  14.3 1.9 %collective-permute-start.3 = (f32[3,32,256]{2,1,0:T(8,128)}, f32[3,32,256]{2,1,0:T(8,128)S(1)}, u32[]{:S(2)}, u32[]{:S(2)}) collective-permute-start(f32[3,32,256]{2,1,0:T(8,128)} %get-tuple-element.40), channel_id=1, source_target_pairs={{0,4},{4,8},{8,12},{1,5},{5,9},{9,13},{2,6},{6,10},{10,14},{3,7},{... | collective-permute-start | bytes 294920 | tf_op jit(solution)/shard_map/ppermute | solution.py:328
  16.2 3.6 %collective-permute-start.4 = (f32[3,32,256]{2,1,0:T(8,128)}, f32[3,32,256]{2,1,0:T(8,128)S(1)}, u32[]{:S(2)}, u32[]{:S(2)}) collective-permute-start(f32[3,32,256]{2,1,0:T(8,128)} %get-tuple-element.41), channel_id=1, source_target_pairs={{4,0},{8,4},{12,8},{5,1},{9,5},{13,9},{6,2},{10,6},{14,10},{7,3},{... | collective-permute-start | bytes 294920 | tf_op jit(solution)/shard_map/ppermute | solution.py:329
  19.9 3.5 %collective-permute-start.5 = (f32[3,16,32]{2,1,0:T(8,128)}, f32[3,16,32]{2,1,0:T(8,128)S(1)}, u32[]{:S(2)}, u32[]{:S(2)}) collective-permute-start(f32[3,16,32]{2,1,0:T(8,128)} %get-tuple-element.42), channel_id=1, source_target_pairs={{0,1},{1,2},{2,3},{4,5},{5,6},{6,7},{8,9},{9,10},{10,11},{12,13},{... | collective-permute-start | bytes 18440 | tf_op jit(solution)/shard_map/ppermute | solution.py:328
  23.3 1.3 %collective-permute-start.6 = (f32[3,16,32]{2,1,0:T(8,128)}, f32[3,16,32]{2,1,0:T(8,128)S(1)}, u32[]{:S(2)}, u32[]{:S(2)}) collective-permute-start(f32[3,16,32]{2,1,0:T(8,128)} %get-tuple-element.43), channel_id=1, source_target_pairs={{1,0},{2,1},{3,2},{5,4},{6,5},{7,6},{9,8},{10,9},{11,10},{13,12},{... | collective-permute-start | bytes 18440 | tf_op jit(solution)/shard_map/ppermute | solution.py:329
  24.6 2.6 %shard_map.62 = (f32[32,16,256]{2,1,0:T(8,128)}, f32[2,16,256]{2,1,0:T(8,128)}) custom-call(f32[32,16,256]{2,1,0:T(8,128)} %cot_ref.1, f32[3,32,16,256]{3,2,1,0:T(8,128)} %get-tuple-element.47.fac_ref.r_3_), custom_call_target="tpu_custom_call" | custom-call | tf_op jit(solution)/shard_map/pallas_call | solution.py:383
  27.2 1.5 %collective-permute-start.8 = (f32[2,16,256]{2,1,0:T(8,128)}, f32[2,16,256]{2,1,0:T(8,128)S(1)}, u32[]{:S(2)}, u32[]{:S(2)}) collective-permute-start(f32[2,16,256]{2,1,0:T(8,128)} %get-tuple-element.48.r_3_), channel_id=1, source_target_pairs={{0,16},{16,0},{1,17},{17,1},{2,18},{18,2},{3,19},{19,3},{4,20},{20... | collective-permute-start | bytes 98312 | tf_op jit(solution)/shard_map/ppermute | solution.py:337
  28.7 0.6 collective-permute-done.6.gz_hi.r_7_
  29.3 0.6 copy-done.4
  29.9 0.1 copy-done.1
  29.9 0.0 copy-done.2
  30.0 4.5 %shard_map.61 = (f32[32,16,256]{2,1,0:T(8,128)}, f32[2,16,256]{2,1,0:T(8,128)}) custom-call(f32[32,16,256]{2,1,0:T(8,128)} %vac_ref.3, s32[32,16,256]{2,1,0:T(8,128)} %pore_ref.5, s32[32,16,256]{2,1,0:T(8,128)} %lab_ref.5, f32[3,32,16,256]{3,2,1,0:T(8,128)} %get-tuple-element.39.fac_ref.r_3_, f32[3,32,256]{2,1,0:T(8,128)} %copy-done.1, ...), custom_call_target="tpu_custom_call" | custom-call | tf_op jit(solution)/shard_map/pallas_call | solution.py:390
  34.5 1.4 %collective-permute-start.7 = (f32[2,16,256]{2,1,0:T(8,128)}, f32[2,16,256]{2,1,0:T(8,128)S(1)}, u32[]{:S(2)}, u32[]{:S(2)}) collective-permute-start(f32[2,16,256]{2,1,0:T(8,128)} %get-tuple-element.44.r_3_), channel_id=1, source_target_pairs={{0,16},{16,0},{1,17},{17,1},{2,18},{18,2},{3,19},{19,3},{4,20},{20... | collective-permute-start | bytes 98312 | tf_op jit(solution)/shard_map/ppermute | solution.py:337
  36.0 0.6 copy-done.11
  36.5 0.1 copy-done
  36.6 2.6 %shard_map.63 = (f32[32,16,256]{2,1,0:T(8,128)}, f32[1,32,256]{2,1,0:T(8,128)}, f32[1,32,256]{2,1,0:T(8,128)}, f32[1,16,32]{2,1,0:T(8,128)}, f32[1,16,32]{2,1,0:T(8,128)}) custom-call(s32[1]{0:T(128)} %bitcast.r_0_, f32[2,5,16,256]{3,2,1,0:T(8,128)} %get-tuple-element.38.r_1_, f32[2,5,16,256]{3,2,1,0:T(8,128)} %copy-done, ...), custom_call_target="tpu_custom_call" | custom-call | tf_op jit(solution)/shard_map/pallas_call | solution.py:401
  39.2 0.6 copy-done.13
  39.8 2.6 %shard_map.64 = (f32[32,16,256]{2,1,0:T(8,128)}, f32[2,32,256]{2,1,0:T(8,128)}, f32[2,32,256]{2,1,0:T(8,128)}, f32[2,16,32]{2,1,0:T(8,128)}, f32[2,16,32]{2,1,0:T(8,128)}) custom-call(s32[1]{0:T(128)} %bitcast.r_0_, f32[2,5,16,256]{3,2,1,0:T(8,128)} %get-tuple-element.38.r_1_, f32[2,5,16,256]{3,2,1,0:T(8,128)} %copy-done, ...), custom_call_target="tpu_custom_call" | custom-call | tf_op jit(solution)/shard_map/pallas_call | solution.py:401
  42.4 1.9 %collective-permute-start.9 = (f32[2,32,256]{2,1,0:T(8,128)}, f32[2,32,256]{2,1,0:T(8,128)S(1)}, u32[]{:S(2)}, u32[]{:S(2)}) collective-permute-start(f32[2,32,256]{2,1,0:T(8,128)} %get-tuple-element.56), channel_id=1, source_target_pairs={{0,4},{4,8},{8,12},{1,5},{5,9},{9,13},{2,6},{6,10},{10,14},{3,7},{... | collective-permute-start | bytes 196616 | tf_op jit(solution)/shard_map/ppermute | solution.py:328
  44.3 3.6 %collective-permute-start.10 = (f32[2,32,256]{2,1,0:T(8,128)}, f32[2,32,256]{2,1,0:T(8,128)S(1)}, u32[]{:S(2)}, u32[]{:S(2)}) collective-permute-start(f32[2,32,256]{2,1,0:T(8,128)} %get-tuple-element.57), channel_id=1, source_target_pairs={{4,0},{8,4},{12,8},{5,1},{9,5},{13,9},{6,2},{10,6},{14,10},{7,3},{... | collective-permute-start | bytes 196616 | tf_op jit(solution)/shard_map/ppermute | solution.py:329
  48.0 3.5 %collective-permute-start.11 = (f32[2,16,32]{2,1,0:T(8,128)}, f32[2,16,32]{2,1,0:T(8,128)S(1)}, u32[]{:S(2)}, u32[]{:S(2)}) collective-permute-start(f32[2,16,32]{2,1,0:T(8,128)} %get-tuple-element.58), channel_id=1, source_target_pairs={{0,1},{1,2},{2,3},{4,5},{5,6},{6,7},{8,9},{9,10},{10,11},{12,13},{... | collective-permute-start | bytes 12296 | tf_op jit(solution)/shard_map/ppermute | solution.py:328
  51.5 1.3 %collective-permute-start.12 = (f32[2,16,32]{2,1,0:T(8,128)}, f32[2,16,32]{2,1,0:T(8,128)S(1)}, u32[]{:S(2)}, u32[]{:S(2)}) collective-permute-start(f32[2,16,32]{2,1,0:T(8,128)} %get-tuple-element.59), channel_id=1, source_target_pairs={{1,0},{2,1},{3,2},{5,4},{6,5},{7,6},{9,8},{10,9},{11,10},{13,12},{... | collective-permute-start | bytes 12296 | tf_op jit(solution)/shard_map/ppermute | solution.py:329
  52.8 0.3 collective-permute-done.11.r_10_
  53.1 4.2 %collective-permute-done.12.r_11_ = f32[2,16,32]{2,1,0:T(8,128)S(1)} collective-permute-done((f32[2,16,32]{2,1,0:T(8,128)}, f32[2,16,32]{2,1,0:T(8,128)S(1)}, u32[]{:S(2)}, u32[]{:S(2)}) %collective-permute-start.12) | collective-permute-done | bytes 4128 | tf_op jit(solution)/shard_map/ppermute | solution.py:329
  57.3 0.6 copy-done.8
  57.9 0.1 copy-done.5
  58.0 4.4 %shard_map.67 = (f32[32,16,256]{2,1,0:T(8,128)}, f32[2,16,256]{2,1,0:T(8,128)}) custom-call(s32[32,16,256]{2,1,0:T(8,128)} %pore_ref.5, s32[32,16,256]{2,1,0:T(8,128)} %lab_ref.5, f32[32,16,256]{2,1,0:T(8,128)} %get-tuple-element.62.r_2_, f32[3,32,16,256]{3,2,1,0:T(8,128)} %get-tuple-element.47.fac_ref.r_3_, f32[3,32,256]{2,1,0:T(8,128)} %copy-done.1, ...), custom_call_target="tpu_custom_call" | custom-call | tf_op jit(solution)/shard_map/pallas_call | solution.py:420
  62.4 1.1 %collective-permute-start.14 = (f32[2,16,256]{2,1,0:T(8,128)}, f32[2,16,256]{2,1,0:T(8,128)S(1)}, u32[]{:S(2)}, u32[]{:S(2)}) collective-permute-start(f32[2,16,256]{2,1,0:T(8,128)} %get-tuple-element.63.r_3_), channel_id=1, source_target_pairs={{0,16},{16,0},{1,17},{17,1},{2,18},{18,2},{3,19},{19,3},{4,20},{20... | collective-permute-start | bytes 98312 | tf_op jit(solution)/shard_map/ppermute | solution.py:337
  63.5 4.7 %shard_map.65 = (f32[32,16,256]{2,1,0:T(8,128)}, f32[2,16,256]{2,1,0:T(8,128)}) custom-call(s32[32,16,256]{2,1,0:T(8,128)} %pore_ref.5, s32[32,16,256]{2,1,0:T(8,128)} %lab_ref.5, f32[32,16,256]{2,1,0:T(8,128)} %get-tuple-element.55.r_2_, f32[3,32,16,256]{3,2,1,0:T(8,128)} %get-tuple-element.39.fac_ref.r_3_, f32[3,32,256]{2,1,0:T(8,128)} %copy-done.1, ...), custom_call_target="tpu_custom_call" | custom-call | tf_op jit(solution)/shard_map/pallas_call | solution.py:420
  68.2 0.9 collective-permute-start.13
  69.1 0.6 copy-done.14
  69.7 2.6 %shard_map.68 = (f32[32,16,256]{2,1,0:T(8,128)}, f32[1,32,256]{2,1,0:T(8,128)}, f32[1,32,256]{2,1,0:T(8,128)}, f32[1,16,32]{2,1,0:T(8,128)}, f32[1,16,32]{2,1,0:T(8,128)}) custom-call(s32[1]{0:T(128)} %bitcast.r_0_, f32[2,5,16,256]{3,2,1,0:T(8,128)} %get-tuple-element.38.r_1_, f32[2,5,16,256]{3,2,1,0:T(8,128)} %copy-done, ...), custom_call_target="tpu_custom_call" | custom-call | tf_op jit(solution)/shard_map/pallas_call | solution.py:401
  72.3 1.9 %collective-permute-start.15 = (f32[1,32,256]{2,1,0:T(8,128)}, f32[1,32,256]{2,1,0:T(8,128)S(1)}, u32[]{:S(2)}, u32[]{:S(2)}) collective-permute-start(f32[1,32,256]{2,1,0:T(8,128)} %get-tuple-element.66), channel_id=1, source_target_pairs={{0,4},{4,8},{8,12},{1,5},{5,9},{9,13},{2,6},{6,10},{10,14},{3,7},{... | collective-permute-start | bytes 98312 | tf_op jit(solution)/shard_map/ppermute | solution.py:328
  74.2 3.6 %collective-permute-start.16 = (f32[1,32,256]{2,1,0:T(8,128)}, f32[1,32,256]{2,1,0:T(8,128)S(1)}, u32[]{:S(2)}, u32[]{:S(2)}) collective-permute-start(f32[1,32,256]{2,1,0:T(8,128)} %get-tuple-element.67), channel_id=1, source_target_pairs={{4,0},{8,4},{12,8},{5,1},{9,5},{13,9},{6,2},{10,6},{14,10},{7,3},{... | collective-permute-start | bytes 98312 | tf_op jit(solution)/shard_map/ppermute | solution.py:329
  77.9 3.5 %collective-permute-start.17 = (f32[1,16,32]{2,1,0:T(8,128)}, f32[1,16,32]{2,1,0:T(8,128)S(1)}, u32[]{:S(2)}, u32[]{:S(2)}) collective-permute-start(f32[1,16,32]{2,1,0:T(8,128)} %get-tuple-element.68), channel_id=1, source_target_pairs={{0,1},{1,2},{2,3},{4,5},{5,6},{6,7},{8,9},{9,10},{10,11},{12,13},{... | collective-permute-start | bytes 6152 | tf_op jit(solution)/shard_map/ppermute | solution.py:328
  81.3 1.3 %collective-permute-start.18 = (f32[1,16,32]{2,1,0:T(8,128)}, f32[1,16,32]{2,1,0:T(8,128)S(1)}, u32[]{:S(2)}, u32[]{:S(2)}) collective-permute-start(f32[1,16,32]{2,1,0:T(8,128)} %get-tuple-element.69), channel_id=1, source_target_pairs={{1,0},{2,1},{3,2},{5,4},{6,5},{7,6},{9,8},{10,9},{11,10},{13,12},{... | collective-permute-start | bytes 6152 | tf_op jit(solution)/shard_map/ppermute | solution.py:329
  82.7 0.6 copy-done.12
  83.3 2.5 %shard_map.66 = f32[32,16,256]{2,1,0:T(8,128)} custom-call(s32[1]{0:T(128)} %bitcast.r_0_, f32[2,5,16,256]{3,2,1,0:T(8,128)} %get-tuple-element.38.r_1_, f32[2,5,16,256]{3,2,1,0:T(8,128)} %copy-done, f32[2,16,256]{2,1,0:T(8,128)} %get-tuple-element.60.r_3_, f32[2,16,256]{2,1,0:T(8,128)} %copy-done.12, f32[2,32,16,256]{3,2,1,0:T(8,128)} %get-tuple-element.45.r_5_, ...), custom_call_target="tpu_custom_call" | custom-call | tf_op jit(solution)/shard_map/pallas_call | solution.py:401
  85.8 1.3 %collective-permute-done.18.hz_hi = f32[1,16,32]{2,1,0:T(8,128)S(1)} collective-permute-done((f32[1,16,32]{2,1,0:T(8,128)}, f32[1,16,32]{2,1,0:T(8,128)S(1)}, u32[]{:S(2)}, u32[]{:S(2)}) %collective-permute-start.18) | collective-permute-done | bytes 2080 | tf_op jit(solution)/shard_map/ppermute | solution.py:329
  87.1 0.6 copy-done.18
  87.7 3.8 %shard_map.69 = f32[32,16,256]{2,1,0:T(8,128)} custom-call(s32[32,16,256]{2,1,0:T(8,128)} %pore_ref.5, s32[32,16,256]{2,1,0:T(8,128)} %lab_ref.5, f32[32,16,256]{2,1,0:T(8,128)} %get-tuple-element.65.a2_ref, f32[3,32,256]{2,1,0:T(8,128)} %copy-done.1, f32[3,32,256]{2,1,0:T(8,128)} %copy-done.2, f32[3,16,32]{2,1,0:T(8,128)} %copy-done.3, ...), custom_call_target="tpu_custom_call" | custom-call | tf_op jit(solution)/shard_map/pallas_call | solution.py:435
  (39 shorter events, 0.1 us)
Async XLA Ops:
  3.1 4.4 %collective-permute-start = (f32[2,16,256]{2,1,0:T(8,128)}, f32[2,16,256]{2,1,0:T(8,128)S(1)}, u32[]{:S(2)}, u32[]{:S(2)}) collective-permute-start(f32[2,16,256]{2,1,0:T(8,128)} %get-tuple-element.36), channel_id=1, source_target_pairs={{0,16},{16,0},{1,17},{17,1},{2,18},{18,2},{3,19},{19,3},{4,20},{20... | collective-permute-start | bytes 98312 | tf_op jit(solution)/shard_map/ppermute | solution.py:328
  4.6 4.1 %collective-permute-start.1 = (f32[2,16,256]{2,1,0:T(8,128)}, f32[2,16,256]{2,1,0:T(8,128)S(1)}, u32[]{:S(2)}, u32[]{:S(2)}) collective-permute-start(f32[2,16,256]{2,1,0:T(8,128)} %get-tuple-element.37), channel_id=1, source_target_pairs={{16,0},{0,16},{17,1},{1,17},{18,2},{2,18},{19,3},{3,19},{20,4},{4,... | collective-permute-start | bytes 98312 | tf_op jit(solution)/shard_map/ppermute | solution.py:329
  7.5 1.2 %copy-start.15 = (f32[2,16,256]{2,1,0:T(8,128)}, f32[2,16,256]{2,1,0:T(8,128)S(1)}, u32[]{:S(2)}) copy-start(f32[2,16,256]{2,1,0:T(8,128)S(1)} %collective-permute-done.r_2_) | copy-start | bytes 98308
  8.7 0.6 copy-start.16
  13.7 22.3 %collective-permute-start.2 = (f32[2,5,16,256]{3,2,1,0:T(8,128)}, f32[2,5,16,256]{3,2,1,0:T(8,128)S(1)}, u32[]{:S(2)}, u32[]{:S(2)}) collective-permute-start(f32[2,5,16,256]{3,2,1,0:T(8,128)} %get-tuple-element.38.r_1_), channel_id=1, source_target_pairs={{0,16},{16,0},{1,17},{17,1},{2,18},{18,2},{3,19},{19,3},{4,20},{20... | collective-permute-start | bytes 491528 | tf_op jit(solution)/shard_map/ppermute | solution.py:337
  14.3 15.0 %collective-permute-start.3 = (f32[3,32,256]{2,1,0:T(8,128)}, f32[3,32,256]{2,1,0:T(8,128)S(1)}, u32[]{:S(2)}, u32[]{:S(2)}) collective-permute-start(f32[3,32,256]{2,1,0:T(8,128)} %get-tuple-element.40), channel_id=1, source_target_pairs={{0,4},{4,8},{8,12},{1,5},{5,9},{9,13},{2,6},{6,10},{10,14},{3,7},{... | collective-permute-start | bytes 294920 | tf_op jit(solution)/shard_map/ppermute | solution.py:328
  16.2 13.1 %collective-permute-start.4 = (f32[3,32,256]{2,1,0:T(8,128)}, f32[3,32,256]{2,1,0:T(8,128)S(1)}, u32[]{:S(2)}, u32[]{:S(2)}) collective-permute-start(f32[3,32,256]{2,1,0:T(8,128)} %get-tuple-element.41), channel_id=1, source_target_pairs={{4,0},{8,4},{12,8},{5,1},{9,5},{13,9},{6,2},{10,6},{14,10},{7,3},{... | collective-permute-start | bytes 294920 | tf_op jit(solution)/shard_map/ppermute | solution.py:329
  19.9 7.4 %collective-permute-start.5 = (f32[3,16,32]{2,1,0:T(8,128)}, f32[3,16,32]{2,1,0:T(8,128)S(1)}, u32[]{:S(2)}, u32[]{:S(2)}) collective-permute-start(f32[3,16,32]{2,1,0:T(8,128)} %get-tuple-element.42), channel_id=1, source_target_pairs={{0,1},{1,2},{2,3},{4,5},{5,6},{6,7},{8,9},{9,10},{10,11},{12,13},{... | collective-permute-start | bytes 18440 | tf_op jit(solution)/shard_map/ppermute | solution.py:328
  23.3 5.9 %collective-permute-start.6 = (f32[3,16,32]{2,1,0:T(8,128)}, f32[3,16,32]{2,1,0:T(8,128)S(1)}, u32[]{:S(2)}, u32[]{:S(2)}) collective-permute-start(f32[3,16,32]{2,1,0:T(8,128)} %get-tuple-element.43), channel_id=1, source_target_pairs={{1,0},{2,1},{3,2},{5,4},{6,5},{7,6},{9,8},{10,9},{11,10},{13,12},{... | collective-permute-start | bytes 18440 | tf_op jit(solution)/shard_map/ppermute | solution.py:329
  27.2 2.1 %copy-start.3 = (f32[3,16,32]{2,1,0:T(8,128)}, f32[3,16,32]{2,1,0:T(8,128)S(1)}, u32[]{:S(2)}) copy-start(f32[3,16,32]{2,1,0:T(8,128)S(1)} %collective-permute-done.5.gz_lo.r_6_) | copy-start | bytes 18436
  27.2 8.7 %collective-permute-start.8 = (f32[2,16,256]{2,1,0:T(8,128)}, f32[2,16,256]{2,1,0:T(8,128)S(1)}, u32[]{:S(2)}, u32[]{:S(2)}) collective-permute-start(f32[2,16,256]{2,1,0:T(8,128)} %get-tuple-element.48.r_3_), channel_id=1, source_target_pairs={{0,16},{16,0},{1,17},{17,1},{2,18},{18,2},{3,19},{19,3},{4,20},{20... | collective-permute-start | bytes 98312 | tf_op jit(solution)/shard_map/ppermute | solution.py:337
  29.3 0.6 copy-start.4
  29.3 0.6 copy-start.1
  29.3 0.7 copy-start.2
  34.5 4.7 %collective-permute-start.7 = (f32[2,16,256]{2,1,0:T(8,128)}, f32[2,16,256]{2,1,0:T(8,128)S(1)}, u32[]{:S(2)}, u32[]{:S(2)}) collective-permute-start(f32[2,16,256]{2,1,0:T(8,128)} %get-tuple-element.44.r_3_), channel_id=1, source_target_pairs={{0,16},{16,0},{1,17},{17,1},{2,18},{18,2},{3,19},{19,3},{4,20},{20... | collective-permute-start | bytes 98312 | tf_op jit(solution)/shard_map/ppermute | solution.py:337
  35.9 0.6 copy-start.11
  35.9 0.7 copy-start
  39.2 0.6 copy-start.13
  42.4 14.9 %collective-permute-start.9 = (f32[2,32,256]{2,1,0:T(8,128)}, f32[2,32,256]{2,1,0:T(8,128)S(1)}, u32[]{:S(2)}, u32[]{:S(2)}) collective-permute-start(f32[2,32,256]{2,1,0:T(8,128)} %get-tuple-element.56), channel_id=1, source_target_pairs={{0,4},{4,8},{8,12},{1,5},{5,9},{9,13},{2,6},{6,10},{10,14},{3,7},{... | collective-permute-start | bytes 196616 | tf_op jit(solution)/shard_map/ppermute | solution.py:328
  44.3 13.0 %collective-permute-start.10 = (f32[2,32,256]{2,1,0:T(8,128)}, f32[2,32,256]{2,1,0:T(8,128)S(1)}, u32[]{:S(2)}, u32[]{:S(2)}) collective-permute-start(f32[2,32,256]{2,1,0:T(8,128)} %get-tuple-element.57), channel_id=1, source_target_pairs={{4,0},{8,4},{12,8},{5,1},{9,5},{13,9},{6,2},{10,6},{14,10},{7,3},{... | collective-permute-start | bytes 196616 | tf_op jit(solution)/shard_map/ppermute | solution.py:329
  48.0 5.1 %collective-permute-start.11 = (f32[2,16,32]{2,1,0:T(8,128)}, f32[2,16,32]{2,1,0:T(8,128)S(1)}, u32[]{:S(2)}, u32[]{:S(2)}) collective-permute-start(f32[2,16,32]{2,1,0:T(8,128)} %get-tuple-element.58), channel_id=1, source_target_pairs={{0,1},{1,2},{2,3},{4,5},{5,6},{6,7},{8,9},{9,10},{10,11},{12,13},{... | collective-permute-start | bytes 12296 | tf_op jit(solution)/shard_map/ppermute | solution.py:328
  51.5 5.8 %collective-permute-start.12 = (f32[2,16,32]{2,1,0:T(8,128)}, f32[2,16,32]{2,1,0:T(8,128)S(1)}, u32[]{:S(2)}, u32[]{:S(2)}) collective-permute-start(f32[2,16,32]{2,1,0:T(8,128)} %get-tuple-element.59), channel_id=1, source_target_pairs={{1,0},{2,1},{3,2},{5,4},{6,5},{7,6},{9,8},{10,9},{11,10},{13,12},{... | collective-permute-start | bytes 12296 | tf_op jit(solution)/shard_map/ppermute | solution.py:329
  53.1 4.2 %copy-start.7 = (f32[2,16,32]{2,1,0:T(8,128)}, f32[2,16,32]{2,1,0:T(8,128)S(1)}, u32[]{:S(2)}) copy-start(f32[2,16,32]{2,1,0:T(8,128)S(1)} %collective-permute-done.11.r_10_) | copy-start | bytes 12292
  57.3 0.6 copy-start.8
  57.3 0.6 copy-start.5
  57.3 0.7 copy-start.6
  62.4 6.7 %collective-permute-start.14 = (f32[2,16,256]{2,1,0:T(8,128)}, f32[2,16,256]{2,1,0:T(8,128)S(1)}, u32[]{:S(2)}, u32[]{:S(2)}) collective-permute-start(f32[2,16,256]{2,1,0:T(8,128)} %get-tuple-element.63.r_3_), channel_id=1, source_target_pairs={{0,16},{16,0},{1,17},{17,1},{2,18},{18,2},{3,19},{19,3},{4,20},{20... | collective-permute-start | bytes 98312 | tf_op jit(solution)/shard_map/ppermute | solution.py:337
  68.2 14.4 %collective-permute-start.13 = (f32[2,16,256]{2,1,0:T(8,128)}, f32[2,16,256]{2,1,0:T(8,128)S(1)}, u32[]{:S(2)}, u32[]{:S(2)}) collective-permute-start(f32[2,16,256]{2,1,0:T(8,128)} %get-tuple-element.60.r_3_), channel_id=1, source_target_pairs={{0,16},{16,0},{1,17},{17,1},{2,18},{18,2},{3,19},{19,3},{4,20},{20... | collective-permute-start | bytes 98312 | tf_op jit(solution)/shard_map/ppermute | solution.py:337
  69.1 0.6 copy-start.14
  72.3 14.8 %collective-permute-start.15 = (f32[1,32,256]{2,1,0:T(8,128)}, f32[1,32,256]{2,1,0:T(8,128)S(1)}, u32[]{:S(2)}, u32[]{:S(2)}) collective-permute-start(f32[1,32,256]{2,1,0:T(8,128)} %get-tuple-element.66), channel_id=1, source_target_pairs={{0,4},{4,8},{8,12},{1,5},{5,9},{9,13},{2,6},{6,10},{10,14},{3,7},{... | collective-permute-start | bytes 98312 | tf_op jit(solution)/shard_map/ppermute | solution.py:328
  74.2 12.9 %collective-permute-start.16 = (f32[1,32,256]{2,1,0:T(8,128)}, f32[1,32,256]{2,1,0:T(8,128)S(1)}, u32[]{:S(2)}, u32[]{:S(2)}) collective-permute-start(f32[1,32,256]{2,1,0:T(8,128)} %get-tuple-element.67), channel_id=1, source_target_pairs={{4,0},{8,4},{12,8},{5,1},{9,5},{13,9},{6,2},{10,6},{14,10},{7,3},{... | collective-permute-start | bytes 98312 | tf_op jit(solution)/shard_map/ppermute | solution.py:329
  77.9 7.9 %collective-permute-start.17 = (f32[1,16,32]{2,1,0:T(8,128)}, f32[1,16,32]{2,1,0:T(8,128)S(1)}, u32[]{:S(2)}, u32[]{:S(2)}) collective-permute-start(f32[1,16,32]{2,1,0:T(8,128)} %get-tuple-element.68), channel_id=1, source_target_pairs={{0,1},{1,2},{2,3},{4,5},{5,6},{6,7},{8,9},{9,10},{10,11},{12,13},{... | collective-permute-start | bytes 6152 | tf_op jit(solution)/shard_map/ppermute | solution.py:328
  81.3 5.8 %collective-permute-start.18 = (f32[1,16,32]{2,1,0:T(8,128)}, f32[1,16,32]{2,1,0:T(8,128)S(1)}, u32[]{:S(2)}, u32[]{:S(2)}) collective-permute-start(f32[1,16,32]{2,1,0:T(8,128)} %get-tuple-element.69), channel_id=1, source_target_pairs={{1,0},{2,1},{3,2},{5,4},{6,5},{7,6},{9,8},{10,9},{11,10},{13,12},{... | collective-permute-start | bytes 6152 | tf_op jit(solution)/shard_map/ppermute | solution.py:329
  82.7 0.6 copy-start.12
  85.8 1.4 %copy-start.17 = (f32[1,16,32]{2,1,0:T(8,128)}, f32[1,16,32]{2,1,0:T(8,128)S(1)}, u32[]{:S(2)}) copy-start(f32[1,16,32]{2,1,0:T(8,128)S(1)} %collective-permute-done.17.hz_lo) | copy-start | bytes 6148
  87.1 0.6 copy-start.18
  87.1 0.6 copy-start.9
  87.1 0.6 copy-start.10
